TPU v7x, 32 devices: a whole 2x2x4 slice. The times are simulated.
32 devices in a mesh: ctx: 8 (over z, core), head: 4 (over y, x).
Axes of the slice: x: 2, y: 2, z: 4, core: 2. Of those that a mesh axis runs over, the one named last changes fastest.
Arguments:
- lin_query: bfloat16 [2048, 8192], P('ctx', 'head'), may hold values from -6 to 6
- lin_key: bfloat16 [2048, 8192], P('ctx', 'head'), may hold values from -6 to 6
- lin_value: bfloat16 [2048, 8192], P('ctx', 'head'), may hold values from -6 to 6
- norm_gain: float32 [8192], P('head'), may hold values from 0.1 to 1.9
- soft_query: bfloat16 [2048, 8192], P(('ctx', 'head')), may hold values from -180 to 180
- soft_key: bfloat16 [2048, 1024], P(('ctx', 'head')), may hold values from -6.2 to 6.2
- soft_value: bfloat16 [2048, 1024], P(('ctx', 'head')), may hold values from -6 to 6
- doc_lengths: int32 [4], replicated, may hold values from 1 to 768, 2048 in all
Outputs:
- lightning_out: bfloat16 [2048, 8192], P('ctx', 'head')
- attended: bfloat16 [2048, 8192], P('ctx', 'head')
Inputs may be any that keep to these rules, and one draw needn't show every extreme that they name: `doc_lengths`: 4 documents whose lengths sum to 2048.
All inputs are finite; a program needn't handle non-finite values.
Results may differ from a plain program's by a relative error of at most 0.0037.
Values may be sent and summed in bfloat16 or wider, within the bound.
No kernel may reach another device: no remote copies, remote signals or barrier semaphores. Data moves between devices by JAX's collectives and lax.ppermute only.
A program may use at most 64 MiB of HBM per device.

v0:
```python
import math

import jax
import jax.numpy as jnp
import numpy as np
from jax import lax
from jax.experimental import pallas as pl
from jax.experimental.pallas import tpu as pltpu
from jax.sharding import PartitionSpec as P

HEADS = 64
HD = 128
KV_HEADS = 8
SPAN = 3

F32 = jnp.float32
BF16 = jnp.bfloat16


def document_index(doc_lengths, positions):
    doc_ends = jnp.cumsum(doc_lengths)
    counted = jnp.sum((positions[:, None] >= doc_ends[None, :]).astype(jnp.int32), axis=1)
    return jnp.where(positions < 0, -1, counted).astype(jnp.int32)


def from_behind(value, axis, steps):
    count = lax.axis_size(axis)
    pairs = [(source, source + steps) for source in range(0, count - steps)]
    if not pairs:
        return jnp.zeros_like(value)
    return lax.ppermute(value, axis, pairs)


def split_bf16(x):
    hi = x.astype(BF16)
    lo = (x - hi.astype(F32)).astype(BF16)
    return hi, lo


def dot_nt(a, b):
    return lax.dot_general(a, b, (((1,), (1,)), ((), ())), preferred_element_type=F32)


def head_cols(j):
    return slice(j * HD, (j + 1) * HD)


def tail_kernel(hpb, mask_ref, k_ref, v_ref, t_ref):
    mask = mask_ref[...]
    for j in range(hpb):
        masked = v_ref[:, head_cols(j)] * mask
        t_ref[j] = lax.dot_general(
            k_ref[:, head_cols(j)], masked, (((0,), (0,)), ((), ())), preferred_element_type=F32
        )


def lin_local_kernel(hpb, dq_ref, dk_ref, q_ref, k_ref, v_ref, lin_ref):
    rows = q_ref.shape[0]
    row = lax.broadcasted_iota(jnp.int32, (rows, rows), 0)
    col = lax.broadcasted_iota(jnp.int32, (rows, rows), 1)
    visible = (dq_ref[...] == dk_ref[...]) & (col <= row)
    for j in range(hpb):
        scores = dot_nt(q_ref[:, head_cols(j)], k_ref[:, head_cols(j)])
        scores = jnp.where(visible, scores, 0.0)
        hi, lo = split_bf16(scores)
        v = v_ref[:, head_cols(j)]
        lin_ref[:, head_cols(j)] = jnp.dot(hi, v, preferred_element_type=F32) + jnp.dot(
            lo, v, preferred_element_type=F32
        )


def lin_finish_kernel(hpb, sees_ref, q_ref, c_ref, lin_ref, g_ref, o_ref):
    sees = sees_ref[...]
    for j in range(hpb):
        hi, lo = split_bf16(c_ref[j])
        q = q_ref[:, head_cols(j)]
        carried = jnp.dot(q, hi, preferred_element_type=F32) + jnp.dot(
            q, lo, preferred_element_type=F32
        )
        lin = lin_ref[:, head_cols(j)] + carried * sees
        mean_sq = jnp.mean(lin * lin, axis=-1, keepdims=True)
        normed = lin * lax.rsqrt(mean_sq + 1e-06) * g_ref[:, head_cols(j)]
        o_ref[:, head_cols(j)] = normed.astype(o_ref.dtype)


def col_spec(rows, width=HD):
    return pl.BlockSpec((rows, width), lambda h: (0, h))


def full_spec(shape):
    return pl.BlockSpec(shape, lambda h: (0,) * len(shape))


def params():
    return pltpu.CompilerParams(dimension_semantics=("arbitrary",))


def soft_kernel(blocks, hpb, need_ref, bias_ref, q_ref, *rest):
    key_refs = rest[0:blocks]
    value_refs = rest[blocks : 2 * blocks]
    o_ref = rest[2 * blocks]
    s_ref, mx_ref, tot_ref, acc_ref = rest[2 * blocks + 1 :]
    scale = 1.0 / math.sqrt(HD)
    for j in range(hpb):
        q = q_ref[:, head_cols(j)]
        first = dot_nt(q, key_refs[0][...]) * scale + bias_ref[0]
        s_ref[0] = first
        mx_ref[...] = jnp.max(first, axis=-1, keepdims=True)
        for m in range(1, blocks):

            @pl.when(need_ref[m] > 0)
            def _():
                s = dot_nt(q, key_refs[m][...]) * scale + bias_ref[m]
                s_ref[m] = s
                mx_ref[...] = jnp.maximum(mx_ref[...], jnp.max(s, axis=-1, keepdims=True))

        weights = jnp.exp(s_ref[0] - mx_ref[...])
        tot_ref[...] = jnp.sum(weights, axis=-1, keepdims=True)
        acc_ref[...] = jnp.dot(
            weights.astype(BF16), value_refs[0][...], preferred_element_type=F32
        )
        for m in range(1, blocks):

            @pl.when(need_ref[m] > 0)
            def _():
                w = jnp.exp(s_ref[m] - mx_ref[...])
                tot_ref[...] += jnp.sum(w, axis=-1, keepdims=True)
                acc_ref[...] += jnp.dot(
                    w.astype(BF16), value_refs[m][...], preferred_element_type=F32
                )

        o_ref[:, head_cols(j)] = (acc_ref[...] / tot_ref[...]).astype(o_ref.dtype)


def body(lin_query, lin_key, lin_value, norm_gain, soft_query, soft_key, soft_value, doc_lengths):
    rows, width = lin_query.shape
    local_heads = width // HD
    shard_index = lax.axis_index("ctx")
    shard_start = shard_index * rows
    offsets = jnp.arange(rows, dtype=jnp.int32)
    own_docs = document_index(doc_lengths, shard_start + offsets)
    edges = document_index(
        doc_lengths,
        jnp.stack(
            [
                shard_start - 1,
                shard_start + rows - 1,
                shard_start - rows - 1,
                shard_start - 2 * rows - 1,
            ]
        ),
    )
    before_doc, last_doc, before1, before2 = edges[0], edges[1], edges[2], edges[3]

    head_devices = lax.axis_size("head")
    group_size = HEADS // KV_HEADS
    per_device = HEADS // head_devices
    kv_local = max(1, per_device // group_size)
    kv_table = (
        np.arange(head_devices)[:, None] * per_device // group_size + np.arange(kv_local)[None, :]
    ).reshape(-1)
    short_rows = soft_key.shape[0]

    def spread(field):
        if np.array_equal(kv_table, np.arange(KV_HEADS)):
            return field.reshape(short_rows, head_devices, kv_local * HD)
        taken = jnp.take(field.reshape(short_rows, KV_HEADS, HD), kv_table, axis=1)
        return taken.reshape(short_rows, head_devices, kv_local * HD)

    packed = jnp.concatenate(
        [
            soft_query.reshape(short_rows, head_devices, per_device * HD),
            spread(soft_key),
            spread(soft_value),
        ],
        axis=2,
    )
    per_dest = packed.shape[2]
    packed = packed.reshape(short_rows, head_devices * per_dest)
    mixed = lax.all_to_all(packed, "head", split_axis=1, concat_axis=0, tiled=True)
    own_kv = mixed[:, per_device * HD :]
    older = [from_behind(own_kv, "ctx", step) for step in range(1, SPAN + 1)]

    lhpb = min(local_heads, group_size)
    lsteps = local_heads // lhpb
    lwide = lhpb * HD
    tail_mask = (own_docs == last_doc).astype(BF16)[:, None]
    tail = pl.pallas_call(
        lambda *refs: tail_kernel(lhpb, *refs),
        out_shape=jax.ShapeDtypeStruct((local_heads, HD, HD), F32),
        grid=(lsteps,),
        in_specs=[full_spec((rows, 1)), col_spec(rows, lwide), col_spec(rows, lwide)],
        out_specs=pl.BlockSpec((lhpb, HD, HD), lambda h: (h, 0, 0)),
        compiler_params=params(),
        cost_estimate=pl.CostEstimate(
            flops=2 * rows * HD * HD * local_heads,
            transcendentals=0,
            bytes_accessed=2 * rows * width * 2 + local_heads * HD * HD * 4,
        ),
    )(tail_mask, lin_key, lin_value)
    tails = [from_behind(tail, "ctx", step) for step in range(1, SPAN + 1)]

    lin_local = pl.pallas_call(
        lambda *refs: lin_local_kernel(lhpb, *refs),
        out_shape=jax.ShapeDtypeStruct((rows, width), F32),
        grid=(lsteps,),
        in_specs=[
            full_spec((rows, 1)),
            full_spec((1, rows)),
            col_spec(rows, lwide),
            col_spec(rows, lwide),
            col_spec(rows, lwide),
        ],
        out_specs=col_spec(rows, lwide),
        compiler_params=params(),
        cost_estimate=pl.CostEstimate(
            flops=6 * rows * rows * HD * local_heads,
            transcendentals=0,
            bytes_accessed=3 * rows * width * 2 + rows * width * 4,
        ),
    )(own_docs[:, None], own_docs[None, :], lin_query, lin_key, lin_value)

    blocks = SPAN + 1
    key_docs = jnp.stack(
        [
            document_index(doc_lengths, (shard_index - step) * rows + offsets)
            for step in range(blocks)
        ]
    )
    causal = offsets[None, :] <= offsets[:, None]
    visible = own_docs[None, :, None] == key_docs[:, None, :]
    visible = visible & jnp.concatenate(
        [causal[None], jnp.ones((SPAN, rows, rows), jnp.bool_)], axis=0
    )
    bias = jnp.where(visible, 0.0, -1e30).astype(F32)
    need = (key_docs[:, rows - 1] == own_docs[0]).astype(jnp.int32)
    shpb = min(per_device, group_size)
    ssteps = per_device // shpb
    kv_index = lambda i: (i * shpb * kv_local) // per_device
    own_k_spec = pl.BlockSpec((rows, HD), lambda i: (0, per_device + kv_index(i)))
    own_v_spec = pl.BlockSpec((rows, HD), lambda i: (0, per_device + kv_local + kv_index(i)))
    old_k_spec = pl.BlockSpec((rows, HD), lambda i: (0, kv_index(i)))
    old_v_spec = pl.BlockSpec((rows, HD), lambda i: (0, kv_local + kv_index(i)))
    attended = pl.pallas_call(
        lambda *refs: soft_kernel(blocks, shpb, *refs),
        out_shape=jax.ShapeDtypeStruct((rows, per_device * HD), BF16),
        grid=(ssteps,),
        in_specs=[
            pl.BlockSpec(memory_space=pltpu.SMEM),
            full_spec((blocks, rows, rows)),
            col_spec(rows, shpb * HD),
        ]
        + [own_k_spec]
        + [old_k_spec] * SPAN
        + [own_v_spec]
        + [old_v_spec] * SPAN,
        out_specs=col_spec(rows, shpb * HD),
        scratch_shapes=[
            pltpu.VMEM((blocks, rows, rows), F32),
            pltpu.VMEM((rows, 1), F32),
            pltpu.VMEM((rows, 1), F32),
            pltpu.VMEM((rows, HD), F32),
        ],
        compiler_params=params(),
        cost_estimate=pl.CostEstimate(
            flops=4 * rows * rows * blocks * HD * per_device,
            transcendentals=rows * rows * blocks * per_device,
            bytes_accessed=rows * per_device * HD * 4 + 2 * blocks * rows * HD * 2 * per_device,
        ),
    )(need, bias, mixed, mixed, *older, mixed, *older)

    through1 = (before1 == before_doc).astype(F32)
    through2 = (before2 == before1).astype(F32)
    carried = tails[0] + through1 * (tails[1] + through2 * tails[2])
    sees_carry = (own_docs == before_doc).astype(F32)[:, None]
    lightning_out = pl.pallas_call(
        lambda *refs: lin_finish_kernel(lhpb, *refs),
        out_shape=jax.ShapeDtypeStruct((rows, width), BF16),
        grid=(lsteps,),
        in_specs=[
            full_spec((rows, 1)),
            col_spec(rows, lwide),
            pl.BlockSpec((lhpb, HD, HD), lambda h: (h, 0, 0)),
            col_spec(rows, lwide),
            pl.BlockSpec((1, lwide), lambda h: (0, h)),
        ],
        out_specs=col_spec(rows, lwide),
        compiler_params=params(),
        cost_estimate=pl.CostEstimate(
            flops=4 * rows * HD * HD * local_heads,
            transcendentals=rows * local_heads,
            bytes_accessed=rows * width * (2 + 4 + 2) + local_heads * HD * HD * 4,
        ),
    )(sees_carry, lin_query, carried, lin_local, norm_gain.reshape(1, width))
    return (lightning_out, attended)


def solution(mesh):
    placed = (
        P("ctx", "head"),
        P("ctx", "head"),
        P("ctx", "head"),
        P("head"),
        P(("ctx", "head"), None),
        P(("ctx", "head"), None),
        P(("ctx", "head"), None),
        P(),
    )
    return jax.shard_map(
        body,
        mesh=mesh,
        in_specs=placed,
        out_specs=(P("ctx", "head"), P("ctx", "head")),
        check_vma=False,
    )
```

profile of v0, /device:TPU:9, one launch (start us, length us, event | category | flops | bytes accessed | tf_op | source)
XLA Modules:
  0.0 122.1 jit_solution(8275570291690072527)
XLA Ops:
  0.6 0.9 reduce-window.8
  2.8 1.3 %compare_convert_fusion = (bf16[256,1]{1,0:T(8,128)(2,1)}, s32[256,1]{1,0:T(8,128)}) fusion(s32[]{:T(128)} %bitcast.8, s32[256,1]{1,0:T(8,128)S(1)} %copy.17, s32[]{:T(128)S(6)} %mul.25), kind=kLoop, calls=%fused_computation.9 | loop fusion | flops 1280 | bytes 2568 | tf_op jit(solution)/shard_map/convert_element_type | solution.py:187
  4.1 2.9 %shard_map.95 = f32[16,128,128]{2,1,0:T(8,128)} custom-call(bf16[256,1]{1,0:T(8,128)(2,1)} %get-tuple-element.6.refs_0_, bf16[256,2048]{1,0:T(8,128)(2,1)} %refs_3_.1, bf16[256,2048]{1,0:T(8,128)(2,1)} %refs_4_.1), custom_call_target="tpu_custom_call" | custom-call | flops 134217728 | bytes 3145728 | tf_op jit(solution)/shard_map/pallas_call | solution.py:188
  7.0 3.8 %collective-permute-start = (f32[16,128,128]{2,1,0:T(8,128)}, f32[16,128,128]{2,1,0:T(8,128)S(1)}, u32[]{:S(2)}, u32[]{:S(2)}) collective-permute-start(f32[16,128,128]{2,1,0:T(8,128)} %shard_map.95), channel_id=1, source_target_pairs={{0,4},{4,8},{8,12},{12,16},{16,20},{20,24},{24,28},{1,5},{5,9},{9,... | collective-permute-start | bytes 3145736 | tf_op jit(solution)/shard_map/ppermute | solution.py:31
  10.7 3.2 %collective-permute-start.1 = (f32[16,128,128]{2,1,0:T(8,128)}, f32[16,128,128]{2,1,0:T(8,128)S(1)}, u32[]{:S(2)}, u32[]{:S(2)}) collective-permute-start(f32[16,128,128]{2,1,0:T(8,128)} %shard_map.95), channel_id=1, source_target_pairs={{0,8},{4,12},{8,16},{12,20},{16,24},{20,28},{1,9},{5,13},{9,17},{1... | collective-permute-start | bytes 3145736 | tf_op jit(solution)/shard_map/ppermute | solution.py:31
  14.0 1.9 %collective-permute-start.2 = (f32[16,128,128]{2,1,0:T(8,128)}, f32[16,128,128]{2,1,0:T(8,128)}, u32[]{:S(2)}, u32[]{:S(2)}) collective-permute-start(f32[16,128,128]{2,1,0:T(8,128)} %shard_map.95), channel_id=1, source_target_pairs={{0,12},{4,16},{8,20},{12,24},{16,28},{1,13},{5,17},{9,21},{13,25},... | collective-permute-start | bytes 3145736 | tf_op jit(solution)/shard_map/ppermute | solution.py:31
  16.0 1.2 pad_maximum_fusion
  17.2 3.5 %all-to-all-start = ((bf16[64,4,2560]{2,0,1:T(8,128)(2,1)}), bf16[64,4,2560]{2,0,1:T(8,128)(2,1)S(1)}, u32[]{:S(2)}, u32[]{:S(2)}) async-start(bf16[64,4,2560]{2,0,1:T(8,128)(2,1)} %pad_maximum_fusion), calls=%async_computation | async-start | bytes 2621440 | tf_op jit(solution)/shard_map/all_to_all | solution.py:180
  21.9 6.2 %shard_map.96.refs_3_ = f32[256,2048]{1,0:T(8,128)} custom-call(s32[256,1]{1,0:T(8,128)} %get-tuple-element.7.refs_0_, s32[1,256]{1,0:T(1,128)} %compare_select_fusion.3.refs_1_, bf16[256,2048]{1,0:T(8,128)(2,1)} %refs_1_.3, bf16[256,2048]{1,0:T(8,128)(2,1)} %refs_3_.1, bf16[256,2048]{1,0:T(8,128)(2,1)} %refs_4_.1), custom_call_target="tpu_custom_call" | custom-call | flops 805306368 | bytes 5242880 | tf_op jit(solution)/shard_map/pallas_call | solution.py:203
  31.2 0.7 pad_add_fusion
  31.9 1.4 %convert_reduce_fusion.4.refs_0_ = s32[4]{0:T(128)} fusion(s32[4,256]{1,0:T(4,128)S(1)} %pad_add_fusion, s32[]{:T(128)} %bitcast.16), kind=kLoop, calls=%fused_computation.21 | loop fusion | flops 8 | bytes 36 | tf_op jit(solution)/shard_map/convert_element_type | solution.py:236
  33.4 1.3 %compare_convert_fusion.1.refs_0_ = f32[256,1]{1,0:T(8,128)} fusion(s32[256,1]{1,0:T(8,128)S(1)} %copy-done.1, s32[]{:T(128)} %bitcast.7), kind=kLoop, calls=%fused_computation.10 | loop fusion | flops 512 | bytes 2052 | tf_op jit(solution)/shard_map/convert_element_type | solution.py:275
  34.6 1.2 and_select_fusion.refs_1_
  35.9 0.8 all-to-all-done
  36.6 0.8 slice.29
  37.4 2.6 %collective-permute-start.3 = (bf16[256,512]{1,0:T(8,128)(2,1)}, bf16[256,512]{1,0:T(8,128)(2,1)}, u32[]{:S(2)}, u32[]{:S(2)}) collective-permute-start(bf16[256,512]{1,0:T(8,128)(2,1)} %slice.29), channel_id=1, source_target_pairs={{0,4},{4,8},{8,12},{12,16},{16,20},{20,24},{24,28},{1,5},{5,9},{9,... | collective-permute-start | bytes 786440 | tf_op jit(solution)/shard_map/ppermute | solution.py:31
  40.0 1.9 %collective-permute-start.4 = (bf16[256,512]{1,0:T(8,128)(2,1)}, bf16[256,512]{1,0:T(8,128)(2,1)}, u32[]{:S(2)}, u32[]{:S(2)}) collective-permute-start(bf16[256,512]{1,0:T(8,128)(2,1)} %slice.29), channel_id=1, source_target_pairs={{0,8},{4,12},{8,16},{12,20},{16,24},{20,28},{1,9},{5,13},{9,17},{1... | collective-permute-start | bytes 786440 | tf_op jit(solution)/shard_map/ppermute | solution.py:31
  42.0 2.1 %collective-permute-start.5 = (bf16[256,512]{1,0:T(8,128)(2,1)}, bf16[256,512]{1,0:T(8,128)(2,1)}, u32[]{:S(2)}, u32[]{:S(2)}) collective-permute-start(bf16[256,512]{1,0:T(8,128)(2,1)} %slice.29), channel_id=1, source_target_pairs={{0,12},{4,16},{8,20},{12,24},{16,28},{1,13},{5,17},{9,21},{13,25},... | collective-permute-start | bytes 786440 | tf_op jit(solution)/shard_map/ppermute | solution.py:31
  44.1 10.4 %collective-permute-done.1 = f32[16,128,128]{2,1,0:T(8,128)S(1)} collective-permute-done((f32[16,128,128]{2,1,0:T(8,128)}, f32[16,128,128]{2,1,0:T(8,128)S(1)}, u32[]{:S(2)}, u32[]{:S(2)}) %collective-permute-start.1) | collective-permute-done | bytes 1048608 | tf_op jit(solution)/shard_map/ppermute | solution.py:31
  54.5 32.9 %collective-permute-done.2 = f32[16,128,128]{2,1,0:T(8,128)} collective-permute-done((f32[16,128,128]{2,1,0:T(8,128)}, f32[16,128,128]{2,1,0:T(8,128)}, u32[]{:S(2)}, u32[]{:S(2)}) %collective-permute-start.2) | collective-permute-done | bytes 1048608 | tf_op jit(solution)/shard_map/ppermute | solution.py:31
  87.4 2.4 %multiply_add_fusion.refs_2_ = f32[16,128,128]{2,1,0:T(8,128)} fusion(f32[16,128,128]{2,1,0:T(8,128)S(1)} %collective-permute-done, f32[16,128,128]{2,1,0:T(8,128)S(1)} %collective-permute-done.1, f32[16,128,128]{2,1,0:T(8,128)} %collective-permute-done.2, f32[]{:T(128)S(6)} %convert_element_type.52, f32[]{:T(128)S(6)} %convert_element_type.51), kind=kLoop, calls=%fused_computation.2 | loop fusion | flops 1048576 | bytes 4194312 | tf_op jit(solution)/shard_map/add | solution.py:274
  89.8 3.7 %shard_map.97 = bf16[256,2048]{1,0:T(8,128)(2,1)} custom-call(f32[256,1]{1,0:T(8,128)} %compare_convert_fusion.1.refs_0_, bf16[256,2048]{1,0:T(8,128)(2,1)} %refs_1_.3, f32[16,128,128]{2,1,0:T(8,128)} %multiply_add_fusion.refs_2_, f32[256,2048]{1,0:T(8,128)} %shard_map.96.refs_3_, f32[1,2048]{1,0:T(1,128)} %bitcast.40), custom_call_target="tpu_custom_call" | custom-call | flops 268435456 | bytes 5242880 | tf_op jit(solution)/shard_map/pallas_call | solution.py:276
  93.5 2.3 %collective-permute-done.5.refs_6_.refs_10_ = bf16[256,512]{1,0:T(8,128)(2,1)} collective-permute-done((bf16[256,512]{1,0:T(8,128)(2,1)}, bf16[256,512]{1,0:T(8,128)(2,1)}, u32[]{:S(2)}, u32[]{:S(2)}) %collective-permute-start.5) | collective-permute-done | bytes 262176 | tf_op jit(solution)/shard_map/ppermute | solution.py:31
  95.8 26.3 %shard_map.98 = bf16[256,2048]{1,0:T(8,128)(2,1)} custom-call(s32[4]{0:T(128)} %convert_reduce_fusion.4.refs_0_, f32[4,256,256]{2,1,0:T(8,128)} %and_select_fusion.refs_1_, bf16[256,2560]{1,0:T(8,128)(2,1)} %bitcast.32, bf16[256,2560]{1,0:T(8,128)(2,1)} %bitcast.33, bf16[256,512]{1,0:T(8,128)(2,1)} %collective-permute-done.3.refs_4_.refs_8_, ...), custom_call_target="tpu_custom_call" | custom-call | flops 2147483648 | bytes 10485760 | tf_op jit(solution)/shard_map/pallas_call | solution.py:244
  (32 shorter events, 3.1 us)
Async XLA Ops:
  0.6 15.3 %copy-start.2 = (bf16[64,8192]{1,0:T(8,128)(2,1)S(1)}, bf16[64,8192]{1,0:T(8,128)(2,1)}, u32[]{:S(2)}) copy-start(bf16[64,8192]{1,0:T(8,128)(2,1)} %param.12) | copy-start | bytes 3145732
  4.1 11.9 %copy-start.3 = (bf16[64,1024]{1,0:T(8,128)(2,1)S(1)}, bf16[64,1024]{1,0:T(8,128)(2,1)}, u32[]{:S(2)}) copy-start(bf16[64,1024]{1,0:T(8,128)(2,1)} %param.14) | copy-start | bytes 393220
  4.1 11.9 %copy-start.4 = (bf16[64,1024]{1,0:T(8,128)(2,1)S(1)}, bf16[64,1024]{1,0:T(8,128)(2,1)}, u32[]{:S(2)}) copy-start(bf16[64,1024]{1,0:T(8,128)(2,1)} %param.13) | copy-start | bytes 393220
  7.0 35.0 %collective-permute-start = (f32[16,128,128]{2,1,0:T(8,128)}, f32[16,128,128]{2,1,0:T(8,128)S(1)}, u32[]{:S(2)}, u32[]{:S(2)}) collective-permute-start(f32[16,128,128]{2,1,0:T(8,128)} %shard_map.95), channel_id=1, source_target_pairs={{0,4},{4,8},{8,12},{12,16},{16,20},{20,24},{24,28},{1,5},{5,9},{9,... | collective-permute-start | bytes 3145736 | tf_op jit(solution)/shard_map/ppermute | solution.py:31
  10.7 43.7 %collective-permute-start.1 = (f32[16,128,128]{2,1,0:T(8,128)}, f32[16,128,128]{2,1,0:T(8,128)S(1)}, u32[]{:S(2)}, u32[]{:S(2)}) collective-permute-start(f32[16,128,128]{2,1,0:T(8,128)} %shard_map.95), channel_id=1, source_target_pairs={{0,8},{4,12},{8,16},{12,20},{16,24},{20,28},{1,9},{5,13},{9,17},{1... | collective-permute-start | bytes 3145736 | tf_op jit(solution)/shard_map/ppermute | solution.py:31
  14.0 73.4 %collective-permute-start.2 = (f32[16,128,128]{2,1,0:T(8,128)}, f32[16,128,128]{2,1,0:T(8,128)}, u32[]{:S(2)}, u32[]{:S(2)}) collective-permute-start(f32[16,128,128]{2,1,0:T(8,128)} %shard_map.95), channel_id=1, source_target_pairs={{0,12},{4,16},{8,20},{12,24},{16,28},{1,13},{5,17},{9,21},{13,25},... | collective-permute-start | bytes 3145736 | tf_op jit(solution)/shard_map/ppermute | solution.py:31
  17.2 19.5 %all-to-all-start = ((bf16[64,4,2560]{2,0,1:T(8,128)(2,1)}), bf16[64,4,2560]{2,0,1:T(8,128)(2,1)S(1)}, u32[]{:S(2)}, u32[]{:S(2)}) async-start(bf16[64,4,2560]{2,0,1:T(8,128)(2,1)} %pad_maximum_fusion), calls=%async_computation | async-start | bytes 2621440 | tf_op jit(solution)/shard_map/all_to_all | solution.py:180
  21.9 9.3 %copy-start.5 = (s32[1,256]{1,0:T(1,128)S(1)}, s32[1,256]{1,0:T(1,128)}, u32[]{:S(2)}) copy-start(s32[1,256]{1,0:T(1,128)} %compare_select_fusion.3.refs_1_) | copy-start | bytes 3076
  21.9 11.4 %copy-start.1 = (s32[256,1]{1,0:T(8,128)S(1)}, s32[256,1]{1,0:T(8,128)}, u32[]{:S(2)}) copy-start(s32[256,1]{1,0:T(8,128)} %get-tuple-element.7.refs_0_) | copy-start | bytes 3076
  36.6 53.1 %copy-start = (bf16[64,4,2560]{2,0,1:T(8,128)(2,1)}, bf16[64,4,2560]{2,0,1:T(8,128)(2,1)S(1)}, u32[]{:S(2)}) copy-start(bf16[64,4,2560]{2,0,1:T(8,128)(2,1)S(1)} %all-to-all-done) | copy-start | bytes 3932164
  37.4 56.1 %collective-permute-start.3 = (bf16[256,512]{1,0:T(8,128)(2,1)}, bf16[256,512]{1,0:T(8,128)(2,1)}, u32[]{:S(2)}, u32[]{:S(2)}) collective-permute-start(bf16[256,512]{1,0:T(8,128)(2,1)} %slice.29), channel_id=1, source_target_pairs={{0,4},{4,8},{8,12},{12,16},{16,20},{20,24},{24,28},{1,5},{5,9},{9,... | collective-permute-start | bytes 786440 | tf_op jit(solution)/shard_map/ppermute | solution.py:31
  40.0 53.5 %collective-permute-start.4 = (bf16[256,512]{1,0:T(8,128)(2,1)}, bf16[256,512]{1,0:T(8,128)(2,1)}, u32[]{:S(2)}, u32[]{:S(2)}) collective-permute-start(bf16[256,512]{1,0:T(8,128)(2,1)} %slice.29), channel_id=1, source_target_pairs={{0,8},{4,12},{8,16},{12,20},{16,24},{20,28},{1,9},{5,13},{9,17},{1... | collective-permute-start | bytes 786440 | tf_op jit(solution)/shard_map/ppermute | solution.py:31
  42.0 53.9 %collective-permute-start.5 = (bf16[256,512]{1,0:T(8,128)(2,1)}, bf16[256,512]{1,0:T(8,128)(2,1)}, u32[]{:S(2)}, u32[]{:S(2)}) collective-permute-start(bf16[256,512]{1,0:T(8,128)(2,1)} %slice.29), channel_id=1, source_target_pairs={{0,12},{4,16},{8,20},{12,24},{16,28},{1,13},{5,17},{9,21},{13,25},... | collective-permute-start | bytes 786440 | tf_op jit(solution)/shard_map/ppermute | solution.py:31
where the time goes:
time: 124 us; the launch traced here: 122 us
  waiting for transfers between devices  46.4 us (37%)
  Pallas kernels  39.1 us (32%)
  starting transfers between devices  19 us (15%)
  other arithmetic  12.1 us (10%)
  between operations  3.32 us (3%)
  local copies, waits for them, and re-layouts  2.14 us (2%)
    ppermute x6, waiting for transfers between devices, from_behind(): return lax.ppermute(value, axis, pairs)  45.6 us
    pallas_call x1, Pallas kernels, body(): pl.pallas_call(lambda *refs: soft_kernel(blocks, shpb, *refs), out_shape=...  26.3 us
    ppermute x6, starting transfers between devices, from_behind(): return lax.ppermute(value, axis, pairs)  15.5 us
    pallas_call x1, Pallas kernels, body(): pl.pallas_call(lambda *refs: lin_local_kernel(lhpb, *refs), out_shape=jax...  6.23 us
    pallas_call x1, Pallas kernels, body(): pl.pallas_call(lambda *refs: lin_finish_kernel(lhpb, *refs), out_shape=ja...  3.71 us
    all_to_all x1, starting transfers between devices, body(): lax.all_to_all(packed, 'head', split_axis=1, concat_axis=0, tiled=True)  3.54 us
    pallas_call x1, Pallas kernels, body(): pl.pallas_call(lambda *refs: tail_kernel(lhpb, *refs), out_shape=jax.Shap...  2.86 us
  transfers between devices with their start and end apart: 7, of which 4 were waited for; matrix products, arithmetic and copies ran while one was open for 9% of the time, Pallas kernels for 8%

commit v1 on v0

--- a/solution.py
+++ b/solution.py
@@ -179,7 +179,11 @@
     packed = packed.reshape(short_rows, head_devices * per_dest)
     mixed = lax.all_to_all(packed, "head", split_axis=1, concat_axis=0, tiled=True)
     own_kv = mixed[:, per_device * HD :]
-    older = [from_behind(own_kv, "ctx", step) for step in range(1, SPAN + 1)]
+    older = []
+    moving = own_kv
+    for _ in range(SPAN):
+        moving = from_behind(moving, "ctx", 1)
+        older.append(moving)
 
     lhpb = min(local_heads, group_size)
     lsteps = local_heads // lhpb
@@ -198,7 +202,11 @@
             bytes_accessed=2 * rows * width * 2 + local_heads * HD * HD * 4,
         ),
     )(tail_mask, lin_key, lin_value)
-    tails = [from_behind(tail, "ctx", step) for step in range(1, SPAN + 1)]
+    through_own = (before_doc == last_doc).astype(F32)
+    received = from_behind(tail, "ctx", 1)
+    for _ in range(SPAN - 1):
+        received = from_behind(tail + through_own * received, "ctx", 1)
+    carried = received
 
     lin_local = pl.pallas_call(
         lambda *refs: lin_local_kernel(lhpb, *refs),
@@ -269,9 +277,6 @@
         ),
     )(need, bias, mixed, mixed, *older, mixed, *older)
 
-    through1 = (before1 == before_doc).astype(F32)
-    through2 = (before2 == before1).astype(F32)
-    carried = tails[0] + through1 * (tails[1] + through2 * tails[2])
     sees_carry = (own_docs == before_doc).astype(F32)[:, None]
     lightning_out = pl.pallas_call(
         lambda *refs: lin_finish_kernel(lhpb, *refs),

time: 124 us -> 104 us (0.84)
  the two profiles are of different devices: /device:TPU:9 before, /device:TPU:8 now
where the time goes in v1:
time: 104 us; the launch traced here: 102 us
  Pallas kernels  39.1 us (38%)
  waiting for transfers between devices  26.3 us (25%)
  starting transfers between devices  17.6 us (17%)
  other arithmetic  14.6 us (14%)
  local copies, waits for them, and re-layouts  2.43 us (2%)
  between operations  2.1 us (2%)
    pallas_call x1, Pallas kernels, body(): pl.pallas_call(lambda *refs: soft_kernel(blocks, shpb, *refs), out_shape=...  26.3 us
    ppermute x6, waiting for transfers between devices, from_behind(): return lax.ppermute(value, axis, pairs)  25.3 us
    ppermute x6, starting transfers between devices, from_behind(): return lax.ppermute(value, axis, pairs)  13.9 us
    pallas_call x1, Pallas kernels, body(): pl.pallas_call(lambda *refs: lin_local_kernel(lhpb, *refs), out_shape=jax...  6.21 us
    all_to_all x1, starting transfers between devices, body(): lax.all_to_all(packed, 'head', split_axis=1, concat_axis=0, tiled=True)  3.72 us
    pallas_call x1, Pallas kernels, body(): pl.pallas_call(lambda *refs: lin_finish_kernel(lhpb, *refs), out_shape=ja...  3.7 us
    select_n x6, other arithmetic, document_index(): return jnp.where(positions < 0, -1, counted).astype(jnp.int32)  3.08 us
    pallas_call x1, Pallas kernels, body(): pl.pallas_call(lambda *refs: tail_kernel(lhpb, *refs), out_shape=jax.Shap...  2.89 us
  transfers between devices with their start and end apart: 7, of which 4 were waited for; matrix products, arithmetic and copies ran while one was open for 12% of the time, Pallas kernels for 32%

profile of v1, /device:TPU:8, one launch (start us, length us, event | category | flops | bytes accessed | tf_op | source)
XLA Modules:
  0.0 102.1 jit_solution(4376510128504560293)
XLA Ops:
  3.3 1.2 %compare_convert_fusion = (bf16[256,1]{1,0:T(8,128)(2,1)}, s32[256,1]{1,0:T(8,128)S(1)}) fusion(s32[]{:T(128)} %bitcast.8, s32[256,1]{1,0:T(8,128)S(1)} %copy.17, s32[]{:T(128)S(6)} %mul.23), kind=kLoop, calls=%fused_computation.10 | loop fusion | flops 1280 | bytes 2568 | tf_op jit(solution)/shard_map/convert_element_type | solution.py:191
  4.5 2.9 %shard_map.95 = f32[16,128,128]{2,1,0:T(8,128)} custom-call(bf16[256,1]{1,0:T(8,128)(2,1)} %get-tuple-element.6.refs_0_, bf16[256,2048]{1,0:T(8,128)(2,1)} %refs_3_.1, bf16[256,2048]{1,0:T(8,128)(2,1)} %refs_4_.1), custom_call_target="tpu_custom_call" | custom-call | flops 134217728 | bytes 3145728 | tf_op jit(solution)/shard_map/pallas_call | solution.py:192
  7.4 1.9 %collective-permute-start = (f32[16,128,128]{2,1,0:T(8,128)}, f32[16,128,128]{2,1,0:T(8,128)}, u32[]{:S(2)}, u32[]{:S(2)}) collective-permute-start(f32[16,128,128]{2,1,0:T(8,128)} %shard_map.95), channel_id=1, source_target_pairs={{0,4},{4,8},{8,12},{12,16},{16,20},{20,24},{24,28},{1,5},{5,9},{9,... | collective-permute-start | bytes 3145736 | tf_op jit(solution)/shard_map/ppermute | solution.py:31
  9.5 1.2 %pad_maximum_fusion = bf16[64,4,2560]{2,0,1:T(8,128)(2,1)} fusion(bf16[64,4,256]{2,0,1:T(8,128)(2,1)S(1)} %get-tuple-element.14, bf16[64,4,256]{2,0,1:T(8,128)(2,1)S(1)} %get-tuple-element.15, bf16[64,4,2048]{2,0,1:T(8,128)(2,1)S(1)} %bitcast.28), kind=kLoop, calls=%fused_computation | loop fusion | flops 3932160 | bytes 2621440 | tf_op jit(solution)/shard_map/concatenate | solution.py:170
  10.7 3.7 %all-to-all-start = ((bf16[64,4,2560]{2,0,1:T(8,128)(2,1)}), bf16[64,4,2560]{2,0,1:T(8,128)(2,1)S(1)}, u32[]{:S(2)}, u32[]{:S(2)}) async-start(bf16[64,4,2560]{2,0,1:T(8,128)(2,1)} %pad_maximum_fusion), calls=%async_computation | async-start | bytes 2621440 | tf_op jit(solution)/shard_map/all_to_all | solution.py:180
  15.6 8.2 %collective-permute-done = f32[16,128,128]{2,1,0:T(8,128)} collective-permute-done((f32[16,128,128]{2,1,0:T(8,128)}, f32[16,128,128]{2,1,0:T(8,128)}, u32[]{:S(2)}, u32[]{:S(2)}) %collective-permute-start) | collective-permute-done | bytes 1048608 | tf_op jit(solution)/shard_map/ppermute | solution.py:31
  23.8 1.3 %multiply_add_fusion.1 = f32[16,128,128]{2,1,0:T(8,128)S(1)} fusion(f32[16,128,128]{2,1,0:T(8,128)S(1)} %copy-done, f32[16,128,128]{2,1,0:T(8,128)} %collective-permute-done, f32[]{:T(128)S(6)} %convert_element_type.48), kind=kLoop, calls=%fused_computation.3 | loop fusion | flops 524288 | bytes 3145732 | tf_op jit(solution)/shard_map/add | solution.py:208
  25.2 1.9 %collective-permute-start.1 = (f32[16,128,128]{2,1,0:T(8,128)S(1)}, f32[16,128,128]{2,1,0:T(8,128)}, u32[]{:S(2)}, u32[]{:S(2)}) collective-permute-start(f32[16,128,128]{2,1,0:T(8,128)S(1)} %multiply_add_fusion.1), channel_id=1, source_target_pairs={{0,4},{4,8},{8,12},{12,16},{16,20},{20,24},{24,28},{1,5},{5,9},{9,... | collective-permute-start | bytes 3145736 | tf_op jit(solution)/shard_map/ppermute | solution.py:31
  27.7 1.2 %compare_select_fusion = s32[1,256]{1,0:T(1,128)} fusion(s32[1,256]{1,0:T(1,128)} %bitcast.41, s32[]{:T(128)S(6)} %mul.29), kind=kLoop, calls=%fused_computation.17 | loop fusion | flops 768 | bytes 2052 | tf_op jit(solution)/shard_map/jit(_where)/select_n | solution.py:23
  28.9 1.2 %compare_select_fusion.1 = s32[1,256]{1,0:T(1,128)} fusion(s32[1,256]{1,0:T(1,128)} %bitcast.40, s32[]{:T(128)S(6)} %mul.28), kind=kLoop, calls=%fused_computation.18 | loop fusion | flops 768 | bytes 2052 | tf_op jit(solution)/shard_map/jit(_where)/select_n | solution.py:23
  30.7 1.0 %all-to-all-done = bf16[64,4,2560]{2,0,1:T(8,128)(2,1)S(1)} async-done(((bf16[64,4,2560]{2,0,1:T(8,128)(2,1)}), bf16[64,4,2560]{2,0,1:T(8,128)(2,1)S(1)}, u32[]{:S(2)}, u32[]{:S(2)}) %all-to-all-start) | async-done | bytes 1310752 | tf_op jit(solution)/shard_map/all_to_all | solution.py:180
  31.8 2.6 %collective-permute-start.3 = (bf16[256,512]{1,0:T(8,128)(2,1)S(1)}, bf16[256,512]{1,0:T(8,128)(2,1)S(1)}, u32[]{:S(2)}, u32[]{:S(2)}) collective-permute-start(bf16[256,512]{1,0:T(8,128)(2,1)S(1)} %slice.21), channel_id=1, source_target_pairs={{0,4},{4,8},{8,12},{12,16},{16,20},{20,24},{24,28},{1,5},{5,9},{9,... | collective-permute-start | bytes 786440 | tf_op jit(solution)/shard_map/ppermute | solution.py:31
  34.4 7.0 %collective-permute-done.1 = f32[16,128,128]{2,1,0:T(8,128)} collective-permute-done((f32[16,128,128]{2,1,0:T(8,128)S(1)}, f32[16,128,128]{2,1,0:T(8,128)}, u32[]{:S(2)}, u32[]{:S(2)}) %collective-permute-start.1) | collective-permute-done | bytes 1048608 | tf_op jit(solution)/shard_map/ppermute | solution.py:31
  41.4 1.3 %multiply_add_fusion = f32[16,128,128]{2,1,0:T(8,128)S(1)} fusion(f32[16,128,128]{2,1,0:T(8,128)S(1)} %copy-done, f32[16,128,128]{2,1,0:T(8,128)} %collective-permute-done.1, f32[]{:T(128)S(6)} %convert_element_type.48), kind=kLoop, calls=%fused_computation.2 | loop fusion | flops 524288 | bytes 3145732 | tf_op jit(solution)/shard_map/add | solution.py:208
  42.7 1.9 %collective-permute-start.2 = (f32[16,128,128]{2,1,0:T(8,128)S(1)}, f32[16,128,128]{2,1,0:T(8,128)S(1)}, u32[]{:S(2)}, u32[]{:S(2)}) collective-permute-start(f32[16,128,128]{2,1,0:T(8,128)S(1)} %multiply_add_fusion), channel_id=1, source_target_pairs={{0,4},{4,8},{8,12},{12,16},{16,20},{20,24},{24,28},{1,5},{5,9},{9,... | collective-permute-start | bytes 3145736 | tf_op jit(solution)/shard_map/ppermute | solution.py:31
  45.4 3.6 %collective-permute-start.4 = (bf16[256,512]{1,0:T(8,128)(2,1)S(1)}, bf16[256,512]{1,0:T(8,128)(2,1)}, u32[]{:S(2)}, u32[]{:S(2)}) collective-permute-start(bf16[256,512]{1,0:T(8,128)(2,1)S(1)} %collective-permute-done.3.refs_4_.refs_8_), channel_id=1, source_target_pairs={{0,4},{4,8},{8,12},{12,16},{16,20},{20,24},{24,28},{1,5},{5,9},{9,... | collective-permute-start | bytes 786440 | tf_op jit(solution)/shard_map/ppermute | solution.py:31
  49.0 1.4 %convert_reduce_fusion.4.refs_0_ = s32[4]{0:T(128)} fusion(s32[4,256]{1,0:T(4,128)S(1)} %pad_add_fusion, s32[]{:T(128)} %bitcast.14), kind=kLoop, calls=%fused_computation.22 | loop fusion | flops 8 | bytes 36 | tf_op jit(solution)/shard_map/convert_element_type | solution.py:244
  50.4 1.3 %compare_convert_fusion.1.refs_0_ = f32[256,1]{1,0:T(8,128)} fusion(s32[256,1]{1,0:T(8,128)S(1)} %get-tuple-element.7.refs_0_, s32[]{:T(128)} %bitcast.7), kind=kLoop, calls=%fused_computation.11 | loop fusion | flops 512 | bytes 2052 | tf_op jit(solution)/shard_map/convert_element_type | solution.py:280
  51.7 10.1 %collective-permute-done.4.refs_5_.refs_9_ = bf16[256,512]{1,0:T(8,128)(2,1)} collective-permute-done((bf16[256,512]{1,0:T(8,128)(2,1)S(1)}, bf16[256,512]{1,0:T(8,128)(2,1)}, u32[]{:S(2)}, u32[]{:S(2)}) %collective-permute-start.4) | collective-permute-done | bytes 262176 | tf_op jit(solution)/shard_map/ppermute | solution.py:31
  61.8 1.9 %collective-permute-start.5 = (bf16[256,512]{1,0:T(8,128)(2,1)}, bf16[256,512]{1,0:T(8,128)(2,1)}, u32[]{:S(2)}, u32[]{:S(2)}) collective-permute-start(bf16[256,512]{1,0:T(8,128)(2,1)} %collective-permute-done.4.refs_5_.refs_9_), channel_id=1, source_target_pairs={{0,4},{4,8},{8,12},{12,16},{16,20},{20,24},{24,28},{1,5},{5,9},{9,... | collective-permute-start | bytes 786440 | tf_op jit(solution)/shard_map/ppermute | solution.py:31
  63.7 6.2 %shard_map.96.refs_3_ = f32[256,2048]{1,0:T(8,128)} custom-call(s32[256,1]{1,0:T(8,128)} %copy-done.2, s32[1,256]{1,0:T(1,128)} %copy-done.8, bf16[256,2048]{1,0:T(8,128)(2,1)} %refs_1_.3, bf16[256,2048]{1,0:T(8,128)(2,1)} %refs_3_.1, bf16[256,2048]{1,0:T(8,128)(2,1)} %refs_4_.1), custom_call_target="tpu_custom_call" | custom-call | flops 805306368 | bytes 5242880 | tf_op jit(solution)/shard_map/pallas_call | solution.py:211
  69.9 1.2 %and_select_fusion.refs_1_ = f32[4,256,256]{2,1,0:T(8,128)} fusion(pred[1,256,256]{2,1,0:T(8,128)(4,1)S(1)} %copy-done.5, s32[4,256]{1,0:T(4,128)S(1)} %pad_add_fusion, s32[256]{0:T(256)S(1)} %compare_select_fusion.4), kind=kLoop, calls=%fused_computation.4 | loop fusion | flops 786432 | bytes 1119232 | tf_op jit(solution)/shard_map/jit(_where)/select_n | solution.py:243
  71.1 26.3 %shard_map.98 = bf16[256,2048]{1,0:T(8,128)(2,1)} custom-call(s32[4]{0:T(128)} %convert_reduce_fusion.4.refs_0_, f32[4,256,256]{2,1,0:T(8,128)} %and_select_fusion.refs_1_, bf16[256,2560]{1,0:T(8,128)(2,1)} %bitcast.30, bf16[256,2560]{1,0:T(8,128)(2,1)} %bitcast.31, bf16[256,512]{1,0:T(8,128)(2,1)} %copy-done.12, ...), custom_call_target="tpu_custom_call" | custom-call | flops 2147483648 | bytes 10485760 | tf_op jit(solution)/shard_map/pallas_call | solution.py:252
  98.4 3.7 %shard_map.97 = bf16[256,2048]{1,0:T(8,128)(2,1)} custom-call(f32[256,1]{1,0:T(8,128)} %compare_convert_fusion.1.refs_0_, bf16[256,2048]{1,0:T(8,128)(2,1)} %refs_1_.3, f32[16,128,128]{2,1,0:T(8,128)} %copy-done.4, f32[256,2048]{1,0:T(8,128)} %shard_map.96.refs_3_, f32[1,2048]{1,0:T(1,128)} %bitcast.38), custom_call_target="tpu_custom_call" | custom-call | flops 268435456 | bytes 5242880 | tf_op jit(solution)/shard_map/pallas_call | solution.py:281
  (47 shorter events, 5.6 us)
Async XLA Ops:
  0.6 8.7 %copy-start.3 = (bf16[64,8192]{1,0:T(8,128)(2,1)S(1)}, bf16[64,8192]{1,0:T(8,128)(2,1)}, u32[]{:S(2)}) copy-start(bf16[64,8192]{1,0:T(8,128)(2,1)} %param.12) | copy-start | bytes 3145732
  4.5 45.8 %copy-start.2 = (s32[256,1]{1,0:T(8,128)}, s32[256,1]{1,0:T(8,128)S(1)}, u32[]{:S(2)}) copy-start(s32[256,1]{1,0:T(8,128)S(1)} %get-tuple-element.7.refs_0_) | copy-start | bytes 3076
  4.5 4.9 %copy-start.6 = (bf16[64,1024]{1,0:T(8,128)(2,1)S(1)}, bf16[64,1024]{1,0:T(8,128)(2,1)}, u32[]{:S(2)}) copy-start(bf16[64,1024]{1,0:T(8,128)(2,1)} %param.14) | copy-start | bytes 393220
  4.5 4.9 %copy-start.7 = (bf16[64,1024]{1,0:T(8,128)(2,1)S(1)}, bf16[64,1024]{1,0:T(8,128)(2,1)}, u32[]{:S(2)}) copy-start(bf16[64,1024]{1,0:T(8,128)(2,1)} %param.13) | copy-start | bytes 393220
  7.4 16.4 %collective-permute-start = (f32[16,128,128]{2,1,0:T(8,128)}, f32[16,128,128]{2,1,0:T(8,128)}, u32[]{:S(2)}, u32[]{:S(2)}) collective-permute-start(f32[16,128,128]{2,1,0:T(8,128)} %shard_map.95), channel_id=1, source_target_pairs={{0,4},{4,8},{8,12},{12,16},{16,20},{20,24},{24,28},{1,5},{5,9},{9,... | collective-permute-start | bytes 3145736 | tf_op jit(solution)/shard_map/ppermute | solution.py:31
  9.5 14.4 %copy-start = (f32[16,128,128]{2,1,0:T(8,128)S(1)}, f32[16,128,128]{2,1,0:T(8,128)}, u32[]{:S(2)}) copy-start(f32[16,128,128]{2,1,0:T(8,128)} %shard_map.95) | copy-start | bytes 3145732
  10.7 21.1 %all-to-all-start = ((bf16[64,4,2560]{2,0,1:T(8,128)(2,1)}), bf16[64,4,2560]{2,0,1:T(8,128)(2,1)S(1)}, u32[]{:S(2)}, u32[]{:S(2)}) async-start(bf16[64,4,2560]{2,0,1:T(8,128)(2,1)} %pad_maximum_fusion), calls=%async_computation | async-start | bytes 2621440 | tf_op jit(solution)/shard_map/all_to_all | solution.py:180
  25.2 16.2 %collective-permute-start.1 = (f32[16,128,128]{2,1,0:T(8,128)S(1)}, f32[16,128,128]{2,1,0:T(8,128)}, u32[]{:S(2)}, u32[]{:S(2)}) collective-permute-start(f32[16,128,128]{2,1,0:T(8,128)S(1)} %multiply_add_fusion.1), channel_id=1, source_target_pairs={{0,4},{4,8},{8,12},{12,16},{16,20},{20,24},{24,28},{1,5},{5,9},{9,... | collective-permute-start | bytes 3145736 | tf_op jit(solution)/shard_map/ppermute | solution.py:31
  27.7 36.0 %copy-start.8 = (s32[1,256]{1,0:T(1,128)}, s32[1,256]{1,0:T(1,128)S(1)}, u32[]{:S(2)}) copy-start(s32[1,256]{1,0:T(1,128)S(1)} %compare_select_fusion.3.refs_1_) | copy-start | bytes 3076
  30.7 14.0 %copy-start.9 = (s32[1,256]{1,0:T(1,128)S(1)}, s32[1,256]{1,0:T(1,128)}, u32[]{:S(2)}) copy-start(s32[1,256]{1,0:T(1,128)} %compare_select_fusion) | copy-start | bytes 3076
  31.7 38.2 %copy-start.1 = (bf16[64,4,2560]{2,0,1:T(8,128)(2,1)}, bf16[64,4,2560]{2,0,1:T(8,128)(2,1)S(1)}, u32[]{:S(2)}) copy-start(bf16[64,4,2560]{2,0,1:T(8,128)(2,1)S(1)} %all-to-all-done) | copy-start | bytes 3932164
  31.7 12.9 %copy-start.10 = (s32[1,256]{1,0:T(1,128)S(1)}, s32[1,256]{1,0:T(1,128)}, u32[]{:S(2)}) copy-start(s32[1,256]{1,0:T(1,128)} %compare_select_fusion.1) | copy-start | bytes 3076
  31.7 13.0 %copy-start.11 = (s32[1,256]{1,0:T(1,128)S(1)}, s32[1,256]{1,0:T(1,128)}, u32[]{:S(2)}) copy-start(s32[1,256]{1,0:T(1,128)} %compare_select_fusion.2) | copy-start | bytes 3076
  31.8 13.6 %collective-permute-start.3 = (bf16[256,512]{1,0:T(8,128)(2,1)S(1)}, bf16[256,512]{1,0:T(8,128)(2,1)S(1)}, u32[]{:S(2)}, u32[]{:S(2)}) collective-permute-start(bf16[256,512]{1,0:T(8,128)(2,1)S(1)} %slice.21), channel_id=1, source_target_pairs={{0,4},{4,8},{8,12},{12,16},{16,20},{20,24},{24,28},{1,5},{5,9},{9,... | collective-permute-start | bytes 786440 | tf_op jit(solution)/shard_map/ppermute | solution.py:31
  42.7 54.7 %collective-permute-start.2 = (f32[16,128,128]{2,1,0:T(8,128)S(1)}, f32[16,128,128]{2,1,0:T(8,128)S(1)}, u32[]{:S(2)}, u32[]{:S(2)}) collective-permute-start(f32[16,128,128]{2,1,0:T(8,128)S(1)} %multiply_add_fusion), channel_id=1, source_target_pairs={{0,4},{4,8},{8,12},{12,16},{16,20},{20,24},{24,28},{1,5},{5,9},{9,... | collective-permute-start | bytes 3145736 | tf_op jit(solution)/shard_map/ppermute | solution.py:31
  45.4 6.3 %copy-start.12 = (bf16[256,512]{1,0:T(8,128)(2,1)}, bf16[256,512]{1,0:T(8,128)(2,1)S(1)}, u32[]{:S(2)}) copy-start(bf16[256,512]{1,0:T(8,128)(2,1)S(1)} %collective-permute-done.3.refs_4_.refs_8_) | copy-start | bytes 786436
  45.4 16.4 %collective-permute-start.4 = (bf16[256,512]{1,0:T(8,128)(2,1)S(1)}, bf16[256,512]{1,0:T(8,128)(2,1)}, u32[]{:S(2)}, u32[]{:S(2)}) collective-permute-start(bf16[256,512]{1,0:T(8,128)(2,1)S(1)} %collective-permute-done.3.refs_4_.refs_8_), channel_id=1, source_target_pairs={{0,4},{4,8},{8,12},{12,16},{16,20},{20,24},{24,28},{1,5},{5,9},{9,... | collective-permute-start | bytes 786440 | tf_op jit(solution)/shard_map/ppermute | solution.py:31
  51.7 18.2 %copy-start.5 = (pred[1,256,256]{2,1,0:T(8,128)(4,1)S(1)}, pred[1,256,256]{2,1,0:T(8,128)(4,1)}, u32[]{:S(2)}) copy-start(pred[1,256,256]{2,1,0:T(8,128)(4,1)} %iota_compare_fusion) | copy-start | bytes 196612
  61.8 9.4 %collective-permute-start.5 = (bf16[256,512]{1,0:T(8,128)(2,1)}, bf16[256,512]{1,0:T(8,128)(2,1)}, u32[]{:S(2)}, u32[]{:S(2)}) collective-permute-start(bf16[256,512]{1,0:T(8,128)(2,1)} %collective-permute-done.4.refs_5_.refs_9_), channel_id=1, source_target_pairs={{0,4},{4,8},{8,12},{12,16},{16,20},{20,24},{24,28},{1,5},{5,9},{9,... | collective-permute-start | bytes 786440 | tf_op jit(solution)/shard_map/ppermute | solution.py:31
  97.5 1.0 copy-start.4

commit v2 on v1

v2 whole, which is shorter than its diff:
```python
import math

import jax
import jax.numpy as jnp
import numpy as np
from jax import lax
from jax.experimental import pallas as pl
from jax.experimental.pallas import tpu as pltpu
from jax.sharding import PartitionSpec as P

HEADS = 64
HD = 128
KV_HEADS = 8
SPAN = 3

F32 = jnp.float32
BF16 = jnp.bfloat16


def document_index(doc_lengths, positions):
    doc_ends = jnp.cumsum(doc_lengths)
    counted = jnp.sum((positions[:, None] >= doc_ends[None, :]).astype(jnp.int32), axis=1)
    return jnp.where(positions < 0, -1, counted).astype(jnp.int32)


def from_behind(value, axis, steps):
    count = lax.axis_size(axis)
    pairs = [(source, source + steps) for source in range(0, count - steps)]
    if not pairs:
        return jnp.zeros_like(value)
    return lax.ppermute(value, axis, pairs)


def split_bf16(x):
    hi = x.astype(BF16)
    lo = (x - hi.astype(F32)).astype(BF16)
    return hi, lo


def dot_nt(a, b):
    return lax.dot_general(a, b, (((1,), (1,)), ((), ())), preferred_element_type=F32)


def head_cols(j):
    return slice(j * HD, (j + 1) * HD)


def doc_ends(len_ref, ndocs):
    ends = []
    total = jnp.int32(0)
    for i in range(ndocs):
        total = total + len_ref[i]
        ends.append(total)
    return ends


def doc_of(ends, pos):
    counted = jnp.zeros_like(pos)
    for e in ends:
        counted = counted + (pos >= e).astype(jnp.int32)
    return jnp.where(pos < 0, -1, counted)


def tail_kernel(hpb, ndocs, len_ref, start_ref, k_ref, v_ref, t_ref):
    rows = k_ref.shape[0]
    ends = doc_ends(len_ref, ndocs)
    start = start_ref[0]
    pos = start + lax.broadcasted_iota(jnp.int32, (rows, 1), 0)
    last = doc_of(ends, start + rows - 1)
    mask = (doc_of(ends, pos) == last).astype(BF16)
    for j in range(hpb):
        masked = v_ref[:, head_cols(j)] * mask
        t_ref[j] = lax.dot_general(
            k_ref[:, head_cols(j)], masked, (((0,), (0,)), ((), ())), preferred_element_type=F32
        )


def lin_local_kernel(hpb, ndocs, len_ref, start_ref, q_ref, k_ref, v_ref, lin_ref):
    rows = q_ref.shape[0]
    ends = doc_ends(len_ref, ndocs)
    start = start_ref[0]
    qpos = start + lax.broadcasted_iota(jnp.int32, (rows, 1), 0)
    kpos = start + lax.broadcasted_iota(jnp.int32, (1, rows), 1)
    visible = (doc_of(ends, qpos) == doc_of(ends, kpos)) & (kpos <= qpos)
    for j in range(hpb):
        scores = dot_nt(q_ref[:, head_cols(j)], k_ref[:, head_cols(j)])
        scores = jnp.where(visible, scores, 0.0)
        hi, lo = split_bf16(scores)
        v = v_ref[:, head_cols(j)]
        lin_ref[:, head_cols(j)] = jnp.dot(hi, v, preferred_element_type=F32) + jnp.dot(
            lo, v, preferred_element_type=F32
        )


def lin_finish_kernel(hpb, ndocs, len_ref, start_ref, q_ref, c_ref, lin_ref, g_ref, o_ref):
    rows = q_ref.shape[0]
    ends = doc_ends(len_ref, ndocs)
    start = start_ref[0]
    pos = start + lax.broadcasted_iota(jnp.int32, (rows, 1), 0)
    sees = (doc_of(ends, pos) == doc_of(ends, start - 1)).astype(F32)
    for j in range(hpb):
        hi, lo = split_bf16(c_ref[j])
        q = q_ref[:, head_cols(j)]
        carried = jnp.dot(q, hi, preferred_element_type=F32) + jnp.dot(
            q, lo, preferred_element_type=F32
        )
        lin = lin_ref[:, head_cols(j)] + carried * sees
        mean_sq = jnp.mean(lin * lin, axis=-1, keepdims=True)
        normed = lin * lax.rsqrt(mean_sq + 1e-06) * g_ref[:, head_cols(j)]
        o_ref[:, head_cols(j)] = normed.astype(o_ref.dtype)


def col_spec(rows, width=HD):
    return pl.BlockSpec((rows, width), lambda h: (0, h))


def full_spec(shape):
    return pl.BlockSpec(shape, lambda h: (0,) * len(shape))


def params():
    return pltpu.CompilerParams(dimension_semantics=("arbitrary",))


def soft_kernel(blocks, hpb, ndocs, len_ref, start_ref, q_ref, *rest):
    key_refs = rest[0:blocks]
    value_refs = rest[blocks : 2 * blocks]
    o_ref = rest[2 * blocks]
    s_ref, mx_ref, tot_ref, acc_ref = rest[2 * blocks + 1 :]
    rows = q_ref.shape[0]
    scale = 1.0 / math.sqrt(HD)
    ends = doc_ends(len_ref, ndocs)
    start = start_ref[0]
    qpos = start + lax.broadcasted_iota(jnp.int32, (rows, 1), 0)
    kpos = start + lax.broadcasted_iota(jnp.int32, (1, rows), 1)
    dq = doc_of(ends, qpos)
    first_doc = doc_of(ends, start)
    q = jnp.concatenate([q_ref[:, head_cols(j)] for j in range(hpb)], axis=0)

    def block_scores(m):
        shifted = kpos - m * rows
        visible = dq == doc_of(ends, shifted)
        if m == 0:
            visible = visible & (shifted <= qpos)
        s = dot_nt(q, key_refs[m][...]).reshape(hpb, rows, rows) * scale
        return jnp.where(visible[None], s, -1e30)

    def needed(m):
        return doc_of(ends, start - (m - 1) * rows - 1) == first_doc

    s0 = block_scores(0)
    s_ref[0] = s0
    mx_ref[...] = jnp.max(s0, axis=-1, keepdims=True)
    for m in range(1, blocks):

        @pl.when(needed(m))
        def _():
            s = block_scores(m)
            s_ref[m] = s
            mx_ref[...] = jnp.maximum(mx_ref[...], jnp.max(s, axis=-1, keepdims=True))

    def weighted(m):
        w = jnp.exp(s_ref[m] - mx_ref[...])
        part = jnp.sum(w, axis=-1, keepdims=True)
        term = jnp.dot(
            w.reshape(hpb * rows, rows).astype(BF16),
            value_refs[m][...],
            preferred_element_type=F32,
        ).reshape(hpb, rows, HD)
        return part, term

    part, term = weighted(0)
    tot_ref[...] = part
    acc_ref[...] = term
    for m in range(1, blocks):

        @pl.when(needed(m))
        def _():
            part, term = weighted(m)
            tot_ref[...] += part
            acc_ref[...] += term

    out = acc_ref[...] / tot_ref[...]
    for j in range(hpb):
        o_ref[:, head_cols(j)] = out[j].astype(o_ref.dtype)


def smem_spec():
    return pl.BlockSpec(memory_space=pltpu.SMEM)


def body(lin_query, lin_key, lin_value, norm_gain, soft_query, soft_key, soft_value, doc_lengths):
    rows, width = lin_query.shape
    local_heads = width // HD
    ndocs = doc_lengths.shape[0]
    lengths = doc_lengths.astype(jnp.int32)
    shard_start = (lax.axis_index("ctx") * rows).astype(jnp.int32).reshape(1)
    ends = jnp.cumsum(lengths)

    def doc_at(pos):
        return jnp.where(pos < 0, -1, jnp.sum((pos >= ends).astype(jnp.int32)))

    through_own = (doc_at(shard_start[0] - 1) == doc_at(shard_start[0] + rows - 1)).astype(F32)

    head_devices = lax.axis_size("head")
    group_size = HEADS // KV_HEADS
    per_device = HEADS // head_devices
    kv_local = max(1, per_device // group_size)
    kv_table = (
        np.arange(head_devices)[:, None] * per_device // group_size + np.arange(kv_local)[None, :]
    ).reshape(-1)
    short_rows = soft_key.shape[0]

    def spread(field):
        if np.array_equal(kv_table, np.arange(KV_HEADS)):
            return field.reshape(short_rows, head_devices, kv_local * HD)
        taken = jnp.take(field.reshape(short_rows, KV_HEADS, HD), kv_table, axis=1)
        return taken.reshape(short_rows, head_devices, kv_local * HD)

    packed = jnp.concatenate(
        [
            soft_query.reshape(short_rows, head_devices, per_device * HD),
            spread(soft_key),
            spread(soft_value),
        ],
        axis=2,
    )
    per_dest = packed.shape[2]
    packed = packed.reshape(short_rows, head_devices * per_dest)
    mixed = lax.all_to_all(packed, "head", split_axis=1, concat_axis=0, tiled=True)
    own_kv = mixed[:, per_device * HD :]
    older = []
    moving = own_kv
    for _ in range(SPAN):
        moving = from_behind(moving, "ctx", 1)
        older.append(moving)

    lhpb = min(local_heads, group_size)
    lsteps = local_heads // lhpb
    lwide = lhpb * HD
    tail = pl.pallas_call(
        lambda *refs: tail_kernel(lhpb, ndocs, *refs),
        out_shape=jax.ShapeDtypeStruct((local_heads, HD, HD), F32),
        grid=(lsteps,),
        in_specs=[smem_spec(), smem_spec(), col_spec(rows, lwide), col_spec(rows, lwide)],
        out_specs=pl.BlockSpec((lhpb, HD, HD), lambda h: (h, 0, 0)),
        compiler_params=params(),
        cost_estimate=pl.CostEstimate(
            flops=2 * rows * HD * HD * local_heads,
            transcendentals=0,
            bytes_accessed=2 * rows * width * 2 + local_heads * HD * HD * 4,
        ),
    )(lengths, shard_start, lin_key, lin_value)
    received = from_behind(tail, "ctx", 1)

    lin_local = pl.pallas_call(
        lambda *refs: lin_local_kernel(lhpb, ndocs, *refs),
        out_shape=jax.ShapeDtypeStruct((rows, width), F32),
        grid=(lsteps,),
        in_specs=[
            smem_spec(),
            smem_spec(),
            col_spec(rows, lwide),
            col_spec(rows, lwide),
            col_spec(rows, lwide),
        ],
        out_specs=col_spec(rows, lwide),
        compiler_params=params(),
        cost_estimate=pl.CostEstimate(
            flops=6 * rows * rows * HD * local_heads,
            transcendentals=0,
            bytes_accessed=3 * rows * width * 2 + rows * width * 4,
        ),
    )(lengths, shard_start, lin_query, lin_key, lin_value)

    onward = tail + through_own * received
    lin_local, onward = lax.optimization_barrier((lin_local, onward))
    received = from_behind(onward, "ctx", 1)
    for _ in range(SPAN - 2):
        received = from_behind(tail + through_own * received, "ctx", 1)
    carried = received

    blocks = SPAN + 1
    shpb = min(per_device, group_size)
    ssteps = per_device // shpb
    kv_index = lambda i: (i * shpb * kv_local) // per_device
    own_k_spec = pl.BlockSpec((rows, HD), lambda i: (0, per_device + kv_index(i)))
    own_v_spec = pl.BlockSpec((rows, HD), lambda i: (0, per_device + kv_local + kv_index(i)))
    old_k_spec = pl.BlockSpec((rows, HD), lambda i: (0, kv_index(i)))
    old_v_spec = pl.BlockSpec((rows, HD), lambda i: (0, kv_local + kv_index(i)))
    attended = pl.pallas_call(
        lambda *refs: soft_kernel(blocks, shpb, ndocs, *refs),
        out_shape=jax.ShapeDtypeStruct((rows, per_device * HD), BF16),
        grid=(ssteps,),
        in_specs=[smem_spec(), smem_spec(), col_spec(rows, shpb * HD)]
        + [own_k_spec]
        + [old_k_spec] * SPAN
        + [own_v_spec]
        + [old_v_spec] * SPAN,
        out_specs=col_spec(rows, shpb * HD),
        scratch_shapes=[
            pltpu.VMEM((blocks, shpb, rows, rows), F32),
            pltpu.VMEM((shpb, rows, 1), F32),
            pltpu.VMEM((shpb, rows, 1), F32),
            pltpu.VMEM((shpb, rows, HD), F32),
        ],
        compiler_params=pltpu.CompilerParams(
            dimension_semantics=("arbitrary",), vmem_limit_bytes=48 * 1024 * 1024
        ),
        cost_estimate=pl.CostEstimate(
            flops=4 * rows * rows * blocks * HD * per_device,
            transcendentals=rows * rows * blocks * per_device,
            bytes_accessed=rows * per_device * HD * 4 + 2 * blocks * rows * HD * 2 * per_device,
        ),
    )(lengths, shard_start, mixed, mixed, *older, mixed, *older)

    lightning_out = pl.pallas_call(
        lambda *refs: lin_finish_kernel(lhpb, ndocs, *refs),
        out_shape=jax.ShapeDtypeStruct((rows, width), BF16),
        grid=(lsteps,),
        in_specs=[
            smem_spec(),
            smem_spec(),
            col_spec(rows, lwide),
            pl.BlockSpec((lhpb, HD, HD), lambda h: (h, 0, 0)),
            col_spec(rows, lwide),
            pl.BlockSpec((1, lwide), lambda h: (0, h)),
        ],
        out_specs=col_spec(rows, lwide),
        compiler_params=params(),
        cost_estimate=pl.CostEstimate(
            flops=4 * rows * HD * HD * local_heads,
            transcendentals=rows * local_heads,
            bytes_accessed=rows * width * (2 + 4 + 2) + local_heads * HD * HD * 4,
        ),
    )(lengths, shard_start, lin_query, carried, lin_local, norm_gain.reshape(1, width))
    return (lightning_out, attended)


def solution(mesh):
    placed = (
        P("ctx", "head"),
        P("ctx", "head"),
        P("ctx", "head"),
        P("head"),
        P(("ctx", "head"), None),
        P(("ctx", "head"), None),
        P(("ctx", "head"), None),
        P(),
    )
    return jax.shard_map(
        body,
        mesh=mesh,
        in_specs=placed,
        out_specs=(P("ctx", "head"), P("ctx", "head")),
        check_vma=False,
    )
```

time: 104 us -> 87.7 us (0.84)
  Pallas kernels: 39.1 us -> 22.2 us
  waiting for transfers between devices: 26.3 us -> 41.3 us
  other arithmetic: 14.6 us -> 3.53 us
  starting transfers between devices: 17.6 us -> 15.8 us
  local copies, waits for them, and re-layouts: 2.43 us -> 1.12 us
    pallas_call x4, Pallas kernels: 39.1 us -> 22.2 us  [the longest x1 9.69 us: body(): pl.pallas_call(lambda *refs: soft_kernel(blocks, shpb, ndocs, *refs), out...]
    ppermute x6, waiting for transfers between devices: 25.3 us -> 36.5 us  [from_behind(): return lax.ppermute(value, axis, pairs)]
    select_n x7 -> x0, other arithmetic: 4.29 us -> none  [the longest x6 3.08 us: document_index(): return jnp.where(positions < 0, -1, counted).astype(jnp.int32)]
    convert_element_type x3 -> x0, other arithmetic: 3.95 us -> none  [the longest x1 1.38 us: body(): need = (key_docs[:, rows - 1] == own_docs[0]).astype(jnp.int32)]
    all_to_all x1, waiting for transfers between devices: 1.04 us -> 4.81 us  [body(): lax.all_to_all(packed, 'head', split_axis=1, concat_axis=0, tiled=True)]
    ppermute x6, starting transfers between devices: 13.9 us -> 12.1 us  [from_behind(): return lax.ppermute(value, axis, pairs)]
    add x2 -> x1, other arithmetic: 2.68 us -> 1.34 us  [body(): received = from_behind(tail + through_own * received, 'ctx', 1)]
    slice x2 -> x0, local copies, waits for them, and re-layouts: 1.18 us -> none  [the longest x1 0.6 us: body(): edges[0]]
  transfers between devices with their start and end apart: 7 -> 7, of which waited for: 4 -> 6; matrix products, arithmetic and copies ran while one was open for 12% -> 4% of each run, Pallas kernels for 32% -> 18%
where the time goes in v2:
time: 87.7 us; the launch traced here: 86.1 us
  waiting for transfers between devices  41.3 us (47%)
  Pallas kernels  22.2 us (25%)
  starting transfers between devices  15.8 us (18%)
  other arithmetic  3.53 us (4%)
  between operations  2.11 us (2%)
  local copies, waits for them, and re-layouts  1.12 us (1%)
    ppermute x6, waiting for transfers between devices, from_behind(): return lax.ppermute(value, axis, pairs)  36.5 us
    ppermute x6, starting transfers between devices, from_behind(): return lax.ppermute(value, axis, pairs)  12.1 us
    pallas_call x1, Pallas kernels, body(): pl.pallas_call(lambda *refs: soft_kernel(blocks, shpb, ndocs, *refs), out...  9.69 us
    pallas_call x1, Pallas kernels, body(): pl.pallas_call(lambda *refs: lin_local_kernel(lhpb, ndocs, *refs), out_sh...  6.12 us
    all_to_all x1, waiting for transfers between devices, body(): lax.all_to_all(packed, 'head', split_axis=1, concat_axis=0, tiled=True)  4.81 us
    all_to_all x1, starting transfers between devices, body(): lax.all_to_all(packed, 'head', split_axis=1, concat_axis=0, tiled=True)  3.71 us
    pallas_call x1, Pallas kernels, body(): pl.pallas_call(lambda *refs: lin_finish_kernel(lhpb, ndocs, *refs), out_s...  3.58 us
    pallas_call x1, Pallas kernels, body(): pl.pallas_call(lambda *refs: tail_kernel(lhpb, ndocs, *refs), out_shape=j...  2.86 us
  transfers between devices with their start and end apart: 7, of which 6 were waited for; matrix products, arithmetic and copies ran while one was open for 4% of the time, Pallas kernels for 18%

profile of v2, /device:TPU:8, one launch (start us, length us, event | category | flops | bytes accessed | tf_op | source)
XLA Modules:
  0.0 86.1 jit_solution(1785394029432056036)
XLA Ops:
  0.6 2.9 %shard_map.95 = f32[16,128,128]{2,1,0:T(8,128)} custom-call(s32[4]{0:T(128)} %refs_0_.7, s32[1]{0:T(128)} %bitcast.refs_1_, bf16[256,2048]{1,0:T(8,128)(2,1)} %refs_3_.3, bf16[256,2048]{1,0:T(8,128)(2,1)} %refs_4_.1), custom_call_target="tpu_custom_call" | custom-call | flops 134217728 | bytes 3145728 | tf_op jit(solution)/shard_map/pallas_call | solution.py:241
  3.5 1.9 %collective-permute-start = (f32[16,128,128]{2,1,0:T(8,128)}, f32[16,128,128]{2,1,0:T(8,128)S(1)}, u32[]{:S(2)}, u32[]{:S(2)}) collective-permute-start(f32[16,128,128]{2,1,0:T(8,128)} %shard_map.95), channel_id=1, source_target_pairs={{0,4},{4,8},{8,12},{12,16},{16,20},{20,24},{24,28},{1,5},{5,9},{9,... | collective-permute-start | bytes 3145736 | tf_op jit(solution)/shard_map/ppermute | solution.py:31
  5.4 0.2 reduce-window.9
  5.6 0.7 fusion.1
  7.7 6.1 %shard_map.96.refs_4_ = f32[256,2048]{1,0:T(8,128)} custom-call(s32[4]{0:T(128)} %refs_0_.7, s32[1]{0:T(128)} %bitcast.refs_1_, bf16[256,2048]{1,0:T(8,128)(2,1)} %refs_2_.5, bf16[256,2048]{1,0:T(8,128)(2,1)} %refs_3_.3, bf16[256,2048]{1,0:T(8,128)(2,1)} %refs_4_.1), custom_call_target="tpu_custom_call" | custom-call | flops 805306368 | bytes 5242880 | tf_op jit(solution)/shard_map/pallas_call | solution.py:256
  13.8 6.0 %collective-permute-done = f32[16,128,128]{2,1,0:T(8,128)S(1)} collective-permute-done((f32[16,128,128]{2,1,0:T(8,128)}, f32[16,128,128]{2,1,0:T(8,128)S(1)}, u32[]{:S(2)}, u32[]{:S(2)}) %collective-permute-start) | collective-permute-done | bytes 1048608 | tf_op jit(solution)/shard_map/ppermute | solution.py:31
  19.8 0.1 multiply_add_fusion.1
  20.0 1.9 %collective-permute-start.1 = (f32[16,128,128]{2,1,0:T(8,128)S(1)}, f32[16,128,128]{2,1,0:T(8,128)}, u32[]{:S(2)}, u32[]{:S(2)}) collective-permute-start(f32[16,128,128]{2,1,0:T(8,128)S(1)} %multiply_add_fusion.1), channel_id=1, source_target_pairs={{0,4},{4,8},{8,12},{12,16},{16,20},{20,24},{24,28},{1,5},{5,9},{9,... | collective-permute-start | bytes 3145736 | tf_op jit(solution)/shard_map/ppermute | solution.py:31
  22.0 0.1 copy.19
  22.0 1.2 %pad_maximum_fusion = bf16[64,4,2560]{2,0,1:T(8,128)(2,1)} fusion(bf16[64,4,256]{2,0,1:T(8,128)(2,1)S(1)} %get-tuple-element.8, bf16[64,4,256]{2,0,1:T(8,128)(2,1)S(1)} %get-tuple-element.9, bf16[64,4,2048]{2,0,1:T(8,128)(2,1)S(1)} %bitcast.21), kind=kLoop, calls=%fused_computation | loop fusion | flops 3932160 | bytes 2621440 | tf_op jit(solution)/shard_map/concatenate | solution.py:220
  23.2 3.7 %all-to-all-start = ((bf16[64,4,2560]{2,0,1:T(8,128)(2,1)}), bf16[64,4,2560]{2,0,1:T(8,128)(2,1)S(1)}, u32[]{:S(2)}, u32[]{:S(2)}) async-start(bf16[64,4,2560]{2,0,1:T(8,128)(2,1)} %pad_maximum_fusion), calls=%async_computation | async-start | bytes 2621440 | tf_op jit(solution)/shard_map/all_to_all | solution.py:230
  26.9 9.3 %collective-permute-done.1 = f32[16,128,128]{2,1,0:T(8,128)} collective-permute-done((f32[16,128,128]{2,1,0:T(8,128)S(1)}, f32[16,128,128]{2,1,0:T(8,128)}, u32[]{:S(2)}, u32[]{:S(2)}) %collective-permute-start.1) | collective-permute-done | bytes 1048608 | tf_op jit(solution)/shard_map/ppermute | solution.py:31
  36.2 1.3 %multiply_add_fusion = f32[16,128,128]{2,1,0:T(8,128)S(1)} fusion(f32[16,128,128]{2,1,0:T(8,128)S(1)} %copy-done.2, f32[16,128,128]{2,1,0:T(8,128)} %collective-permute-done.1, f32[]{:T(128)S(6)} %convert_element_type.13), kind=kLoop, calls=%fused_computation.2 | loop fusion | flops 524288 | bytes 3145732 | tf_op jit(solution)/shard_map/add | solution.py:280
  37.5 1.9 %collective-permute-start.2 = (f32[16,128,128]{2,1,0:T(8,128)S(1)}, f32[16,128,128]{2,1,0:T(8,128)S(1)}, u32[]{:S(2)}, u32[]{:S(2)}) collective-permute-start(f32[16,128,128]{2,1,0:T(8,128)S(1)} %multiply_add_fusion), channel_id=1, source_target_pairs={{0,4},{4,8},{8,12},{12,16},{16,20},{20,24},{24,28},{1,5},{5,9},{9,... | collective-permute-start | bytes 3145736 | tf_op jit(solution)/shard_map/ppermute | solution.py:31
  39.5 4.8 %all-to-all-done = bf16[64,4,2560]{2,0,1:T(8,128)(2,1)S(1)} async-done(((bf16[64,4,2560]{2,0,1:T(8,128)(2,1)}), bf16[64,4,2560]{2,0,1:T(8,128)(2,1)S(1)}, u32[]{:S(2)}, u32[]{:S(2)}) %all-to-all-start) | async-done | bytes 1310752 | tf_op jit(solution)/shard_map/all_to_all | solution.py:230
  44.3 2.5 %collective-permute-start.3 = (bf16[256,512]{1,0:T(8,128)(2,1)S(1)}, bf16[256,512]{1,0:T(8,128)(2,1)S(1)}, u32[]{:S(2)}, u32[]{:S(2)}) collective-permute-start(bf16[256,512]{1,0:T(8,128)(2,1)S(1)} %slice.4), channel_id=1, source_target_pairs={{0,4},{4,8},{8,12},{12,16},{16,20},{20,24},{24,28},{1,5},{5,9},{9,... | collective-permute-start | bytes 786440 | tf_op jit(solution)/shard_map/ppermute | solution.py:31
  46.8 9.6 %collective-permute-done.3.refs_4_.refs_8_ = bf16[256,512]{1,0:T(8,128)(2,1)S(1)} collective-permute-done((bf16[256,512]{1,0:T(8,128)(2,1)S(1)}, bf16[256,512]{1,0:T(8,128)(2,1)S(1)}, u32[]{:S(2)}, u32[]{:S(2)}) %collective-permute-start.3) | collective-permute-done | bytes 262176 | tf_op jit(solution)/shard_map/ppermute | solution.py:31
  56.5 1.9 %collective-permute-start.4 = (bf16[256,512]{1,0:T(8,128)(2,1)S(1)}, bf16[256,512]{1,0:T(8,128)(2,1)S(1)}, u32[]{:S(2)}, u32[]{:S(2)}) collective-permute-start(bf16[256,512]{1,0:T(8,128)(2,1)S(1)} %collective-permute-done.3.refs_4_.refs_8_), channel_id=1, source_target_pairs={{0,4},{4,8},{8,12},{12,16},{16,20},{20,24},{24,28},{1,5},{5,9},{9,... | collective-permute-start | bytes 786440 | tf_op jit(solution)/shard_map/ppermute | solution.py:31
  58.4 5.8 %collective-permute-done.4.refs_5_.refs_9_ = bf16[256,512]{1,0:T(8,128)(2,1)S(1)} collective-permute-done((bf16[256,512]{1,0:T(8,128)(2,1)S(1)}, bf16[256,512]{1,0:T(8,128)(2,1)S(1)}, u32[]{:S(2)}, u32[]{:S(2)}) %collective-permute-start.4) | collective-permute-done | bytes 262176 | tf_op jit(solution)/shard_map/ppermute | solution.py:31
  64.1 1.9 %collective-permute-start.5 = (bf16[256,512]{1,0:T(8,128)(2,1)S(1)}, bf16[256,512]{1,0:T(8,128)(2,1)S(1)}, u32[]{:S(2)}, u32[]{:S(2)}) collective-permute-start(bf16[256,512]{1,0:T(8,128)(2,1)S(1)} %collective-permute-done.4.refs_5_.refs_9_), channel_id=1, source_target_pairs={{0,4},{4,8},{8,12},{12,16},{16,20},{20,24},{24,28},{1,5},{5,9},{9,... | collective-permute-start | bytes 786440 | tf_op jit(solution)/shard_map/ppermute | solution.py:31
  66.1 5.8 %collective-permute-done.5.refs_6_.refs_10_ = bf16[256,512]{1,0:T(8,128)(2,1)S(1)} collective-permute-done((bf16[256,512]{1,0:T(8,128)(2,1)S(1)}, bf16[256,512]{1,0:T(8,128)(2,1)S(1)}, u32[]{:S(2)}, u32[]{:S(2)}) %collective-permute-start.5) | collective-permute-done | bytes 262176 | tf_op jit(solution)/shard_map/ppermute | solution.py:31
  71.8 9.7 %shard_map.98 = bf16[256,2048]{1,0:T(8,128)(2,1)} custom-call(s32[4]{0:T(128)S(1)} %copy-done.1, s32[1]{0:T(128)} %bitcast.refs_1_, bf16[256,2560]{1,0:T(8,128)(2,1)S(1)} %bitcast.17, bf16[256,2560]{1,0:T(8,128)(2,1)S(1)} %bitcast.18, bf16[256,512]{1,0:T(8,128)(2,1)S(1)} %collective-permute-done.3.refs_4_.refs_8_, ...), custom_call_target="tpu_custom_call" | custom-call | flops 2147483648 | bytes 10485760 | tf_op jit(solution)/shard_map/pallas_call | solution.py:291
  81.5 1.0 %copy-done.4 = f32[16,128,128]{2,1,0:T(8,128)} copy-done((f32[16,128,128]{2,1,0:T(8,128)}, f32[16,128,128]{2,1,0:T(8,128)S(1)}, u32[]{:S(2)}) %copy-start.4) | copy-done | bytes 1048600
  82.5 3.6 %shard_map.97 = bf16[256,2048]{1,0:T(8,128)(2,1)} custom-call(s32[4]{0:T(128)} %refs_0_.7, s32[1]{0:T(128)} %bitcast.refs_1_, bf16[256,2048]{1,0:T(8,128)(2,1)} %refs_2_.5, f32[16,128,128]{2,1,0:T(8,128)} %copy-done.4, f32[256,2048]{1,0:T(8,128)} %shard_map.96.refs_4_, f32[1,2048]{1,0:T(1,128)} %bitcast.25), custom_call_target="tpu_custom_call" | custom-call | flops 268435456 | bytes 5242880 | tf_op jit(solution)/shard_map/pallas_call | solution.py:317
  (16 shorter events, 0.1 us)
Async XLA Ops:
  0.6 4.8 %copy-start = (s32[4]{0:T(128)S(1)}, s32[4]{0:T(128)}, u32[]{:S(2)}) copy-start(s32[4]{0:T(128)} %refs_0_.7) | copy-start | bytes 52
  3.5 16.3 %collective-permute-start = (f32[16,128,128]{2,1,0:T(8,128)}, f32[16,128,128]{2,1,0:T(8,128)S(1)}, u32[]{:S(2)}, u32[]{:S(2)}) collective-permute-start(f32[16,128,128]{2,1,0:T(8,128)} %shard_map.95), channel_id=1, source_target_pairs={{0,4},{4,8},{8,12},{12,16},{16,20},{20,24},{24,28},{1,5},{5,9},{9,... | collective-permute-start | bytes 3145736 | tf_op jit(solution)/shard_map/ppermute | solution.py:31
  7.7 12.2 %copy-start.2 = (f32[16,128,128]{2,1,0:T(8,128)S(1)}, f32[16,128,128]{2,1,0:T(8,128)}, u32[]{:S(2)}) copy-start(f32[16,128,128]{2,1,0:T(8,128)} %shard_map.95) | copy-start | bytes 3145732
  13.8 8.1 %copy-start.5 = (bf16[64,1024]{1,0:T(8,128)(2,1)S(1)}, bf16[64,1024]{1,0:T(8,128)(2,1)}, u32[]{:S(2)}) copy-start(bf16[64,1024]{1,0:T(8,128)(2,1)} %param.14) | copy-start | bytes 393220
  13.8 8.1 %copy-start.6 = (bf16[64,1024]{1,0:T(8,128)(2,1)S(1)}, bf16[64,1024]{1,0:T(8,128)(2,1)}, u32[]{:S(2)}) copy-start(bf16[64,1024]{1,0:T(8,128)(2,1)} %param.13) | copy-start | bytes 393220
  13.8 8.2 %copy-start.3 = (bf16[64,8192]{1,0:T(8,128)(2,1)S(1)}, bf16[64,8192]{1,0:T(8,128)(2,1)}, u32[]{:S(2)}) copy-start(bf16[64,8192]{1,0:T(8,128)(2,1)} %param.12) | copy-start | bytes 3145732
  20.0 16.2 %collective-permute-start.1 = (f32[16,128,128]{2,1,0:T(8,128)S(1)}, f32[16,128,128]{2,1,0:T(8,128)}, u32[]{:S(2)}, u32[]{:S(2)}) collective-permute-start(f32[16,128,128]{2,1,0:T(8,128)S(1)} %multiply_add_fusion.1), channel_id=1, source_target_pairs={{0,4},{4,8},{8,12},{12,16},{16,20},{20,24},{24,28},{1,5},{5,9},{9,... | collective-permute-start | bytes 3145736 | tf_op jit(solution)/shard_map/ppermute | solution.py:31
  23.2 21.1 %all-to-all-start = ((bf16[64,4,2560]{2,0,1:T(8,128)(2,1)}), bf16[64,4,2560]{2,0,1:T(8,128)(2,1)S(1)}, u32[]{:S(2)}, u32[]{:S(2)}) async-start(bf16[64,4,2560]{2,0,1:T(8,128)(2,1)} %pad_maximum_fusion), calls=%async_computation | async-start | bytes 2621440 | tf_op jit(solution)/shard_map/all_to_all | solution.py:230
  26.9 44.9 %copy-start.1 = (s32[4]{0:T(128)S(1)}, s32[4]{0:T(128)}, u32[]{:S(2)}) copy-start(s32[4]{0:T(128)} %refs_0_.7) | copy-start | bytes 52
  37.5 44.0 %collective-permute-start.2 = (f32[16,128,128]{2,1,0:T(8,128)S(1)}, f32[16,128,128]{2,1,0:T(8,128)S(1)}, u32[]{:S(2)}, u32[]{:S(2)}) collective-permute-start(f32[16,128,128]{2,1,0:T(8,128)S(1)} %multiply_add_fusion), channel_id=1, source_target_pairs={{0,4},{4,8},{8,12},{12,16},{16,20},{20,24},{24,28},{1,5},{5,9},{9,... | collective-permute-start | bytes 3145736 | tf_op jit(solution)/shard_map/ppermute | solution.py:31
  44.3 12.2 %collective-permute-start.3 = (bf16[256,512]{1,0:T(8,128)(2,1)S(1)}, bf16[256,512]{1,0:T(8,128)(2,1)S(1)}, u32[]{:S(2)}, u32[]{:S(2)}) collective-permute-start(bf16[256,512]{1,0:T(8,128)(2,1)S(1)} %slice.4), channel_id=1, source_target_pairs={{0,4},{4,8},{8,12},{12,16},{16,20},{20,24},{24,28},{1,5},{5,9},{9,... | collective-permute-start | bytes 786440 | tf_op jit(solution)/shard_map/ppermute | solution.py:31
  56.5 7.7 %collective-permute-start.4 = (bf16[256,512]{1,0:T(8,128)(2,1)S(1)}, bf16[256,512]{1,0:T(8,128)(2,1)S(1)}, u32[]{:S(2)}, u32[]{:S(2)}) collective-permute-start(bf16[256,512]{1,0:T(8,128)(2,1)S(1)} %collective-permute-done.3.refs_4_.refs_8_), channel_id=1, source_target_pairs={{0,4},{4,8},{8,12},{12,16},{16,20},{20,24},{24,28},{1,5},{5,9},{9,... | collective-permute-start | bytes 786440 | tf_op jit(solution)/shard_map/ppermute | solution.py:31
  64.1 7.7 %collective-permute-start.5 = (bf16[256,512]{1,0:T(8,128)(2,1)S(1)}, bf16[256,512]{1,0:T(8,128)(2,1)S(1)}, u32[]{:S(2)}, u32[]{:S(2)}) collective-permute-start(bf16[256,512]{1,0:T(8,128)(2,1)S(1)} %collective-permute-done.4.refs_5_.refs_9_), channel_id=1, source_target_pairs={{0,4},{4,8},{8,12},{12,16},{16,20},{20,24},{24,28},{1,5},{5,9},{9,... | collective-permute-start | bytes 786440 | tf_op jit(solution)/shard_map/ppermute | solution.py:31
  81.5 1.0 %copy-start.4 = (f32[16,128,128]{2,1,0:T(8,128)}, f32[16,128,128]{2,1,0:T(8,128)S(1)}, u32[]{:S(2)}) copy-start(f32[16,128,128]{2,1,0:T(8,128)S(1)} %collective-permute-done.2.refs_3_) | copy-start | bytes 3145732

commit v3 on v2

--- a/solution.py
+++ b/solution.py
@@ -92,14 +92,14 @@
         )
 
 
-def lin_finish_kernel(hpb, ndocs, len_ref, start_ref, q_ref, c_ref, lin_ref, g_ref, o_ref):
+def lin_finish_kernel(hpb, ndocs, len_ref, start_ref, q_ref, hi_ref, lo_ref, lin_ref, g_ref, o_ref):
     rows = q_ref.shape[0]
     ends = doc_ends(len_ref, ndocs)
     start = start_ref[0]
     pos = start + lax.broadcasted_iota(jnp.int32, (rows, 1), 0)
     sees = (doc_of(ends, pos) == doc_of(ends, start - 1)).astype(F32)
     for j in range(hpb):
-        hi, lo = split_bf16(c_ref[j])
+        hi, lo = split_bf16(hi_ref[j])
         q = q_ref[:, head_cols(j)]
         carried = jnp.dot(q, hi, preferred_element_type=F32) + jnp.dot(
             q, lo, preferred_element_type=F32
@@ -142,7 +142,7 @@
         visible = dq == doc_of(ends, shifted)
         if m == 0:
             visible = visible & (shifted <= qpos)
-        s = dot_nt(q, key_refs[m][...]).reshape(hpb, rows, rows) * scale
+        s = dot_nt(q, key_refs[m][...].reshape(rows, HD)).reshape(hpb, rows, rows) * scale
         return jnp.where(visible[None], s, -1e30)
 
     def needed(m):
@@ -164,7 +164,7 @@
         part = jnp.sum(w, axis=-1, keepdims=True)
         term = jnp.dot(
             w.reshape(hpb * rows, rows).astype(BF16),
-            value_refs[m][...],
+            value_refs[m][...].reshape(rows, HD),
             preferred_element_type=F32,
         ).reshape(hpb, rows, HD)
         return part, term
@@ -217,23 +217,18 @@
         taken = jnp.take(field.reshape(short_rows, KV_HEADS, HD), kv_table, axis=1)
         return taken.reshape(short_rows, head_devices, kv_local * HD)
 
-    packed = jnp.concatenate(
-        [
-            soft_query.reshape(short_rows, head_devices, per_device * HD),
-            spread(soft_key),
-            spread(soft_value),
-        ],
-        axis=2,
-    )
+    raw = jnp.concatenate([soft_key, soft_value], axis=1)
+    shards = [raw]
+    for _ in range(SPAN):
+        shards.append(from_behind(shards[-1], "ctx", 1))
+    pieces = [soft_query.reshape(short_rows, head_devices, per_device * HD)]
+    for shard in shards:
+        pieces.append(spread(shard[:, : KV_HEADS * HD]))
+        pieces.append(spread(shard[:, KV_HEADS * HD :]))
+    packed = jnp.concatenate(pieces, axis=2)
     per_dest = packed.shape[2]
     packed = packed.reshape(short_rows, head_devices * per_dest)
     mixed = lax.all_to_all(packed, "head", split_axis=1, concat_axis=0, tiled=True)
-    own_kv = mixed[:, per_device * HD :]
-    older = []
-    moving = own_kv
-    for _ in range(SPAN):
-        moving = from_behind(moving, "ctx", 1)
-        older.append(moving)
 
     lhpb = min(local_heads, group_size)
     lsteps = local_heads // lhpb
@@ -251,7 +246,6 @@
             bytes_accessed=2 * rows * width * 2 + local_heads * HD * HD * 4,
         ),
     )(lengths, shard_start, lin_key, lin_value)
-    received = from_behind(tail, "ctx", 1)
 
     lin_local = pl.pallas_call(
         lambda *refs: lin_local_kernel(lhpb, ndocs, *refs),
@@ -273,30 +267,29 @@
         ),
     )(lengths, shard_start, lin_query, lin_key, lin_value)
 
+    received = from_behind(tail, "ctx", 1)
     onward = tail + through_own * received
     lin_local, onward = lax.optimization_barrier((lin_local, onward))
     received = from_behind(onward, "ctx", 1)
     for _ in range(SPAN - 2):
         received = from_behind(tail + through_own * received, "ctx", 1)
-    carried = received
+    hi_state, lo_state = received, received
 
     blocks = SPAN + 1
     shpb = min(per_device, group_size)
     ssteps = per_device // shpb
     kv_index = lambda i: (i * shpb * kv_local) // per_device
-    own_k_spec = pl.BlockSpec((rows, HD), lambda i: (0, per_device + kv_index(i)))
-    own_v_spec = pl.BlockSpec((rows, HD), lambda i: (0, per_device + kv_local + kv_index(i)))
-    old_k_spec = pl.BlockSpec((rows, HD), lambda i: (0, kv_index(i)))
-    old_v_spec = pl.BlockSpec((rows, HD), lambda i: (0, kv_local + kv_index(i)))
+    def kv_spec(m, value):
+        base = per_device + 2 * kv_local * m + (kv_local if value else 0)
+        return pl.BlockSpec((rows, HD), lambda i: (0, base + kv_index(i)))
+
     attended = pl.pallas_call(
         lambda *refs: soft_kernel(blocks, shpb, ndocs, *refs),
         out_shape=jax.ShapeDtypeStruct((rows, per_device * HD), BF16),
         grid=(ssteps,),
         in_specs=[smem_spec(), smem_spec(), col_spec(rows, shpb * HD)]
-        + [own_k_spec]
-        + [old_k_spec] * SPAN
-        + [own_v_spec]
-        + [old_v_spec] * SPAN,
+        + [kv_spec(m, False) for m in range(blocks)]
+        + [kv_spec(m, True) for m in range(blocks)],
         out_specs=col_spec(rows, shpb * HD),
         scratch_shapes=[
             pltpu.VMEM((blocks, shpb, rows, rows), F32),
@@ -312,7 +305,7 @@
             transcendentals=rows * rows * blocks * per_device,
             bytes_accessed=rows * per_device * HD * 4 + 2 * blocks * rows * HD * 2 * per_device,
         ),
-    )(lengths, shard_start, mixed, mixed, *older, mixed, *older)
+    )(lengths, shard_start, mixed, *([mixed] * (2 * blocks)))
 
     lightning_out = pl.pallas_call(
         lambda *refs: lin_finish_kernel(lhpb, ndocs, *refs),
@@ -322,6 +315,7 @@
             smem_spec(),
             smem_spec(),
             col_spec(rows, lwide),
+            pl.BlockSpec((lhpb, HD, HD), lambda h: (h, 0, 0)),
             pl.BlockSpec((lhpb, HD, HD), lambda h: (h, 0, 0)),
             col_spec(rows, lwide),
             pl.BlockSpec((1, lwide), lambda h: (0, h)),
@@ -333,7 +327,7 @@
             transcendentals=rows * local_heads,
             bytes_accessed=rows * width * (2 + 4 + 2) + local_heads * HD * HD * 4,
         ),
-    )(lengths, shard_start, lin_query, carried, lin_local, norm_gain.reshape(1, width))
+    )(lengths, shard_start, lin_query, hi_state, lo_state, lin_local, norm_gain.reshape(1, width))
     return (lightning_out, attended)
 
 

time: 87.7 us -> 84.8 us (0.967)
  waiting for transfers between devices: 41.3 us -> 27.4 us
  local copies, waits for them, and re-layouts: 1.12 us -> 7.61 us
  starting transfers between devices: 15.8 us -> 18.6 us
  other arithmetic: 3.53 us -> 5.04 us
  Pallas kernels: 22.2 us -> 23.2 us
    ppermute x6, waiting for transfers between devices: 36.5 us -> 14.3 us  [from_behind(): return lax.ppermute(value, axis, pairs)]
    all_to_all x1, waiting for transfers between devices: 4.81 us -> 13.2 us  [body(): lax.all_to_all(packed, 'head', split_axis=1, concat_axis=0, tiled=True)]
    unnamed x14 -> x22, local copies, waits for them, and re-layouts: 1.01 us -> 6.9 us
    ppermute x6, starting transfers between devices: 12.1 us -> 14.9 us  [from_behind(): return lax.ppermute(value, axis, pairs)]
    add x1, other arithmetic: 1.34 us -> 2.35 us  [body(): received = from_behind(tail + through_own * received, 'ctx', 1)]
    add x1, other arithmetic: 0.14 us -> 1.09 us  [body(): onward = tail + through_own * received]
  transfers between devices with their start and end apart: 7 -> 7, of which waited for: 6 -> 4; matrix products, arithmetic and copies ran while one was open for 4% -> 14% of each run, Pallas kernels for 18% -> 19%
where the time goes in v3:
time: 84.8 us; the launch traced here: 84 us
  waiting for transfers between devices  27.4 us (32%)
  Pallas kernels  23.2 us (27%)
  starting transfers between devices  18.6 us (22%)
  local copies, waits for them, and re-layouts  7.61 us (9%)
  other arithmetic  5.04 us (6%)
  between operations  2.12 us (2%)
    ppermute x6, starting transfers between devices, from_behind(): return lax.ppermute(value, axis, pairs)  14.9 us
    ppermute x6, waiting for transfers between devices, from_behind(): return lax.ppermute(value, axis, pairs)  14.3 us
    all_to_all x1, waiting for transfers between devices, body(): lax.all_to_all(packed, 'head', split_axis=1, concat_axis=0, tiled=True)  13.2 us
    pallas_call x1, Pallas kernels, body(): pl.pallas_call(lambda *refs: soft_kernel(blocks, shpb, ndocs, *refs), out...  9.75 us
    unnamed x22, local copies, waits for them, and re-layouts  6.9 us
    pallas_call x1, Pallas kernels, body(): pl.pallas_call(lambda *refs: lin_local_kernel(lhpb, ndocs, *refs), out_sh...  6.05 us
    pallas_call x1, Pallas kernels, body(): pl.pallas_call(lambda *refs: lin_finish_kernel(lhpb, ndocs, *refs), out_s...  4.41 us
    all_to_all x1, starting transfers between devices, body(): lax.all_to_all(packed, 'head', split_axis=1, concat_axis=0, tiled=True)  3.71 us
  transfers between devices with their start and end apart: 7, of which 4 were waited for; matrix products, arithmetic and copies ran while one was open for 14% of the time, Pallas kernels for 19%

profile of v3, /device:TPU:8, one launch (start us, length us, event | category | flops | bytes accessed | tf_op | source)
XLA Modules:
  0.0 84.0 jit_solution(6227820482314368599)
XLA Ops:
  0.7 3.0 %shard_map.95 = f32[16,128,128]{2,1,0:T(8,128)} custom-call(s32[4]{0:T(128)} %refs_0_.7, s32[1]{0:T(128)} %bitcast.refs_1_, bf16[256,2048]{1,0:T(8,128)(2,1)} %refs_3_.3, bf16[256,2048]{1,0:T(8,128)(2,1)} %refs_4_.1), custom_call_target="tpu_custom_call" | custom-call | flops 134217728 | bytes 3145728 | tf_op jit(solution)/shard_map/pallas_call | solution.py:236
  3.6 2.0 %collective-permute-start = (f32[16,128,128]{2,1,0:T(8,128)}, f32[16,128,128]{2,1,0:T(8,128)S(1)}, u32[]{:S(2)}, u32[]{:S(2)}) collective-permute-start(f32[16,128,128]{2,1,0:T(8,128)} %shard_map.95), channel_id=1, source_target_pairs={{0,4},{4,8},{8,12},{12,16},{16,20},{20,24},{24,28},{1,5},{5,9},{9,... | collective-permute-start | bytes 3145736 | tf_op jit(solution)/shard_map/ppermute | solution.py:31
  5.7 0.7 pad_maximum_fusion
  6.4 3.6 %collective-permute-start.3 = (bf16[64,2048]{1,0:T(8,128)(2,1)}, bf16[64,2048]{1,0:T(8,128)(2,1)S(1)}, u32[]{:S(2)}, u32[]{:S(2)}) collective-permute-start(bf16[64,2048]{1,0:T(8,128)(2,1)} %pad_maximum_fusion), channel_id=1, source_target_pairs={{0,4},{4,8},{8,12},{12,16},{16,20},{20,24},{24,28},{1,5},{5,9},{9,... | collective-permute-start | bytes 786440 | tf_op jit(solution)/shard_map/ppermute | solution.py:31
  10.0 1.1 %bitcast_dynamic-update-slice_fusion = bf16[64,4,4096]{2,0,1:T(8,128)(2,1)} fusion(bf16[8,4,8,2048]{3,2,1,0:T(8,128)(2,1)S(1)} %bitcast.43), kind=kLoop, calls=%fused_computation | loop fusion | bytes 2097152
  12.0 0.7 fusion.1
  12.7 6.1 %shard_map.96.refs_5_ = f32[256,2048]{1,0:T(8,128)} custom-call(s32[4]{0:T(128)} %refs_0_.7, s32[1]{0:T(128)} %bitcast.refs_1_, bf16[256,2048]{1,0:T(8,128)(2,1)} %refs_2_.5, bf16[256,2048]{1,0:T(8,128)(2,1)} %refs_3_.3, bf16[256,2048]{1,0:T(8,128)(2,1)} %refs_4_.1), custom_call_target="tpu_custom_call" | custom-call | flops 805306368 | bytes 5242880 | tf_op jit(solution)/shard_map/pallas_call | solution.py:250
  20.1 0.7 bitcast_dynamic-update-slice_fusion.7
  20.8 2.1 %collective-permute-done.3 = bf16[64,2048]{1,0:T(8,128)(2,1)S(1)} collective-permute-done((bf16[64,2048]{1,0:T(8,128)(2,1)}, bf16[64,2048]{1,0:T(8,128)(2,1)S(1)}, u32[]{:S(2)}, u32[]{:S(2)}) %collective-permute-start.3) | collective-permute-done | bytes 262176 | tf_op jit(solution)/shard_map/ppermute | solution.py:31
  22.9 1.9 %collective-permute-start.4 = (bf16[64,2048]{1,0:T(8,128)(2,1)S(1)}, bf16[64,2048]{1,0:T(8,128)(2,1)S(1)}, u32[]{:S(2)}, u32[]{:S(2)}) collective-permute-start(bf16[64,2048]{1,0:T(8,128)(2,1)S(1)} %collective-permute-done.3), channel_id=1, source_target_pairs={{0,4},{4,8},{8,12},{12,16},{16,20},{20,24},{24,28},{1,5},{5,9},{9,... | collective-permute-start | bytes 786440 | tf_op jit(solution)/shard_map/ppermute | solution.py:31
  24.8 0.7 bitcast_dynamic-update-slice_fusion.6
  25.5 0.7 bitcast_dynamic-update-slice_fusion.5
  26.2 4.4 %collective-permute-done.4 = bf16[64,2048]{1,0:T(8,128)(2,1)S(1)} collective-permute-done((bf16[64,2048]{1,0:T(8,128)(2,1)S(1)}, bf16[64,2048]{1,0:T(8,128)(2,1)S(1)}, u32[]{:S(2)}, u32[]{:S(2)}) %collective-permute-start.4) | collective-permute-done | bytes 262176 | tf_op jit(solution)/shard_map/ppermute | solution.py:31
  30.6 1.9 %collective-permute-start.5 = (bf16[64,2048]{1,0:T(8,128)(2,1)S(1)}, bf16[64,2048]{1,0:T(8,128)(2,1)S(1)}, u32[]{:S(2)}, u32[]{:S(2)}) collective-permute-start(bf16[64,2048]{1,0:T(8,128)(2,1)S(1)} %collective-permute-done.4), channel_id=1, source_target_pairs={{0,4},{4,8},{8,12},{12,16},{16,20},{20,24},{24,28},{1,5},{5,9},{9,... | collective-permute-start | bytes 786440 | tf_op jit(solution)/shard_map/ppermute | solution.py:31
  33.9 1.1 %multiply_add_fusion.1 = f32[16,128,128]{2,1,0:T(8,128)} fusion(f32[16,128,128]{2,1,0:T(8,128)S(1)} %copy-done.2, f32[16,128,128]{2,1,0:T(8,128)S(1)} %collective-permute-done, f32[]{:T(128)S(6)} %convert_element_type.13), kind=kLoop, calls=%fused_computation.2 | loop fusion | flops 524288 | bytes 3145732 | tf_op jit(solution)/shard_map/add | solution.py:271
  35.0 3.6 %collective-permute-start.1 = (f32[16,128,128]{2,1,0:T(8,128)}, f32[16,128,128]{2,1,0:T(8,128)}, u32[]{:S(2)}, u32[]{:S(2)}) collective-permute-start(f32[16,128,128]{2,1,0:T(8,128)} %multiply_add_fusion.1), channel_id=1, source_target_pairs={{0,4},{4,8},{8,12},{12,16},{16,20},{20,24},{24,28},{1,5},{5,9},{9,... | collective-permute-start | bytes 3145736 | tf_op jit(solution)/shard_map/ppermute | solution.py:31
  39.9 3.7 %all-to-all-start = ((bf16[64,4,4096]{2,0,1:T(8,128)(2,1)}), bf16[64,4,4096]{2,0,1:T(8,128)(2,1)S(1)}, u32[]{:S(2)}, u32[]{:S(2)}) async-start(bf16[64,4,4096]{2,0,1:T(8,128)(2,1)} %bitcast_dynamic-update-slice_fusion.1), calls=%async_computation | async-start | bytes 4194304 | tf_op jit(solution)/shard_map/all_to_all | solution.py:231
  43.6 7.8 %collective-permute-done.1 = f32[16,128,128]{2,1,0:T(8,128)} collective-permute-done((f32[16,128,128]{2,1,0:T(8,128)}, f32[16,128,128]{2,1,0:T(8,128)}, u32[]{:S(2)}, u32[]{:S(2)}) %collective-permute-start.1) | collective-permute-done | bytes 1048608 | tf_op jit(solution)/shard_map/ppermute | solution.py:31
  51.4 2.4 %multiply_add_fusion = f32[16,128,128]{2,1,0:T(8,128)} fusion(f32[16,128,128]{2,1,0:T(8,128)S(1)} %copy-done.2, f32[16,128,128]{2,1,0:T(8,128)} %collective-permute-done.1, f32[]{:T(128)S(6)} %convert_element_type.13), kind=kLoop, calls=%fused_computation.1 | loop fusion | flops 524288 | bytes 3145732 | tf_op jit(solution)/shard_map/add | solution.py:275
  53.8 1.9 %collective-permute-start.2 = (f32[16,128,128]{2,1,0:T(8,128)}, f32[16,128,128]{2,1,0:T(8,128)S(1)}, u32[]{:S(2)}, u32[]{:S(2)}) collective-permute-start(f32[16,128,128]{2,1,0:T(8,128)} %multiply_add_fusion), channel_id=1, source_target_pairs={{0,4},{4,8},{8,12},{12,16},{16,20},{20,24},{24,28},{1,5},{5,9},{9,... | collective-permute-start | bytes 3145736 | tf_op jit(solution)/shard_map/ppermute | solution.py:31
  55.7 13.2 %all-to-all-done = bf16[64,4,4096]{2,0,1:T(8,128)(2,1)S(1)} async-done(((bf16[64,4,4096]{2,0,1:T(8,128)(2,1)}), bf16[64,4,4096]{2,0,1:T(8,128)(2,1)S(1)}, u32[]{:S(2)}, u32[]{:S(2)}) %all-to-all-start) | async-done | bytes 2097184 | tf_op jit(solution)/shard_map/all_to_all | solution.py:231
  68.8 9.7 %shard_map.98 = bf16[256,2048]{1,0:T(8,128)(2,1)} custom-call(s32[4]{0:T(128)S(1)} %copy-done.1, s32[1]{0:T(128)} %bitcast.refs_1_, bf16[256,4096]{1,0:T(8,128)(2,1)S(1)} %bitcast.33, bf16[256,4096]{1,0:T(8,128)(2,1)S(1)} %bitcast.34, bf16[256,4096]{1,0:T(8,128)(2,1)S(1)} %bitcast.35, bf16[256,4096]{1,0:T(8,128)(2,1)S(1)} %bitcast.36, ...), custom_call_target="tpu_custom_call" | custom-call | flops 2147483648 | bytes 10485760 | tf_op jit(solution)/shard_map/pallas_call | solution.py:286
  78.6 1.0 %copy-done.3 = f32[16,128,128]{2,1,0:T(8,128)} copy-done((f32[16,128,128]{2,1,0:T(8,128)}, f32[16,128,128]{2,1,0:T(8,128)S(1)}, u32[]{:S(2)}) %copy-start.3) | copy-done | bytes 1048600
  79.6 4.4 %shard_map.97 = bf16[256,2048]{1,0:T(8,128)(2,1)} custom-call(s32[4]{0:T(128)} %refs_0_.7, s32[1]{0:T(128)} %bitcast.refs_1_, bf16[256,2048]{1,0:T(8,128)(2,1)} %refs_2_.5, f32[16,128,128]{2,1,0:T(8,128)} %copy-done.3, f32[16,128,128]{2,1,0:T(8,128)} %copy-done.3, f32[256,2048]{1,0:T(8,128)} %shard_map.96.refs_5_, f32[1,2048]{1,0:T(1,128)} %bitcast.52), custom_call_target="tpu_custom_call" | custom-call | flops 268435456 | bytes 5242880 | tf_op jit(solution)/shard_map/pallas_call | solution.py:310
  (25 shorter events, 3.6 us)
Async XLA Ops:
  0.6 5.0 %copy-start.5 = (bf16[64,1024]{1,0:T(8,128)(2,1)S(1)}, bf16[64,1024]{1,0:T(8,128)(2,1)}, u32[]{:S(2)}) copy-start(bf16[64,1024]{1,0:T(8,128)(2,1)} %param.13) | copy-start | bytes 393220
  0.6 5.0 %copy-start.6 = (bf16[64,1024]{1,0:T(8,128)(2,1)S(1)}, bf16[64,1024]{1,0:T(8,128)(2,1)}, u32[]{:S(2)}) copy-start(bf16[64,1024]{1,0:T(8,128)(2,1)} %param.14) | copy-start | bytes 393220
  0.7 9.3 %copy-start.4 = (bf16[64,8192]{1,0:T(8,128)(2,1)S(1)}, bf16[64,8192]{1,0:T(8,128)(2,1)}, u32[]{:S(2)}) copy-start(bf16[64,8192]{1,0:T(8,128)(2,1)} %param.12) | copy-start | bytes 3145732
  3.6 7.5 %copy-start = (s32[4]{0:T(128)S(1)}, s32[4]{0:T(128)}, u32[]{:S(2)}) copy-start(s32[4]{0:T(128)} %refs_0_.7) | copy-start | bytes 52
  3.6 30.3 %collective-permute-start = (f32[16,128,128]{2,1,0:T(8,128)}, f32[16,128,128]{2,1,0:T(8,128)S(1)}, u32[]{:S(2)}, u32[]{:S(2)}) collective-permute-start(f32[16,128,128]{2,1,0:T(8,128)} %shard_map.95), channel_id=1, source_target_pairs={{0,4},{4,8},{8,12},{12,16},{16,20},{20,24},{24,28},{1,5},{5,9},{9,... | collective-permute-start | bytes 3145736 | tf_op jit(solution)/shard_map/ppermute | solution.py:31
  6.4 16.5 %collective-permute-start.3 = (bf16[64,2048]{1,0:T(8,128)(2,1)}, bf16[64,2048]{1,0:T(8,128)(2,1)S(1)}, u32[]{:S(2)}, u32[]{:S(2)}) collective-permute-start(bf16[64,2048]{1,0:T(8,128)(2,1)} %pad_maximum_fusion), channel_id=1, source_target_pairs={{0,4},{4,8},{8,12},{12,16},{16,20},{20,24},{24,28},{1,5},{5,9},{9,... | collective-permute-start | bytes 786440 | tf_op jit(solution)/shard_map/ppermute | solution.py:31
  18.7 15.2 %copy-start.2 = (f32[16,128,128]{2,1,0:T(8,128)S(1)}, f32[16,128,128]{2,1,0:T(8,128)}, u32[]{:S(2)}) copy-start(f32[16,128,128]{2,1,0:T(8,128)} %shard_map.95) | copy-start | bytes 3145732
  22.9 7.7 %collective-permute-start.4 = (bf16[64,2048]{1,0:T(8,128)(2,1)S(1)}, bf16[64,2048]{1,0:T(8,128)(2,1)S(1)}, u32[]{:S(2)}, u32[]{:S(2)}) collective-permute-start(bf16[64,2048]{1,0:T(8,128)(2,1)S(1)} %collective-permute-done.3), channel_id=1, source_target_pairs={{0,4},{4,8},{8,12},{12,16},{16,20},{20,24},{24,28},{1,5},{5,9},{9,... | collective-permute-start | bytes 786440 | tf_op jit(solution)/shard_map/ppermute | solution.py:31
  30.6 8.0 %collective-permute-start.5 = (bf16[64,2048]{1,0:T(8,128)(2,1)S(1)}, bf16[64,2048]{1,0:T(8,128)(2,1)S(1)}, u32[]{:S(2)}, u32[]{:S(2)}) collective-permute-start(bf16[64,2048]{1,0:T(8,128)(2,1)S(1)} %collective-permute-done.4), channel_id=1, source_target_pairs={{0,4},{4,8},{8,12},{12,16},{16,20},{20,24},{24,28},{1,5},{5,9},{9,... | collective-permute-start | bytes 786440 | tf_op jit(solution)/shard_map/ppermute | solution.py:31
  35.0 16.4 %collective-permute-start.1 = (f32[16,128,128]{2,1,0:T(8,128)}, f32[16,128,128]{2,1,0:T(8,128)}, u32[]{:S(2)}, u32[]{:S(2)}) collective-permute-start(f32[16,128,128]{2,1,0:T(8,128)} %multiply_add_fusion.1), channel_id=1, source_target_pairs={{0,4},{4,8},{8,12},{12,16},{16,20},{20,24},{24,28},{1,5},{5,9},{9,... | collective-permute-start | bytes 3145736 | tf_op jit(solution)/shard_map/ppermute | solution.py:31
  39.9 28.9 %all-to-all-start = ((bf16[64,4,4096]{2,0,1:T(8,128)(2,1)}), bf16[64,4,4096]{2,0,1:T(8,128)(2,1)S(1)}, u32[]{:S(2)}, u32[]{:S(2)}) async-start(bf16[64,4,4096]{2,0,1:T(8,128)(2,1)} %bitcast_dynamic-update-slice_fusion.1), calls=%async_computation | async-start | bytes 4194304 | tf_op jit(solution)/shard_map/all_to_all | solution.py:231
  43.6 25.2 %copy-start.1 = (s32[4]{0:T(128)S(1)}, s32[4]{0:T(128)}, u32[]{:S(2)}) copy-start(s32[4]{0:T(128)} %refs_0_.7) | copy-start | bytes 52
  53.8 24.8 %collective-permute-start.2 = (f32[16,128,128]{2,1,0:T(8,128)}, f32[16,128,128]{2,1,0:T(8,128)S(1)}, u32[]{:S(2)}, u32[]{:S(2)}) collective-permute-start(f32[16,128,128]{2,1,0:T(8,128)} %multiply_add_fusion), channel_id=1, source_target_pairs={{0,4},{4,8},{8,12},{12,16},{16,20},{20,24},{24,28},{1,5},{5,9},{9,... | collective-permute-start | bytes 3145736 | tf_op jit(solution)/shard_map/ppermute | solution.py:31
  78.6 1.0 %copy-start.3 = (f32[16,128,128]{2,1,0:T(8,128)}, f32[16,128,128]{2,1,0:T(8,128)S(1)}, u32[]{:S(2)}) copy-start(f32[16,128,128]{2,1,0:T(8,128)S(1)} %collective-permute-done.2.refs_3_.refs_4_) | copy-start | bytes 3145732

commit v4 on v3

--- a/solution.py
+++ b/solution.py
@@ -217,18 +217,40 @@
         taken = jnp.take(field.reshape(short_rows, KV_HEADS, HD), kv_table, axis=1)
         return taken.reshape(short_rows, head_devices, kv_local * HD)
 
-    raw = jnp.concatenate([soft_key, soft_value], axis=1)
-    shards = [raw]
-    for _ in range(SPAN):
-        shards.append(from_behind(shards[-1], "ctx", 1))
-    pieces = [soft_query.reshape(short_rows, head_devices, per_device * HD)]
-    for shard in shards:
-        pieces.append(spread(shard[:, : KV_HEADS * HD]))
-        pieces.append(spread(shard[:, KV_HEADS * HD :]))
-    packed = jnp.concatenate(pieces, axis=2)
+    packed = jnp.concatenate(
+        [
+            soft_query.reshape(short_rows, head_devices, per_device * HD),
+            spread(soft_key),
+            spread(soft_value),
+        ],
+        axis=2,
+    )
     per_dest = packed.shape[2]
     packed = packed.reshape(short_rows, head_devices * per_dest)
     mixed = lax.all_to_all(packed, "head", split_axis=1, concat_axis=0, tiled=True)
+    own_kv = mixed[:, per_device * HD :]
+    kv_width = own_kv.shape[1]
+
+    n_ctx = lax.axis_size("ctx")
+    even_to_odd = [(c, c + 1) for c in range(0, n_ctx - 1, 2)]
+    odd_to_next = [(c, c + 1) for c in range(1, n_ctx - 1, 2)]
+    even_to_even = [(c, c + 2) for c in range(0, n_ctx - 2, 2)]
+    is_odd = lax.rem(lax.axis_index("ctx"), 2) == 1
+
+    def send(value, pairs):
+        if not pairs:
+            return jnp.zeros_like(value)
+        return lax.ppermute(value, "ctx", pairs)
+
+    kv_a = send(own_kv, even_to_odd)
+    kv_b = send(jnp.concatenate([own_kv, kv_a], axis=1), odd_to_next)
+    kv_c1 = send(kv_b[:, :kv_width], even_to_even)
+    kv_c2 = send(kv_b, even_to_odd)
+    older = [
+        jnp.where(is_odd, kv_a, kv_b[:, :kv_width]),
+        jnp.where(is_odd, kv_c2[:, :kv_width], kv_b[:, kv_width:]),
+        jnp.where(is_odd, kv_c2[:, kv_width:], kv_c1),
+    ]
 
     lhpb = min(local_heads, group_size)
     lsteps = local_heads // lhpb
@@ -267,20 +289,26 @@
         ),
     )(lengths, shard_start, lin_query, lin_key, lin_value)
 
-    received = from_behind(tail, "ctx", 1)
-    onward = tail + through_own * received
-    lin_local, onward = lax.optimization_barrier((lin_local, onward))
-    received = from_behind(onward, "ctx", 1)
-    for _ in range(SPAN - 2):
-        received = from_behind(tail + through_own * received, "ctx", 1)
-    hi_state, lo_state = received, received
+    def through(shard):
+        first = shard * rows
+        return (doc_at(first - 1) == doc_at(first + rows - 1)).astype(F32)
+
+    here = lax.axis_index("ctx")
+    state_a = send(tail, even_to_odd)
+    state_v = tail + through_own * state_a
+    lin_local, state_v = lax.optimization_barrier((lin_local, state_v))
+    state_b = send(state_v, odd_to_next)
+    state_c1 = send(through(here) * through(here + 1) * state_b, even_to_even)
+    state_c2 = send(state_b, even_to_odd)
+    carried = jnp.where(is_odd, state_a + through(here - 1) * state_c2, state_b + state_c1)
+    hi_state, lo_state = carried, carried
 
     blocks = SPAN + 1
     shpb = min(per_device, group_size)
     ssteps = per_device // shpb
     kv_index = lambda i: (i * shpb * kv_local) // per_device
     def kv_spec(m, value):
-        base = per_device + 2 * kv_local * m + (kv_local if value else 0)
+        base = (per_device if m == 0 else 0) + (kv_local if value else 0)
         return pl.BlockSpec((rows, HD), lambda i: (0, base + kv_index(i)))
 
     attended = pl.pallas_call(
@@ -305,7 +333,7 @@
             transcendentals=rows * rows * blocks * per_device,
             bytes_accessed=rows * per_device * HD * 4 + 2 * blocks * rows * HD * 2 * per_device,
         ),
-    )(lengths, shard_start, mixed, *([mixed] * (2 * blocks)))
+    )(lengths, shard_start, mixed, mixed, *older, mixed, *older)
 
     lightning_out = pl.pallas_call(
         lambda *refs: lin_finish_kernel(lhpb, ndocs, *refs),

time: 84.8 us -> 77.5 us (0.914)
  the two profiles are of different devices: /device:TPU:8 before, /device:TPU:26 now
where the time goes in v4:
time: 77.5 us; the launch traced here: 78.2 us
  Pallas kernels  25.4 us (33%)
  waiting for transfers between devices  19.6 us (25%)
  starting transfers between devices  16.9 us (22%)
  other arithmetic  9.3 us (12%)
  between operations  4.49 us (6%)
  local copies, waits for them, and re-layouts  2.51 us (3%)
    ppermute x8, waiting for transfers between devices, send(): return lax.ppermute(value, 'ctx', pairs)  14.9 us
    ppermute x8, starting transfers between devices, send(): return lax.ppermute(value, 'ctx', pairs)  12.6 us
    pallas_call x1, Pallas kernels, body(): pl.pallas_call(lambda *refs: soft_kernel(blocks, shpb, ndocs, *refs), out...  12.1 us
    pallas_call x1, Pallas kernels, body(): pl.pallas_call(lambda *refs: lin_local_kernel(lhpb, ndocs, *refs), out_sh...  6.1 us
    all_to_all x1, waiting for transfers between devices, body(): lax.all_to_all(packed, 'head', split_axis=1, concat_axis=0, tiled=True)  4.65 us
    pallas_call x1, Pallas kernels, body(): pl.pallas_call(lambda *refs: lin_finish_kernel(lhpb, ndocs, *refs), out_s...  4.27 us
    all_to_all x1, starting transfers between devices, body(): lax.all_to_all(packed, 'head', split_axis=1, concat_axis=0, tiled=True)  4.25 us
    pallas_call x1, Pallas kernels, body(): pl.pallas_call(lambda *refs: tail_kernel(lhpb, ndocs, *refs), out_shape=j...  2.95 us
  transfers between devices with their start and end apart: 9, of which 5 were waited for; matrix products, arithmetic and copies ran while one was open for 11% of the time, Pallas kernels for 23%

profile of v4, /device:TPU:26, one launch (start us, length us, event | category | flops | bytes accessed | tf_op | source)
XLA Modules:
  0.0 78.2 jit_solution(8649732530517269726)
XLA Ops:
  0.7 3.0 %shard_map.95 = f32[16,128,128]{2,1,0:T(8,128)} custom-call(s32[4]{0:T(128)} %refs_0_.7, s32[1]{0:T(128)} %bitcast.refs_1_, bf16[256,2048]{1,0:T(8,128)(2,1)} %refs_3_.3, bf16[256,2048]{1,0:T(8,128)(2,1)} %refs_4_.1), custom_call_target="tpu_custom_call" | custom-call | flops 134217728 | bytes 3145728 | tf_op jit(solution)/shard_map/pallas_call | solution.py:258
  3.6 1.8 %collective-permute-start = (f32[16,128,128]{2,1,0:T(8,128)}, f32[16,128,128]{2,1,0:T(8,128)S(1)}, u32[]{:S(2)}, u32[]{:S(2)}) collective-permute-start(f32[16,128,128]{2,1,0:T(8,128)} %shard_map.95), channel_id=1, source_target_pairs={{0,4},{8,12},{16,20},{24,28},{1,5},{9,13},{17,21},{25,29},{2,6},{1... | collective-permute-start | bytes 3145736 | tf_op jit(solution)/shard_map/ppermute | solution.py:243
  5.6 1.2 %pad_maximum_fusion = bf16[64,4,2560]{2,0,1:T(8,128)(2,1)} fusion(bf16[64,4,256]{2,0,1:T(8,128)(2,1)S(1)} %get-tuple-element.15, bf16[64,4,256]{2,0,1:T(8,128)(2,1)S(1)} %get-tuple-element.16, bf16[64,4,2048]{2,0,1:T(8,128)(2,1)S(1)} %bitcast.21), kind=kLoop, calls=%fused_computation | loop fusion | flops 3932160 | bytes 2621440 | tf_op jit(solution)/shard_map/concatenate | solution.py:220
  6.7 4.2 %all-to-all-start = ((bf16[64,4,2560]{2,0,1:T(8,128)(2,1)}), bf16[64,4,2560]{2,0,1:T(8,128)(2,1)S(1)}, u32[]{:S(2)}, u32[]{:S(2)}) async-start(bf16[64,4,2560]{2,0,1:T(8,128)(2,1)} %pad_maximum_fusion), calls=%async_computation | async-start | bytes 2621440 | tf_op jit(solution)/shard_map/all_to_all | solution.py:230
  13.2 6.1 %shard_map.96.refs_5_ = f32[256,2048]{1,0:T(8,128)} custom-call(s32[4]{0:T(128)} %refs_0_.7, s32[1]{0:T(128)} %bitcast.refs_1_, bf16[256,2048]{1,0:T(8,128)(2,1)} %refs_2_.5, bf16[256,2048]{1,0:T(8,128)(2,1)} %refs_3_.3, bf16[256,2048]{1,0:T(8,128)(2,1)} %refs_4_.1), custom_call_target="tpu_custom_call" | custom-call | flops 805306368 | bytes 5242880 | tf_op jit(solution)/shard_map/pallas_call | solution.py:272
  19.3 1.1 %multiply_add_fusion = f32[16,128,128]{2,1,0:T(8,128)} fusion(f32[16,128,128]{2,1,0:T(8,128)S(1)} %copy-done.2, f32[16,128,128]{2,1,0:T(8,128)S(1)} %collective-permute-done, f32[]{:T(128)S(6)} %convert_element_type.39), kind=kLoop, calls=%fused_computation.3 | loop fusion | flops 524288 | bytes 3145732 | tf_op jit(solution)/shard_map/add | solution.py:298
  20.4 1.3 %collective-permute-start.1 = (f32[16,128,128]{2,1,0:T(8,128)}, f32[16,128,128]{2,1,0:T(8,128)S(1)}, u32[]{:S(2)}, u32[]{:S(2)}) collective-permute-start(f32[16,128,128]{2,1,0:T(8,128)} %multiply_add_fusion), channel_id=1, source_target_pairs={{4,8},{12,16},{20,24},{5,9},{13,17},{21,25},{6,10},{14,18},{22,26}... | collective-permute-start | bytes 3145736 | tf_op jit(solution)/shard_map/ppermute | solution.py:243
  21.7 4.7 %all-to-all-done = bf16[64,4,2560]{2,0,1:T(8,128)(2,1)S(1)} async-done(((bf16[64,4,2560]{2,0,1:T(8,128)(2,1)}), bf16[64,4,2560]{2,0,1:T(8,128)(2,1)S(1)}, u32[]{:S(2)}, u32[]{:S(2)}) %all-to-all-start) | async-done | bytes 1310752 | tf_op jit(solution)/shard_map/all_to_all | solution.py:230
  26.4 1.3 %collective-permute-start.4 = (bf16[256,512]{1,0:T(8,128)(2,1)S(1)}, bf16[256,512]{1,0:T(8,128)(2,1)S(1)}, u32[]{:S(2)}, u32[]{:S(2)}) collective-permute-start(bf16[256,512]{1,0:T(8,128)(2,1)S(1)} %slice.21), channel_id=1, source_target_pairs={{0,4},{8,12},{16,20},{24,28},{1,5},{9,13},{17,21},{25,29},{2,6},{1... | collective-permute-start | bytes 786440 | tf_op jit(solution)/shard_map/ppermute | solution.py:243
  27.7 1.1 %collective-permute-done.4 = bf16[256,512]{1,0:T(8,128)(2,1)S(1)} collective-permute-done((bf16[256,512]{1,0:T(8,128)(2,1)S(1)}, bf16[256,512]{1,0:T(8,128)(2,1)S(1)}, u32[]{:S(2)}, u32[]{:S(2)}) %collective-permute-start.4) | collective-permute-done | bytes 262176 | tf_op jit(solution)/shard_map/ppermute | solution.py:243
  30.4 1.3 %collective-permute-start.5 = (bf16[256,1024]{1,0:T(8,128)(2,1)}, bf16[256,1024]{1,0:T(8,128)(2,1)}, u32[]{:S(2)}, u32[]{:S(2)}) collective-permute-start(bf16[256,1024]{1,0:T(8,128)(2,1)} %pad_maximum_fusion.1), channel_id=1, source_target_pairs={{4,8},{12,16},{20,24},{5,9},{13,17},{21,25},{6,10},{14,18},{22,26}... | collective-permute-start | bytes 1572872 | tf_op jit(solution)/shard_map/ppermute | solution.py:243
  32.9 3.8 %collective-permute-done.1 = f32[16,128,128]{2,1,0:T(8,128)S(1)} collective-permute-done((f32[16,128,128]{2,1,0:T(8,128)}, f32[16,128,128]{2,1,0:T(8,128)S(1)}, u32[]{:S(2)}, u32[]{:S(2)}) %collective-permute-start.1) | collective-permute-done | bytes 1048608 | tf_op jit(solution)/shard_map/ppermute | solution.py:243
  36.7 1.1 %broadcast_multiply_fusion = f32[16,128,128]{2,1,0:T(8,128)} fusion(f32[16,128,128]{2,1,0:T(8,128)S(1)} %collective-permute-done.1, f32[]{:T(128)S(6)} %mul.38), kind=kLoop, calls=%fused_computation.5 | loop fusion | flops 262144 | bytes 2097156 | tf_op jit(solution)/shard_map/mul | solution.py:301
  37.8 1.3 %collective-permute-start.3 = (f32[16,128,128]{2,1,0:T(8,128)}, f32[16,128,128]{2,1,0:T(8,128)}, u32[]{:S(2)}, u32[]{:S(2)}) collective-permute-start(f32[16,128,128]{2,1,0:T(8,128)} %broadcast_multiply_fusion), channel_id=1, source_target_pairs={{0,8},{8,16},{16,24},{1,9},{9,17},{17,25},{2,10},{10,18},{18,26},{... | collective-permute-start | bytes 3145736 | tf_op jit(solution)/shard_map/ppermute | solution.py:243
  39.1 2.3 %collective-permute-start.2 = (f32[16,128,128]{2,1,0:T(8,128)S(1)}, f32[16,128,128]{2,1,0:T(8,128)}, u32[]{:S(2)}, u32[]{:S(2)}) collective-permute-start(f32[16,128,128]{2,1,0:T(8,128)S(1)} %collective-permute-done.1), channel_id=1, source_target_pairs={{0,4},{8,12},{16,20},{24,28},{1,5},{9,13},{17,21},{25,29},{2,6},{1... | collective-permute-start | bytes 3145736 | tf_op jit(solution)/shard_map/ppermute | solution.py:243
  41.4 1.1 %collective-permute-done.5 = bf16[256,1024]{1,0:T(8,128)(2,1)} collective-permute-done((bf16[256,1024]{1,0:T(8,128)(2,1)}, bf16[256,1024]{1,0:T(8,128)(2,1)}, u32[]{:S(2)}, u32[]{:S(2)}) %collective-permute-start.5) | collective-permute-done | bytes 524320 | tf_op jit(solution)/shard_map/ppermute | solution.py:243
  42.5 2.1 %collective-permute-start.6 = (bf16[256,1024]{1,0:T(8,128)(2,1)}, bf16[256,1024]{1,0:T(8,128)(2,1)}, u32[]{:S(2)}, u32[]{:S(2)}) collective-permute-start(bf16[256,1024]{1,0:T(8,128)(2,1)} %collective-permute-done.5), channel_id=1, source_target_pairs={{0,4},{8,12},{16,20},{24,28},{1,5},{9,13},{17,21},{25,29},{2,6},{1... | collective-permute-start | bytes 1572872 | tf_op jit(solution)/shard_map/ppermute | solution.py:243
  44.6 1.7 %slice.22 = bf16[256,512]{1,0:T(8,128)(2,1)} slice(bf16[256,1024]{1,0:T(8,128)(2,1)} %collective-permute-done.5), slice={[0:256], [0:512]} | slice | bytes 524288 | tf_op jit(solution)/shard_map/slice | solution.py:250
  46.2 1.3 %collective-permute-start.7 = (bf16[256,512]{1,0:T(8,128)(2,1)}, bf16[256,512]{1,0:T(8,128)(2,1)}, u32[]{:S(2)}, u32[]{:S(2)}) collective-permute-start(bf16[256,512]{1,0:T(8,128)(2,1)} %slice.22), channel_id=1, source_target_pairs={{0,8},{8,16},{16,24},{1,9},{9,17},{17,25},{2,10},{10,18},{18,26},{... | collective-permute-start | bytes 786440 | tf_op jit(solution)/shard_map/ppermute | solution.py:243
  48.7 8.9 %collective-permute-done.7 = bf16[256,512]{1,0:T(8,128)(2,1)} collective-permute-done((bf16[256,512]{1,0:T(8,128)(2,1)}, bf16[256,512]{1,0:T(8,128)(2,1)}, u32[]{:S(2)}, u32[]{:S(2)}) %collective-permute-start.7) | collective-permute-done | bytes 262176 | tf_op jit(solution)/shard_map/ppermute | solution.py:243
  57.6 1.4 %slice_select_fusion = (bf16[256,512]{1,0:T(8,128)(2,1)S(1)}, bf16[256,512]{1,0:T(8,128)(2,1)S(1)}, bf16[256,512]{1,0:T(8,128)(2,1)S(1)}) fusion(bf16[256,512]{1,0:T(8,128)(2,1)} %collective-permute-done.7, bf16[256,1024]{1,0:T(8,128)(2,1)} %collective-permute-done.6, pred[]{:T(512)S(6)} %eq.13, bf16[256,1024]{1,0:T(8,128)(2,1)} %collective-permute-done.5, ...), kind=kLoop, calls=%fused_computation.6 | loop fusion | flops 393216 | bytes 2359297 | tf_op jit(solution)/shard_map/jit(_where)/select_n | solution.py:252
  59.0 12.1 %shard_map.98 = bf16[256,2048]{1,0:T(8,128)(2,1)} custom-call(s32[4]{0:T(128)S(1)} %copy-done.1, s32[1]{0:T(128)} %bitcast.refs_1_, bf16[256,2560]{1,0:T(8,128)(2,1)S(1)} %bitcast.17, bf16[256,2560]{1,0:T(8,128)(2,1)S(1)} %bitcast.18, bf16[256,512]{1,0:T(8,128)(2,1)S(1)} %get-tuple-element.14.refs_4_.refs_8_, ...), custom_call_target="tpu_custom_call" | custom-call | flops 2147483648 | bytes 10485760 | tf_op jit(solution)/shard_map/pallas_call | solution.py:314
  71.1 2.8 %add_select_fusion.refs_3_.refs_4_ = f32[16,128,128]{2,1,0:T(8,128)} fusion(f32[16,128,128]{2,1,0:T(8,128)S(1)} %collective-permute-done.1, f32[16,128,128]{2,1,0:T(8,128)} %collective-permute-done.3, f32[16,128,128]{2,1,0:T(8,128)S(1)} %collective-permute-done, f32[16,128,128]{2,1,0:T(8,128)} %collective-permute-done.2, f32[]{:T(128)S(6)} %convert_element_type.36, ...), kind=kLoop, calls=%fused_computation.2 | loop fusion | flops 1048576 | bytes 5242885 | tf_op jit(solution)/shard_map/jit(_where)/select_n | solution.py:303
  73.9 4.3 %shard_map.97 = bf16[256,2048]{1,0:T(8,128)(2,1)} custom-call(s32[4]{0:T(128)} %refs_0_.7, s32[1]{0:T(128)} %bitcast.refs_1_, bf16[256,2048]{1,0:T(8,128)(2,1)} %refs_2_.5, f32[16,128,128]{2,1,0:T(8,128)} %add_select_fusion.refs_3_.refs_4_, f32[16,128,128]{2,1,0:T(8,128)} %add_select_fusion.refs_3_.refs_4_, f32[256,2048]{1,0:T(8,128)} %shard_map.96.refs_5_, ...), custom_call_target="tpu_custom_call" | custom-call | flops 268435456 | bytes 5242880 | tf_op jit(solution)/shard_map/pallas_call | solution.py:338
  (24 shorter events, 2.7 us)
Async XLA Ops:
  0.6 4.8 %copy-start.3 = (bf16[64,8192]{1,0:T(8,128)(2,1)S(1)}, bf16[64,8192]{1,0:T(8,128)(2,1)}, u32[]{:S(2)}) copy-start(bf16[64,8192]{1,0:T(8,128)(2,1)} %param.12) | copy-start | bytes 3145732
  0.6 4.9 %copy-start.5 = (bf16[64,1024]{1,0:T(8,128)(2,1)S(1)}, bf16[64,1024]{1,0:T(8,128)(2,1)}, u32[]{:S(2)}) copy-start(bf16[64,1024]{1,0:T(8,128)(2,1)} %param.14) | copy-start | bytes 393220
  0.7 4.9 %copy-start.6 = (bf16[64,1024]{1,0:T(8,128)(2,1)S(1)}, bf16[64,1024]{1,0:T(8,128)(2,1)}, u32[]{:S(2)}) copy-start(bf16[64,1024]{1,0:T(8,128)(2,1)} %param.13) | copy-start | bytes 393220
  3.6 15.7 %collective-permute-start = (f32[16,128,128]{2,1,0:T(8,128)}, f32[16,128,128]{2,1,0:T(8,128)S(1)}, u32[]{:S(2)}, u32[]{:S(2)}) collective-permute-start(f32[16,128,128]{2,1,0:T(8,128)} %shard_map.95), channel_id=1, source_target_pairs={{0,4},{8,12},{16,20},{24,28},{1,5},{9,13},{17,21},{25,29},{2,6},{1... | collective-permute-start | bytes 3145736 | tf_op jit(solution)/shard_map/ppermute | solution.py:243
  5.6 5.4 %copy-start = (s32[4]{0:T(128)S(1)}, s32[4]{0:T(128)}, u32[]{:S(2)}) copy-start(s32[4]{0:T(128)} %refs_0_.7) | copy-start | bytes 52
  6.7 19.7 %all-to-all-start = ((bf16[64,4,2560]{2,0,1:T(8,128)(2,1)}), bf16[64,4,2560]{2,0,1:T(8,128)(2,1)S(1)}, u32[]{:S(2)}, u32[]{:S(2)}) async-start(bf16[64,4,2560]{2,0,1:T(8,128)(2,1)} %pad_maximum_fusion), calls=%async_computation | async-start | bytes 2621440 | tf_op jit(solution)/shard_map/all_to_all | solution.py:230
  13.2 6.1 %copy-start.2 = (f32[16,128,128]{2,1,0:T(8,128)S(1)}, f32[16,128,128]{2,1,0:T(8,128)}, u32[]{:S(2)}) copy-start(f32[16,128,128]{2,1,0:T(8,128)} %shard_map.95) | copy-start | bytes 3145732
  20.4 16.3 %collective-permute-start.1 = (f32[16,128,128]{2,1,0:T(8,128)}, f32[16,128,128]{2,1,0:T(8,128)S(1)}, u32[]{:S(2)}, u32[]{:S(2)}) collective-permute-start(f32[16,128,128]{2,1,0:T(8,128)} %multiply_add_fusion), channel_id=1, source_target_pairs={{4,8},{12,16},{20,24},{5,9},{13,17},{21,25},{6,10},{14,18},{22,26}... | collective-permute-start | bytes 3145736 | tf_op jit(solution)/shard_map/ppermute | solution.py:243
  26.4 2.4 %collective-permute-start.4 = (bf16[256,512]{1,0:T(8,128)(2,1)S(1)}, bf16[256,512]{1,0:T(8,128)(2,1)S(1)}, u32[]{:S(2)}, u32[]{:S(2)}) collective-permute-start(bf16[256,512]{1,0:T(8,128)(2,1)S(1)} %slice.21), channel_id=1, source_target_pairs={{0,4},{8,12},{16,20},{24,28},{1,5},{9,13},{17,21},{25,29},{2,6},{1... | collective-permute-start | bytes 786440 | tf_op jit(solution)/shard_map/ppermute | solution.py:243
  28.8 0.7 copy-start.4
  30.4 12.0 %collective-permute-start.5 = (bf16[256,1024]{1,0:T(8,128)(2,1)}, bf16[256,1024]{1,0:T(8,128)(2,1)}, u32[]{:S(2)}, u32[]{:S(2)}) collective-permute-start(bf16[256,1024]{1,0:T(8,128)(2,1)} %pad_maximum_fusion.1), channel_id=1, source_target_pairs={{4,8},{12,16},{20,24},{5,9},{13,17},{21,25},{6,10},{14,18},{22,26}... | collective-permute-start | bytes 1572872 | tf_op jit(solution)/shard_map/ppermute | solution.py:243
  32.9 26.1 %copy-start.1 = (s32[4]{0:T(128)S(1)}, s32[4]{0:T(128)}, u32[]{:S(2)}) copy-start(s32[4]{0:T(128)} %refs_0_.7) | copy-start | bytes 52
  37.8 33.3 %collective-permute-start.3 = (f32[16,128,128]{2,1,0:T(8,128)}, f32[16,128,128]{2,1,0:T(8,128)}, u32[]{:S(2)}, u32[]{:S(2)}) collective-permute-start(f32[16,128,128]{2,1,0:T(8,128)} %broadcast_multiply_fusion), channel_id=1, source_target_pairs={{0,8},{8,16},{16,24},{1,9},{9,17},{17,25},{2,10},{10,18},{18,26},{... | collective-permute-start | bytes 3145736 | tf_op jit(solution)/shard_map/ppermute | solution.py:243
  39.1 32.0 %collective-permute-start.2 = (f32[16,128,128]{2,1,0:T(8,128)S(1)}, f32[16,128,128]{2,1,0:T(8,128)}, u32[]{:S(2)}, u32[]{:S(2)}) collective-permute-start(f32[16,128,128]{2,1,0:T(8,128)S(1)} %collective-permute-done.1), channel_id=1, source_target_pairs={{0,4},{8,12},{16,20},{24,28},{1,5},{9,13},{17,21},{25,29},{2,6},{1... | collective-permute-start | bytes 3145736 | tf_op jit(solution)/shard_map/ppermute | solution.py:243
  42.5 15.1 %collective-permute-start.6 = (bf16[256,1024]{1,0:T(8,128)(2,1)}, bf16[256,1024]{1,0:T(8,128)(2,1)}, u32[]{:S(2)}, u32[]{:S(2)}) collective-permute-start(bf16[256,1024]{1,0:T(8,128)(2,1)} %collective-permute-done.5), channel_id=1, source_target_pairs={{0,4},{8,12},{16,20},{24,28},{1,5},{9,13},{17,21},{25,29},{2,6},{1... | collective-permute-start | bytes 1572872 | tf_op jit(solution)/shard_map/ppermute | solution.py:243
  46.2 11.4 %collective-permute-start.7 = (bf16[256,512]{1,0:T(8,128)(2,1)}, bf16[256,512]{1,0:T(8,128)(2,1)}, u32[]{:S(2)}, u32[]{:S(2)}) collective-permute-start(bf16[256,512]{1,0:T(8,128)(2,1)} %slice.22), channel_id=1, source_target_pairs={{0,8},{8,16},{16,24},{1,9},{9,17},{17,25},{2,10},{10,18},{18,26},{... | collective-permute-start | bytes 786440 | tf_op jit(solution)/shard_map/ppermute | solution.py:243

commit v5 on v4

--- a/solution.py
+++ b/solution.py
@@ -92,14 +92,19 @@
         )
 
 
-def lin_finish_kernel(hpb, ndocs, len_ref, start_ref, q_ref, hi_ref, lo_ref, lin_ref, g_ref, o_ref):
+def lin_finish_kernel(
+    hpb, ndocs, len_ref, start_ref, q_ref, a_ref, c2_ref, b_ref, c1_ref, lin_ref, g_ref, o_ref
+):
     rows = q_ref.shape[0]
     ends = doc_ends(len_ref, ndocs)
     start = start_ref[0]
     pos = start + lax.broadcasted_iota(jnp.int32, (rows, 1), 0)
     sees = (doc_of(ends, pos) == doc_of(ends, start - 1)).astype(F32)
+    odd = lax.rem(start // rows, 2) == 1
+    through_prev = (doc_of(ends, start - rows - 1) == doc_of(ends, start - 1)).astype(F32)
     for j in range(hpb):
-        hi, lo = split_bf16(hi_ref[j])
+        state = jnp.where(odd, a_ref[j] + through_prev * c2_ref[j], b_ref[j] + c1_ref[j])
+        hi, lo = split_bf16(state)
         q = q_ref[:, head_cols(j)]
         carried = jnp.dot(q, hi, preferred_element_type=F32) + jnp.dot(
             q, lo, preferred_element_type=F32
@@ -123,11 +128,22 @@
 
 
 def soft_kernel(blocks, hpb, ndocs, len_ref, start_ref, q_ref, *rest):
-    key_refs = rest[0:blocks]
-    value_refs = rest[blocks : 2 * blocks]
-    o_ref = rest[2 * blocks]
-    s_ref, mx_ref, tot_ref, acc_ref = rest[2 * blocks + 1 :]
+    per_kind = 2 * blocks - 1
+    o_ref = rest[2 * per_kind]
+    s_ref, mx_ref, tot_ref, acc_ref = rest[2 * per_kind + 1 :]
     rows = q_ref.shape[0]
+    odd = lax.rem(start_ref[0] // rows, 2) == 1
+
+    def pick(refs):
+        picked = [lambda: refs[0][...]]
+        for m in range(1, blocks):
+            picked.append(
+                lambda m=m: jnp.where(odd, refs[2 * m - 1][...], refs[2 * m][...])
+            )
+        return picked
+
+    key_refs = pick(rest[0:per_kind])
+    value_refs = pick(rest[per_kind : 2 * per_kind])
     scale = 1.0 / math.sqrt(HD)
     ends = doc_ends(len_ref, ndocs)
     start = start_ref[0]
@@ -142,7 +158,7 @@
         visible = dq == doc_of(ends, shifted)
         if m == 0:
             visible = visible & (shifted <= qpos)
-        s = dot_nt(q, key_refs[m][...].reshape(rows, HD)).reshape(hpb, rows, rows) * scale
+        s = dot_nt(q, key_refs[m]()).reshape(hpb, rows, rows) * scale
         return jnp.where(visible[None], s, -1e30)
 
     def needed(m):
@@ -164,7 +180,7 @@
         part = jnp.sum(w, axis=-1, keepdims=True)
         term = jnp.dot(
             w.reshape(hpb * rows, rows).astype(BF16),
-            value_refs[m][...].reshape(rows, HD),
+            value_refs[m](),
             preferred_element_type=F32,
         ).reshape(hpb, rows, HD)
         return part, term
@@ -217,18 +233,10 @@
         taken = jnp.take(field.reshape(short_rows, KV_HEADS, HD), kv_table, axis=1)
         return taken.reshape(short_rows, head_devices, kv_local * HD)
 
-    packed = jnp.concatenate(
-        [
-            soft_query.reshape(short_rows, head_devices, per_device * HD),
-            spread(soft_key),
-            spread(soft_value),
-        ],
-        axis=2,
-    )
-    per_dest = packed.shape[2]
-    packed = packed.reshape(short_rows, head_devices * per_dest)
-    mixed = lax.all_to_all(packed, "head", split_axis=1, concat_axis=0, tiled=True)
-    own_kv = mixed[:, per_device * HD :]
+    kv_packed = jnp.concatenate([spread(soft_key), spread(soft_value)], axis=2)
+    kv_packed = kv_packed.reshape(short_rows, head_devices * 2 * kv_local * HD)
+    own_kv = lax.all_to_all(kv_packed, "head", split_axis=1, concat_axis=0, tiled=True)
+    mixed = lax.all_to_all(soft_query, "head", split_axis=1, concat_axis=0, tiled=True)
     kv_width = own_kv.shape[1]
 
     n_ctx = lax.axis_size("ctx")
@@ -246,11 +254,8 @@
     kv_b = send(jnp.concatenate([own_kv, kv_a], axis=1), odd_to_next)
     kv_c1 = send(kv_b[:, :kv_width], even_to_even)
     kv_c2 = send(kv_b, even_to_odd)
-    older = [
-        jnp.where(is_odd, kv_a, kv_b[:, :kv_width]),
-        jnp.where(is_odd, kv_c2[:, :kv_width], kv_b[:, kv_width:]),
-        jnp.where(is_odd, kv_c2[:, kv_width:], kv_c1),
-    ]
+    odd_src = [(own_kv, 0), (kv_a, 0), (kv_c2, 0), (kv_c2, 2 * kv_local)]
+    even_src = [(own_kv, 0), (kv_b, 0), (kv_b, 2 * kv_local), (kv_c1, 0)]
 
     lhpb = min(local_heads, group_size)
     lsteps = local_heads // lhpb
@@ -300,24 +305,27 @@
     state_b = send(state_v, odd_to_next)
     state_c1 = send(through(here) * through(here + 1) * state_b, even_to_even)
     state_c2 = send(state_b, even_to_odd)
-    carried = jnp.where(is_odd, state_a + through(here - 1) * state_c2, state_b + state_c1)
-    hi_state, lo_state = carried, carried
 
     blocks = SPAN + 1
     shpb = min(per_device, group_size)
     ssteps = per_device // shpb
     kv_index = lambda i: (i * shpb * kv_local) // per_device
-    def kv_spec(m, value):
-        base = (per_device if m == 0 else 0) + (kv_local if value else 0)
+    def kv_spec(offset, value):
+        base = offset + (kv_local if value else 0)
         return pl.BlockSpec((rows, HD), lambda i: (0, base + kv_index(i)))
+
+    kv_arrays, kv_specs = [], []
+    for value in (False, True):
+        for m in range(blocks):
+            for source in ((odd_src[m],) if m == 0 else (odd_src[m], even_src[m])):
+                kv_arrays.append(source[0])
+                kv_specs.append(kv_spec(source[1], value))
 
     attended = pl.pallas_call(
         lambda *refs: soft_kernel(blocks, shpb, ndocs, *refs),
         out_shape=jax.ShapeDtypeStruct((rows, per_device * HD), BF16),
         grid=(ssteps,),
-        in_specs=[smem_spec(), smem_spec(), col_spec(rows, shpb * HD)]
-        + [kv_spec(m, False) for m in range(blocks)]
-        + [kv_spec(m, True) for m in range(blocks)],
+        in_specs=[smem_spec(), smem_spec(), col_spec(rows, shpb * HD)] + kv_specs,
         out_specs=col_spec(rows, shpb * HD),
         scratch_shapes=[
             pltpu.VMEM((blocks, shpb, rows, rows), F32),
@@ -333,7 +341,7 @@
             transcendentals=rows * rows * blocks * per_device,
             bytes_accessed=rows * per_device * HD * 4 + 2 * blocks * rows * HD * 2 * per_device,
         ),
-    )(lengths, shard_start, mixed, mixed, *older, mixed, *older)
+    )(lengths, shard_start, mixed, *kv_arrays)
 
     lightning_out = pl.pallas_call(
         lambda *refs: lin_finish_kernel(lhpb, ndocs, *refs),
@@ -343,6 +351,8 @@
             smem_spec(),
             smem_spec(),
             col_spec(rows, lwide),
+            pl.BlockSpec((lhpb, HD, HD), lambda h: (h, 0, 0)),
+            pl.BlockSpec((lhpb, HD, HD), lambda h: (h, 0, 0)),
             pl.BlockSpec((lhpb, HD, HD), lambda h: (h, 0, 0)),
             pl.BlockSpec((lhpb, HD, HD), lambda h: (h, 0, 0)),
             col_spec(rows, lwide),
@@ -355,7 +365,17 @@
             transcendentals=rows * local_heads,
             bytes_accessed=rows * width * (2 + 4 + 2) + local_heads * HD * HD * 4,
         ),
-    )(lengths, shard_start, lin_query, hi_state, lo_state, lin_local, norm_gain.reshape(1, width))
+    )(
+        lengths,
+        shard_start,
+        lin_query,
+        state_a,
+        state_c2,
+        state_b,
+        state_c1,
+        lin_local,
+        norm_gain.reshape(1, width),
+    )
     return (lightning_out, attended)
 
 

time: 77.5 us -> 72.8 us (0.939)
  the two profiles are of different devices: /device:TPU:26 before, /device:TPU:17 now
where the time goes in v5:
time: 72.8 us; the launch traced here: 72.1 us
  Pallas kernels  25.8 us (35%)
  starting transfers between devices  17.7 us (24%)
  waiting for transfers between devices  11.9 us (16%)
  blocking collectives  7.94 us (11%)
  other arithmetic  4.21 us (6%)
  between operations  3.39 us (5%)
  local copies, waits for them, and re-layouts  1.11 us (2%)
    ppermute x8, starting transfers between devices, send(): return lax.ppermute(value, 'ctx', pairs)  14.2 us
    pallas_call x1, Pallas kernels, body(): pl.pallas_call(lambda *refs: soft_kernel(blocks, shpb, ndocs, *refs), out...  12.3 us
    all_to_all x1, waiting for transfers between devices, body(): lax.all_to_all(soft_query, 'head', split_axis=1, concat_axis=0, tiled=True)  11.1 us
    all_to_all x1, blocking collectives, body(): lax.all_to_all(kv_packed, 'head', split_axis=1, concat_axis=0, tiled=True)  7.94 us
    pallas_call x1, Pallas kernels, body(): pl.pallas_call(lambda *refs: lin_local_kernel(lhpb, ndocs, *refs), out_sh...  6.11 us
    pallas_call x1, Pallas kernels, body(): pl.pallas_call(lambda *refs: lin_finish_kernel(lhpb, ndocs, *refs), out_s...  4.54 us
    all_to_all x1, starting transfers between devices, body(): lax.all_to_all(soft_query, 'head', split_axis=1, concat_axis=0, tiled=True)  3.52 us
    pallas_call x1, Pallas kernels, body(): pl.pallas_call(lambda *refs: tail_kernel(lhpb, ndocs, *refs), out_shape=j...  2.86 us
  transfers between devices with their start and end apart: 9, of which 2 were waited for; matrix products, arithmetic and copies ran while one was open for 7% of the time, Pallas kernels for 26%

profile of v5, /device:TPU:17, one launch (start us, length us, event | category | flops | bytes accessed | tf_op | source)
XLA Modules:
  0.0 72.1 jit_solution(18389828688416164719)
XLA Ops:
  0.6 0.0 copy-start
  0.6 2.9 %shard_map.95 = f32[16,128,128]{2,1,0:T(8,128)} custom-call(s32[4]{0:T(128)} %refs_0_.7, s32[1]{0:T(128)} %bitcast.refs_1_, bf16[256,2048]{1,0:T(8,128)(2,1)} %refs_3_.3, bf16[256,2048]{1,0:T(8,128)(2,1)} %refs_4_.1), custom_call_target="tpu_custom_call" | custom-call | flops 134217728 | bytes 3145728 | tf_op jit(solution)/shard_map/pallas_call | solution.py:263
  3.5 1.3 %collective-permute-start = (f32[16,128,128]{2,1,0:T(8,128)}, f32[16,128,128]{2,1,0:T(8,128)S(1)}, u32[]{:S(2)}, u32[]{:S(2)}) collective-permute-start(f32[16,128,128]{2,1,0:T(8,128)} %shard_map.95), channel_id=1, source_target_pairs={{0,4},{8,12},{16,20},{24,28},{1,5},{9,13},{17,21},{25,29},{2,6},{1... | collective-permute-start | bytes 3145736 | tf_op jit(solution)/shard_map/ppermute | solution.py:251
  4.8 0.2 reduce-window.9
  5.0 0.7 fusion.3
  6.9 6.1 %shard_map.96.refs_7_ = f32[256,2048]{1,0:T(8,128)} custom-call(s32[4]{0:T(128)} %refs_0_.7, s32[1]{0:T(128)} %bitcast.refs_1_, bf16[256,2048]{1,0:T(8,128)(2,1)} %refs_2_.5, bf16[256,2048]{1,0:T(8,128)(2,1)} %refs_3_.3, bf16[256,2048]{1,0:T(8,128)(2,1)} %refs_4_.1), custom_call_target="tpu_custom_call" | custom-call | flops 805306368 | bytes 5242880 | tf_op jit(solution)/shard_map/pallas_call | solution.py:277
  13.1 0.1 multiply_add_fusion
  13.2 5.4 %collective-permute-start.1 = (f32[16,128,128]{2,1,0:T(8,128)S(1)}, f32[16,128,128]{2,1,0:T(8,128)}, u32[]{:S(2)}, u32[]{:S(2)}) collective-permute-start(f32[16,128,128]{2,1,0:T(8,128)S(1)} %multiply_add_fusion), channel_id=1, source_target_pairs={{4,8},{12,16},{20,24},{5,9},{13,17},{21,25},{6,10},{14,18},{22,26}... | collective-permute-start | bytes 3145736 | tf_op jit(solution)/shard_map/ppermute | solution.py:251
  18.6 0.0 copy-start.4
  18.7 7.9 %all_to_all.35 = bf16[64,4,512]{2,0,1:T(8,128)(2,1)S(1)} all-to-all(bf16[64,4,512]{2,0,1:T(8,128)(2,1)S(1)} %pad_maximum_fusion.1), channel_id=1, replica_groups=mesh['ctx'=8,'head'=4] {'head'}, dimensions={1} | all-to-all | bytes 524288 | tf_op jit(solution)/shard_map/all_to_all | solution.py:238
  26.6 1.3 %collective-permute-start.4 = (bf16[256,512]{1,0:T(8,128)(2,1)S(1)}, bf16[256,512]{1,0:T(8,128)(2,1)S(1)}, u32[]{:S(2)}, u32[]{:S(2)}) collective-permute-start(bf16[256,512]{1,0:T(8,128)(2,1)S(1)} %bitcast.20), channel_id=1, source_target_pairs={{0,4},{8,12},{16,20},{24,28},{1,5},{9,13},{17,21},{25,29},{2,6},{1... | collective-permute-start | bytes 786440 | tf_op jit(solution)/shard_map/ppermute | solution.py:251
  29.2 0.8 %collective-permute-done.4.refs_4_.refs_11_ = bf16[256,512]{1,0:T(8,128)(2,1)S(1)} collective-permute-done((bf16[256,512]{1,0:T(8,128)(2,1)S(1)}, bf16[256,512]{1,0:T(8,128)(2,1)S(1)}, u32[]{:S(2)}, u32[]{:S(2)}) %collective-permute-start.4) | collective-permute-done | bytes 262176 | tf_op jit(solution)/shard_map/ppermute | solution.py:251
  30.1 0.9 %pad_maximum_fusion = bf16[256,1024]{1,0:T(8,128)(2,1)} fusion(bf16[256,512]{1,0:T(8,128)(2,1)S(1)} %collective-permute-done.4.refs_4_.refs_11_, bf16[256,512]{1,0:T(8,128)(2,1)S(1)} %bitcast.21), kind=kLoop, calls=%fused_computation.2 | loop fusion | flops 1048576 | bytes 1048576 | tf_op jit(solution)/shard_map/concatenate | solution.py:254
  30.9 1.3 %collective-permute-start.5 = (bf16[256,1024]{1,0:T(8,128)(2,1)}, bf16[256,1024]{1,0:T(8,128)(2,1)S(1)}, u32[]{:S(2)}, u32[]{:S(2)}) collective-permute-start(bf16[256,1024]{1,0:T(8,128)(2,1)} %pad_maximum_fusion), channel_id=1, source_target_pairs={{4,8},{12,16},{20,24},{5,9},{13,17},{21,25},{6,10},{14,18},{22,26}... | collective-permute-start | bytes 1572872 | tf_op jit(solution)/shard_map/ppermute | solution.py:251
  32.3 2.3 %broadcast_multiply_fusion = f32[16,128,128]{2,1,0:T(8,128)} fusion(f32[16,128,128]{2,1,0:T(8,128)} %collective-permute-done.1.refs_5_, f32[]{:T(128)S(6)} %mul.26), kind=kLoop, calls=%fused_computation.3 | loop fusion | flops 262144 | bytes 2097156 | tf_op jit(solution)/shard_map/mul | solution.py:306
  34.6 1.7 %collective-permute-start.3 = (f32[16,128,128]{2,1,0:T(8,128)}, f32[16,128,128]{2,1,0:T(8,128)}, u32[]{:S(2)}, u32[]{:S(2)}) collective-permute-start(f32[16,128,128]{2,1,0:T(8,128)} %broadcast_multiply_fusion), channel_id=1, source_target_pairs={{0,8},{8,16},{16,24},{1,9},{9,17},{17,25},{2,10},{10,18},{18,26},{... | collective-permute-start | bytes 3145736 | tf_op jit(solution)/shard_map/ppermute | solution.py:251
  36.2 1.3 %collective-permute-start.2 = (f32[16,128,128]{2,1,0:T(8,128)}, f32[16,128,128]{2,1,0:T(8,128)}, u32[]{:S(2)}, u32[]{:S(2)}) collective-permute-start(f32[16,128,128]{2,1,0:T(8,128)} %collective-permute-done.1.refs_5_), channel_id=1, source_target_pairs={{0,4},{8,12},{16,20},{24,28},{1,5},{9,13},{17,21},{25,29},{2,6},{1... | collective-permute-start | bytes 3145736 | tf_op jit(solution)/shard_map/ppermute | solution.py:251
  37.5 1.0 %copy.19 = bf16[8,4,8,2048]{3,2,0,1:T(8,128)(2,1)} copy(bf16[8,4,8,2048]{3,2,1,0:T(8,128)(2,1)S(1)} %bitcast.25) | data formatting | bytes 2097152 | tf_op jit(solution)/shard_map/all_to_all | solution.py:239
  38.6 3.5 %all-to-all-start = ((bf16[64,4,2048]{2,0,1:T(8,128)(2,1)}), bf16[64,4,2048]{2,0,1:T(8,128)(2,1)S(1)}, u32[]{:S(2)}, u32[]{:S(2)}) async-start(bf16[64,4,2048]{2,0,1:T(8,128)(2,1)} %bitcast.18), calls=%async_computation | async-start | bytes 2097152 | tf_op jit(solution)/shard_map/all_to_all | solution.py:239
  42.1 1.3 %collective-permute-start.6 = (bf16[256,1024]{1,0:T(8,128)(2,1)S(1)}, bf16[256,1024]{1,0:T(8,128)(2,1)S(1)}, u32[]{:S(2)}, u32[]{:S(2)}) collective-permute-start(bf16[256,1024]{1,0:T(8,128)(2,1)S(1)} %collective-permute-done.5.refs_5_.refs_7_.refs_12_.refs_14_), channel_id=1, source_target_pairs={{0,4},{8,12},{16,20},{24,28},{1,5},{9,13},{17,21},{25,29},{2,6},{1... | collective-permute-start | bytes 1572872 | tf_op jit(solution)/shard_map/ppermute | solution.py:251
  43.4 0.7 collective-permute-start.7
  44.1 11.1 %all-to-all-done = bf16[64,4,2048]{2,0,1:T(8,128)(2,1)S(1)} async-done(((bf16[64,4,2048]{2,0,1:T(8,128)(2,1)}), bf16[64,4,2048]{2,0,1:T(8,128)(2,1)S(1)}, u32[]{:S(2)}, u32[]{:S(2)}) %all-to-all-start) | async-done | bytes 1048608 | tf_op jit(solution)/shard_map/all_to_all | solution.py:239
  55.2 12.3 %shard_map.98 = bf16[256,2048]{1,0:T(8,128)(2,1)} custom-call(s32[4]{0:T(128)S(1)} %copy-done.1, s32[1]{0:T(128)} %bitcast.refs_1_, bf16[256,2048]{1,0:T(8,128)(2,1)S(1)} %bitcast.19, bf16[256,512]{1,0:T(8,128)(2,1)S(1)} %bitcast.22, bf16[256,512]{1,0:T(8,128)(2,1)S(1)} %collective-permute-done.4.refs_4_.refs_11_, ...), custom_call_target="tpu_custom_call" | custom-call | flops 2147483648 | bytes 10485760 | tf_op jit(solution)/shard_map/pallas_call | solution.py:324
  67.5 4.5 %shard_map.97 = bf16[256,2048]{1,0:T(8,128)(2,1)} custom-call(s32[4]{0:T(128)} %refs_0_.7, s32[1]{0:T(128)} %bitcast.refs_1_, bf16[256,2048]{1,0:T(8,128)(2,1)} %refs_2_.5, f32[16,128,128]{2,1,0:T(8,128)} %copy-done.2, f32[16,128,128]{2,1,0:T(8,128)} %collective-permute-done.2.refs_4_, f32[16,128,128]{2,1,0:T(8,128)} %collective-permute-done.1.refs_5_, ...), custom_call_target="tpu_custom_call" | custom-call | flops 268435456 | bytes 5242880 | tf_op jit(solution)/shard_map/pallas_call | solution.py:346
  (22 shorter events, 0.1 us)
Async XLA Ops:
  0.6 4.2 %copy-start = (s32[4]{0:T(128)S(1)}, s32[4]{0:T(128)}, u32[]{:S(2)}) copy-start(s32[4]{0:T(128)} %refs_0_.7) | copy-start | bytes 52
  3.5 9.6 %collective-permute-start = (f32[16,128,128]{2,1,0:T(8,128)}, f32[16,128,128]{2,1,0:T(8,128)S(1)}, u32[]{:S(2)}, u32[]{:S(2)}) collective-permute-start(f32[16,128,128]{2,1,0:T(8,128)} %shard_map.95), channel_id=1, source_target_pairs={{0,4},{8,12},{16,20},{24,28},{1,5},{9,13},{17,21},{25,29},{2,6},{1... | collective-permute-start | bytes 3145736 | tf_op jit(solution)/shard_map/ppermute | solution.py:251
  6.9 6.1 %copy-start.3 = (f32[16,128,128]{2,1,0:T(8,128)S(1)}, f32[16,128,128]{2,1,0:T(8,128)}, u32[]{:S(2)}) copy-start(f32[16,128,128]{2,1,0:T(8,128)} %shard_map.95) | copy-start | bytes 3145732
  13.0 5.6 %copy-start.5 = (bf16[64,1024]{1,0:T(8,128)(2,1)S(1)}, bf16[64,1024]{1,0:T(8,128)(2,1)}, u32[]{:S(2)}) copy-start(bf16[64,1024]{1,0:T(8,128)(2,1)} %param.14) | copy-start | bytes 393220
  13.1 5.6 %copy-start.6 = (bf16[64,1024]{1,0:T(8,128)(2,1)S(1)}, bf16[64,1024]{1,0:T(8,128)(2,1)}, u32[]{:S(2)}) copy-start(bf16[64,1024]{1,0:T(8,128)(2,1)} %param.13) | copy-start | bytes 393220
  13.1 5.6 %copy-start.2 = (f32[16,128,128]{2,1,0:T(8,128)}, f32[16,128,128]{2,1,0:T(8,128)S(1)}, u32[]{:S(2)}) copy-start(f32[16,128,128]{2,1,0:T(8,128)S(1)} %collective-permute-done.refs_3_) | copy-start | bytes 3145732
  13.2 19.0 %collective-permute-start.1 = (f32[16,128,128]{2,1,0:T(8,128)S(1)}, f32[16,128,128]{2,1,0:T(8,128)}, u32[]{:S(2)}, u32[]{:S(2)}) collective-permute-start(f32[16,128,128]{2,1,0:T(8,128)S(1)} %multiply_add_fusion), channel_id=1, source_target_pairs={{4,8},{12,16},{20,24},{5,9},{13,17},{21,25},{6,10},{14,18},{22,26}... | collective-permute-start | bytes 3145736 | tf_op jit(solution)/shard_map/ppermute | solution.py:251
  18.6 18.9 %copy-start.4 = (bf16[64,8192]{1,0:T(8,128)(2,1)S(1)}, bf16[64,8192]{1,0:T(8,128)(2,1)}, u32[]{:S(2)}) copy-start(bf16[64,8192]{1,0:T(8,128)(2,1)} %param.12) | copy-start | bytes 3145732
  26.6 3.4 %collective-permute-start.4 = (bf16[256,512]{1,0:T(8,128)(2,1)S(1)}, bf16[256,512]{1,0:T(8,128)(2,1)S(1)}, u32[]{:S(2)}, u32[]{:S(2)}) collective-permute-start(bf16[256,512]{1,0:T(8,128)(2,1)S(1)} %bitcast.20), channel_id=1, source_target_pairs={{0,4},{8,12},{16,20},{24,28},{1,5},{9,13},{17,21},{25,29},{2,6},{1... | collective-permute-start | bytes 786440 | tf_op jit(solution)/shard_map/ppermute | solution.py:251
  30.9 11.2 %collective-permute-start.5 = (bf16[256,1024]{1,0:T(8,128)(2,1)}, bf16[256,1024]{1,0:T(8,128)(2,1)S(1)}, u32[]{:S(2)}, u32[]{:S(2)}) collective-permute-start(bf16[256,1024]{1,0:T(8,128)(2,1)} %pad_maximum_fusion), channel_id=1, source_target_pairs={{4,8},{12,16},{20,24},{5,9},{13,17},{21,25},{6,10},{14,18},{22,26}... | collective-permute-start | bytes 1572872 | tf_op jit(solution)/shard_map/ppermute | solution.py:251
  34.6 33.0 %collective-permute-start.3 = (f32[16,128,128]{2,1,0:T(8,128)}, f32[16,128,128]{2,1,0:T(8,128)}, u32[]{:S(2)}, u32[]{:S(2)}) collective-permute-start(f32[16,128,128]{2,1,0:T(8,128)} %broadcast_multiply_fusion), channel_id=1, source_target_pairs={{0,8},{8,16},{16,24},{1,9},{9,17},{17,25},{2,10},{10,18},{18,26},{... | collective-permute-start | bytes 3145736 | tf_op jit(solution)/shard_map/ppermute | solution.py:251
  36.2 31.3 %collective-permute-start.2 = (f32[16,128,128]{2,1,0:T(8,128)}, f32[16,128,128]{2,1,0:T(8,128)}, u32[]{:S(2)}, u32[]{:S(2)}) collective-permute-start(f32[16,128,128]{2,1,0:T(8,128)} %collective-permute-done.1.refs_5_), channel_id=1, source_target_pairs={{0,4},{8,12},{16,20},{24,28},{1,5},{9,13},{17,21},{25,29},{2,6},{1... | collective-permute-start | bytes 3145736 | tf_op jit(solution)/shard_map/ppermute | solution.py:251
  37.5 17.7 %copy-start.1 = (s32[4]{0:T(128)S(1)}, s32[4]{0:T(128)}, u32[]{:S(2)}) copy-start(s32[4]{0:T(128)} %refs_0_.7) | copy-start | bytes 52
  38.6 16.6 %all-to-all-start = ((bf16[64,4,2048]{2,0,1:T(8,128)(2,1)}), bf16[64,4,2048]{2,0,1:T(8,128)(2,1)S(1)}, u32[]{:S(2)}, u32[]{:S(2)}) async-start(bf16[64,4,2048]{2,0,1:T(8,128)(2,1)} %bitcast.18), calls=%async_computation | async-start | bytes 2097152 | tf_op jit(solution)/shard_map/all_to_all | solution.py:239
  42.1 13.1 %collective-permute-start.6 = (bf16[256,1024]{1,0:T(8,128)(2,1)S(1)}, bf16[256,1024]{1,0:T(8,128)(2,1)S(1)}, u32[]{:S(2)}, u32[]{:S(2)}) collective-permute-start(bf16[256,1024]{1,0:T(8,128)(2,1)S(1)} %collective-permute-done.5.refs_5_.refs_7_.refs_12_.refs_14_), channel_id=1, source_target_pairs={{0,4},{8,12},{16,20},{24,28},{1,5},{9,13},{17,21},{25,29},{2,6},{1... | collective-permute-start | bytes 1572872 | tf_op jit(solution)/shard_map/ppermute | solution.py:251
  43.4 11.8 %collective-permute-start.7 = (bf16[256,512]{1,0:T(8,128)(2,1)S(1)}, bf16[256,512]{1,0:T(8,128)(2,1)S(1)}, u32[]{:S(2)}, u32[]{:S(2)}) collective-permute-start(bf16[256,512]{1,0:T(8,128)(2,1)S(1)} %slice.4), channel_id=1, source_target_pairs={{0,8},{8,16},{16,24},{1,9},{9,17},{17,25},{2,10},{10,18},{18,26},{... | collective-permute-start | bytes 786440 | tf_op jit(solution)/shard_map/ppermute | solution.py:251

commit v6 on v5

--- a/solution.py
+++ b/solution.py
@@ -305,43 +305,6 @@
     state_b = send(state_v, odd_to_next)
     state_c1 = send(through(here) * through(here + 1) * state_b, even_to_even)
     state_c2 = send(state_b, even_to_odd)
-
-    blocks = SPAN + 1
-    shpb = min(per_device, group_size)
-    ssteps = per_device // shpb
-    kv_index = lambda i: (i * shpb * kv_local) // per_device
-    def kv_spec(offset, value):
-        base = offset + (kv_local if value else 0)
-        return pl.BlockSpec((rows, HD), lambda i: (0, base + kv_index(i)))
-
-    kv_arrays, kv_specs = [], []
-    for value in (False, True):
-        for m in range(blocks):
-            for source in ((odd_src[m],) if m == 0 else (odd_src[m], even_src[m])):
-                kv_arrays.append(source[0])
-                kv_specs.append(kv_spec(source[1], value))
-
-    attended = pl.pallas_call(
-        lambda *refs: soft_kernel(blocks, shpb, ndocs, *refs),
-        out_shape=jax.ShapeDtypeStruct((rows, per_device * HD), BF16),
-        grid=(ssteps,),
-        in_specs=[smem_spec(), smem_spec(), col_spec(rows, shpb * HD)] + kv_specs,
-        out_specs=col_spec(rows, shpb * HD),
-        scratch_shapes=[
-            pltpu.VMEM((blocks, shpb, rows, rows), F32),
-            pltpu.VMEM((shpb, rows, 1), F32),
-            pltpu.VMEM((shpb, rows, 1), F32),
-            pltpu.VMEM((shpb, rows, HD), F32),
-        ],
-        compiler_params=pltpu.CompilerParams(
-            dimension_semantics=("arbitrary",), vmem_limit_bytes=48 * 1024 * 1024
-        ),
-        cost_estimate=pl.CostEstimate(
-            flops=4 * rows * rows * blocks * HD * per_device,
-            transcendentals=rows * rows * blocks * per_device,
-            bytes_accessed=rows * per_device * HD * 4 + 2 * blocks * rows * HD * 2 * per_device,
-        ),
-    )(lengths, shard_start, mixed, *kv_arrays)
 
     lightning_out = pl.pallas_call(
         lambda *refs: lin_finish_kernel(lhpb, ndocs, *refs),
@@ -376,6 +339,47 @@
         lin_local,
         norm_gain.reshape(1, width),
     )
+    lightning_out, kv_c1, kv_c2 = lax.optimization_barrier((lightning_out, kv_c1, kv_c2))
+    odd_src = [(own_kv, 0), (kv_a, 0), (kv_c2, 0), (kv_c2, 2 * kv_local)]
+    even_src = [(own_kv, 0), (kv_b, 0), (kv_b, 2 * kv_local), (kv_c1, 0)]
+
+    blocks = SPAN + 1
+    shpb = min(per_device, group_size)
+    ssteps = per_device // shpb
+    kv_index = lambda i: (i * shpb * kv_local) // per_device
+    def kv_spec(offset, value):
+        base = offset + (kv_local if value else 0)
+        return pl.BlockSpec((rows, HD), lambda i: (0, base + kv_index(i)))
+
+    kv_arrays, kv_specs = [], []
+    for value in (False, True):
+        for m in range(blocks):
+            for source in ((odd_src[m],) if m == 0 else (odd_src[m], even_src[m])):
+                kv_arrays.append(source[0])
+                kv_specs.append(kv_spec(source[1], value))
+
+    attended = pl.pallas_call(
+        lambda *refs: soft_kernel(blocks, shpb, ndocs, *refs),
+        out_shape=jax.ShapeDtypeStruct((rows, per_device * HD), BF16),
+        grid=(ssteps,),
+        in_specs=[smem_spec(), smem_spec(), col_spec(rows, shpb * HD)] + kv_specs,
+        out_specs=col_spec(rows, shpb * HD),
+        scratch_shapes=[
+            pltpu.VMEM((blocks, shpb, rows, rows), F32),
+            pltpu.VMEM((shpb, rows, 1), F32),
+            pltpu.VMEM((shpb, rows, 1), F32),
+            pltpu.VMEM((shpb, rows, HD), F32),
+        ],
+        compiler_params=pltpu.CompilerParams(
+            dimension_semantics=("arbitrary",), vmem_limit_bytes=48 * 1024 * 1024
+        ),
+        cost_estimate=pl.CostEstimate(
+            flops=4 * rows * rows * blocks * HD * per_device,
+            transcendentals=rows * rows * blocks * per_device,
+            bytes_accessed=rows * per_device * HD * 4 + 2 * blocks * rows * HD * 2 * per_device,
+        ),
+    )(lengths, shard_start, mixed, *kv_arrays)
+
     return (lightning_out, attended)
 
 

time: 72.8 us -> 73.3 us (level)
  the two profiles are of different devices: /device:TPU:17 before, /device:TPU:8 now
where the time goes in v6:
time: 73.3 us; the launch traced here: 74 us
  starting transfers between devices  26.5 us (36%)
  Pallas kernels  23.5 us (32%)
  waiting for transfers between devices  15.5 us (21%)
  other arithmetic  4.08 us (6%)
  between operations  3.26 us (4%)
  local copies, waits for them, and re-layouts  1.15 us (2%)
    ppermute x8, starting transfers between devices, send(): return lax.ppermute(value, 'ctx', pairs)  19 us
    ppermute x8, waiting for transfers between devices, send(): return lax.ppermute(value, 'ctx', pairs)  11.3 us
    pallas_call x1, Pallas kernels, body(): pl.pallas_call(lambda *refs: soft_kernel(blocks, shpb, ndocs, *refs), out...  9.91 us
    pallas_call x1, Pallas kernels, body(): pl.pallas_call(lambda *refs: lin_local_kernel(lhpb, ndocs, *refs), out_sh...  6.16 us
    pallas_call x1, Pallas kernels, body(): pl.pallas_call(lambda *refs: lin_finish_kernel(lhpb, ndocs, *refs), out_s...  4.56 us
    all_to_all x1, waiting for transfers between devices, body(): lax.all_to_all(kv_packed, 'head', split_axis=1, concat_axis=0, tiled=True)  4.24 us
    all_to_all x1, starting transfers between devices, body(): lax.all_to_all(soft_query, 'head', split_axis=1, concat_axis=0, tiled=True)  3.71 us
    all_to_all x1, starting transfers between devices, body(): lax.all_to_all(kv_packed, 'head', split_axis=1, concat_axis=0, tiled=True)  3.71 us
  transfers between devices with their start and end apart: 10, of which 4 were waited for; matrix products, arithmetic and copies ran while one was open for 7% of the time, Pallas kernels for 14%

profile of v6, /device:TPU:8, one launch (start us, length us, event | category | flops | bytes accessed | tf_op | source)
XLA Modules:
  0.0 74.0 jit_solution(15515124967545869446)
XLA Ops:
  0.6 2.9 %shard_map.95 = f32[16,128,128]{2,1,0:T(8,128)} custom-call(s32[4]{0:T(128)} %refs_0_.7, s32[1]{0:T(128)} %bitcast.refs_1_, bf16[256,2048]{1,0:T(8,128)(2,1)} %refs_3_.3, bf16[256,2048]{1,0:T(8,128)(2,1)} %refs_4_.1), custom_call_target="tpu_custom_call" | custom-call | flops 134217728 | bytes 3145728 | tf_op jit(solution)/shard_map/pallas_call | solution.py:263
  3.5 1.8 %collective-permute-start = (f32[16,128,128]{2,1,0:T(8,128)}, f32[16,128,128]{2,1,0:T(8,128)S(1)}, u32[]{:S(2)}, u32[]{:S(2)}) collective-permute-start(f32[16,128,128]{2,1,0:T(8,128)} %shard_map.95), channel_id=1, source_target_pairs={{0,4},{8,12},{16,20},{24,28},{1,5},{9,13},{17,21},{25,29},{2,6},{1... | collective-permute-start | bytes 3145736 | tf_op jit(solution)/shard_map/ppermute | solution.py:251
  5.3 0.2 reduce-window.9
  5.5 0.7 fusion.3
  7.5 6.2 %shard_map.96.refs_7_ = f32[256,2048]{1,0:T(8,128)} custom-call(s32[4]{0:T(128)} %refs_0_.7, s32[1]{0:T(128)} %bitcast.refs_1_, bf16[256,2048]{1,0:T(8,128)(2,1)} %refs_2_.5, bf16[256,2048]{1,0:T(8,128)(2,1)} %refs_3_.3, bf16[256,2048]{1,0:T(8,128)(2,1)} %refs_4_.1), custom_call_target="tpu_custom_call" | custom-call | flops 805306368 | bytes 5242880 | tf_op jit(solution)/shard_map/pallas_call | solution.py:277
  13.7 0.1 multiply_add_fusion
  13.8 1.4 %collective-permute-start.1 = (f32[16,128,128]{2,1,0:T(8,128)S(1)}, f32[16,128,128]{2,1,0:T(8,128)}, u32[]{:S(2)}, u32[]{:S(2)}) collective-permute-start(f32[16,128,128]{2,1,0:T(8,128)S(1)} %multiply_add_fusion), channel_id=1, source_target_pairs={{4,8},{12,16},{20,24},{5,9},{13,17},{21,25},{6,10},{14,18},{22,26}... | collective-permute-start | bytes 3145736 | tf_op jit(solution)/shard_map/ppermute | solution.py:251
  15.3 0.7 pad_maximum_fusion.1
  16.0 3.7 %all-to-all-start = ((bf16[64,4,512]{2,0,1:T(8,128)(2,1)}), bf16[64,4,512]{2,0,1:T(8,128)(2,1)S(1)}, u32[]{:S(2)}, u32[]{:S(2)}) async-start(bf16[64,4,512]{2,0,1:T(8,128)(2,1)} %pad_maximum_fusion.1), calls=%async_computation | async-start | bytes 524288 | tf_op jit(solution)/shard_map/all_to_all | solution.py:238
  20.9 4.2 %all-to-all-done = bf16[64,4,512]{2,0,1:T(8,128)(2,1)S(1)} async-done(((bf16[64,4,512]{2,0,1:T(8,128)(2,1)}), bf16[64,4,512]{2,0,1:T(8,128)(2,1)S(1)}, u32[]{:S(2)}, u32[]{:S(2)}) %all-to-all-start) | async-done | bytes 262176 | tf_op jit(solution)/shard_map/all_to_all | solution.py:238
  25.1 4.0 %collective-permute-start.4 = (bf16[256,512]{1,0:T(8,128)(2,1)S(1)}, bf16[256,512]{1,0:T(8,128)(2,1)S(1)}, u32[]{:S(2)}, u32[]{:S(2)}) collective-permute-start(bf16[256,512]{1,0:T(8,128)(2,1)S(1)} %bitcast.20), channel_id=1, source_target_pairs={{0,4},{8,12},{16,20},{24,28},{1,5},{9,13},{17,21},{25,29},{2,6},{1... | collective-permute-start | bytes 786440 | tf_op jit(solution)/shard_map/ppermute | solution.py:251
  29.1 1.1 %collective-permute-done.1.refs_5_ = f32[16,128,128]{2,1,0:T(8,128)} collective-permute-done((f32[16,128,128]{2,1,0:T(8,128)S(1)}, f32[16,128,128]{2,1,0:T(8,128)}, u32[]{:S(2)}, u32[]{:S(2)}) %collective-permute-start.1) | collective-permute-done | bytes 1048608 | tf_op jit(solution)/shard_map/ppermute | solution.py:251
  30.2 2.3 %broadcast_multiply_fusion = f32[16,128,128]{2,1,0:T(8,128)} fusion(f32[16,128,128]{2,1,0:T(8,128)} %collective-permute-done.1.refs_5_, f32[]{:T(128)S(6)} %mul.26), kind=kLoop, calls=%fused_computation.3 | loop fusion | flops 262144 | bytes 2097156 | tf_op jit(solution)/shard_map/mul | solution.py:306
  32.5 3.5 %collective-permute-start.3 = (f32[16,128,128]{2,1,0:T(8,128)}, f32[16,128,128]{2,1,0:T(8,128)}, u32[]{:S(2)}, u32[]{:S(2)}) collective-permute-start(f32[16,128,128]{2,1,0:T(8,128)} %broadcast_multiply_fusion), channel_id=1, source_target_pairs={{0,8},{8,16},{16,24},{1,9},{9,17},{17,25},{2,10},{10,18},{18,26},{... | collective-permute-start | bytes 3145736 | tf_op jit(solution)/shard_map/ppermute | solution.py:251
  36.0 2.3 %collective-permute-start.2 = (f32[16,128,128]{2,1,0:T(8,128)}, f32[16,128,128]{2,1,0:T(8,128)}, u32[]{:S(2)}, u32[]{:S(2)}) collective-permute-start(f32[16,128,128]{2,1,0:T(8,128)} %collective-permute-done.1.refs_5_), channel_id=1, source_target_pairs={{0,4},{8,12},{16,20},{24,28},{1,5},{9,13},{17,21},{25,29},{2,6},{1... | collective-permute-start | bytes 3145736 | tf_op jit(solution)/shard_map/ppermute | solution.py:251
  38.3 1.3 %collective-permute-start.5 = (bf16[256,1024]{1,0:T(8,128)(2,1)S(1)}, bf16[256,1024]{1,0:T(8,128)(2,1)S(1)}, u32[]{:S(2)}, u32[]{:S(2)}) collective-permute-start(bf16[256,1024]{1,0:T(8,128)(2,1)S(1)} %pad_maximum_fusion), channel_id=1, source_target_pairs={{4,8},{12,16},{20,24},{5,9},{13,17},{21,25},{6,10},{14,18},{22,26}... | collective-permute-start | bytes 1572872 | tf_op jit(solution)/shard_map/ppermute | solution.py:251
  39.6 1.1 %copy.19 = bf16[8,4,8,2048]{3,2,0,1:T(8,128)(2,1)} copy(bf16[8,4,8,2048]{3,2,1,0:T(8,128)(2,1)S(1)} %bitcast.25) | data formatting | bytes 2097152 | tf_op jit(solution)/shard_map/all_to_all | solution.py:239
  40.7 3.7 %all-to-all-start.1 = ((bf16[64,4,2048]{2,0,1:T(8,128)(2,1)}), bf16[64,4,2048]{2,0,1:T(8,128)(2,1)S(1)}, u32[]{:S(2)}, u32[]{:S(2)}) async-start(bf16[64,4,2048]{2,0,1:T(8,128)(2,1)} %bitcast.18), calls=%async_computation.1 | async-start | bytes 2097152 | tf_op jit(solution)/shard_map/all_to_all | solution.py:239
  44.4 10.0 %collective-permute-done.5.refs_5_.refs_7_.refs_12_.refs_14_ = bf16[256,1024]{1,0:T(8,128)(2,1)S(1)} collective-permute-done((bf16[256,1024]{1,0:T(8,128)(2,1)S(1)}, bf16[256,1024]{1,0:T(8,128)(2,1)S(1)}, u32[]{:S(2)}, u32[]{:S(2)}) %collective-permute-start.5) | collective-permute-done | bytes 524320 | tf_op jit(solution)/shard_map/ppermute | solution.py:251
  54.4 1.3 %collective-permute-start.7 = (bf16[256,1024]{1,0:T(8,128)(2,1)S(1)}, bf16[256,1024]{1,0:T(8,128)(2,1)S(1)}, u32[]{:S(2)}, u32[]{:S(2)}) collective-permute-start(bf16[256,1024]{1,0:T(8,128)(2,1)S(1)} %collective-permute-done.5.refs_5_.refs_7_.refs_12_.refs_14_), channel_id=1, source_target_pairs={{0,4},{8,12},{16,20},{24,28},{1,5},{9,13},{17,21},{25,29},{2,6},{1... | collective-permute-start | bytes 1572872 | tf_op jit(solution)/shard_map/ppermute | solution.py:251
  55.8 3.5 %collective-permute-start.6 = (bf16[256,512]{1,0:T(8,128)(2,1)S(1)}, bf16[256,512]{1,0:T(8,128)(2,1)S(1)}, u32[]{:S(2)}, u32[]{:S(2)}) collective-permute-start(bf16[256,512]{1,0:T(8,128)(2,1)S(1)} %slice.4), channel_id=1, source_target_pairs={{0,8},{8,16},{16,24},{1,9},{9,17},{17,25},{2,10},{10,18},{18,26},{... | collective-permute-start | bytes 786440 | tf_op jit(solution)/shard_map/ppermute | solution.py:251
  59.3 4.6 %shard_map.97 = bf16[256,2048]{1,0:T(8,128)(2,1)} custom-call(s32[4]{0:T(128)} %refs_0_.7, s32[1]{0:T(128)} %bitcast.refs_1_, bf16[256,2048]{1,0:T(8,128)(2,1)} %refs_2_.5, f32[16,128,128]{2,1,0:T(8,128)} %copy-done.2, f32[16,128,128]{2,1,0:T(8,128)} %collective-permute-done.2.refs_4_, f32[16,128,128]{2,1,0:T(8,128)} %collective-permute-done.1.refs_5_, ...), custom_call_target="tpu_custom_call" | custom-call | flops 268435456 | bytes 5242880 | tf_op jit(solution)/shard_map/pallas_call | solution.py:309
  63.9 0.2 collective-permute-done.6.refs_9_.refs_16_
  64.1 9.9 %shard_map.98 = bf16[256,2048]{1,0:T(8,128)(2,1)} custom-call(s32[4]{0:T(128)S(1)} %copy-done.1, s32[1]{0:T(128)} %bitcast.refs_1_, bf16[256,2048]{1,0:T(8,128)(2,1)S(1)} %bitcast.19, bf16[256,512]{1,0:T(8,128)(2,1)S(1)} %bitcast.22, bf16[256,512]{1,0:T(8,128)(2,1)S(1)} %collective-permute-done.4.refs_4_.refs_11_, ...), custom_call_target="tpu_custom_call" | custom-call | flops 2147483648 | bytes 10485760 | tf_op jit(solution)/shard_map/pallas_call | solution.py:361
  (23 shorter events, 0.1 us)
Async XLA Ops:
  0.6 4.7 %copy-start = (s32[4]{0:T(128)S(1)}, s32[4]{0:T(128)}, u32[]{:S(2)}) copy-start(s32[4]{0:T(128)} %refs_0_.7) | copy-start | bytes 52
  3.5 10.2 %collective-permute-start = (f32[16,128,128]{2,1,0:T(8,128)}, f32[16,128,128]{2,1,0:T(8,128)S(1)}, u32[]{:S(2)}, u32[]{:S(2)}) collective-permute-start(f32[16,128,128]{2,1,0:T(8,128)} %shard_map.95), channel_id=1, source_target_pairs={{0,4},{8,12},{16,20},{24,28},{1,5},{9,13},{17,21},{25,29},{2,6},{1... | collective-permute-start | bytes 3145736 | tf_op jit(solution)/shard_map/ppermute | solution.py:251
  7.5 6.2 %copy-start.3 = (f32[16,128,128]{2,1,0:T(8,128)S(1)}, f32[16,128,128]{2,1,0:T(8,128)}, u32[]{:S(2)}) copy-start(f32[16,128,128]{2,1,0:T(8,128)} %shard_map.95) | copy-start | bytes 3145732
  13.7 1.6 %copy-start.5 = (bf16[64,1024]{1,0:T(8,128)(2,1)S(1)}, bf16[64,1024]{1,0:T(8,128)(2,1)}, u32[]{:S(2)}) copy-start(bf16[64,1024]{1,0:T(8,128)(2,1)} %param.14) | copy-start | bytes 393220
  13.7 1.6 %copy-start.6 = (bf16[64,1024]{1,0:T(8,128)(2,1)S(1)}, bf16[64,1024]{1,0:T(8,128)(2,1)}, u32[]{:S(2)}) copy-start(bf16[64,1024]{1,0:T(8,128)(2,1)} %param.13) | copy-start | bytes 393220
  13.7 2.4 %copy-start.2 = (f32[16,128,128]{2,1,0:T(8,128)}, f32[16,128,128]{2,1,0:T(8,128)S(1)}, u32[]{:S(2)}) copy-start(f32[16,128,128]{2,1,0:T(8,128)S(1)} %collective-permute-done.refs_3_) | copy-start | bytes 3145732
  13.8 16.4 %collective-permute-start.1 = (f32[16,128,128]{2,1,0:T(8,128)S(1)}, f32[16,128,128]{2,1,0:T(8,128)}, u32[]{:S(2)}, u32[]{:S(2)}) collective-permute-start(f32[16,128,128]{2,1,0:T(8,128)S(1)} %multiply_add_fusion), channel_id=1, source_target_pairs={{4,8},{12,16},{20,24},{5,9},{13,17},{21,25},{6,10},{14,18},{22,26}... | collective-permute-start | bytes 3145736 | tf_op jit(solution)/shard_map/ppermute | solution.py:251
  15.3 24.3 %copy-start.4 = (bf16[64,8192]{1,0:T(8,128)(2,1)S(1)}, bf16[64,8192]{1,0:T(8,128)(2,1)}, u32[]{:S(2)}) copy-start(bf16[64,8192]{1,0:T(8,128)(2,1)} %param.12) | copy-start | bytes 3145732
  16.0 9.1 %all-to-all-start = ((bf16[64,4,512]{2,0,1:T(8,128)(2,1)}), bf16[64,4,512]{2,0,1:T(8,128)(2,1)S(1)}, u32[]{:S(2)}, u32[]{:S(2)}) async-start(bf16[64,4,512]{2,0,1:T(8,128)(2,1)} %pad_maximum_fusion.1), calls=%async_computation | async-start | bytes 524288 | tf_op jit(solution)/shard_map/all_to_all | solution.py:238
  25.1 13.1 %collective-permute-start.4 = (bf16[256,512]{1,0:T(8,128)(2,1)S(1)}, bf16[256,512]{1,0:T(8,128)(2,1)S(1)}, u32[]{:S(2)}, u32[]{:S(2)}) collective-permute-start(bf16[256,512]{1,0:T(8,128)(2,1)S(1)} %bitcast.20), channel_id=1, source_target_pairs={{0,4},{8,12},{16,20},{24,28},{1,5},{9,13},{17,21},{25,29},{2,6},{1... | collective-permute-start | bytes 786440 | tf_op jit(solution)/shard_map/ppermute | solution.py:251
  32.5 26.8 %collective-permute-start.3 = (f32[16,128,128]{2,1,0:T(8,128)}, f32[16,128,128]{2,1,0:T(8,128)}, u32[]{:S(2)}, u32[]{:S(2)}) collective-permute-start(f32[16,128,128]{2,1,0:T(8,128)} %broadcast_multiply_fusion), channel_id=1, source_target_pairs={{0,8},{8,16},{16,24},{1,9},{9,17},{17,25},{2,10},{10,18},{18,26},{... | collective-permute-start | bytes 3145736 | tf_op jit(solution)/shard_map/ppermute | solution.py:251
  36.0 23.3 %collective-permute-start.2 = (f32[16,128,128]{2,1,0:T(8,128)}, f32[16,128,128]{2,1,0:T(8,128)}, u32[]{:S(2)}, u32[]{:S(2)}) collective-permute-start(f32[16,128,128]{2,1,0:T(8,128)} %collective-permute-done.1.refs_5_), channel_id=1, source_target_pairs={{0,4},{8,12},{16,20},{24,28},{1,5},{9,13},{17,21},{25,29},{2,6},{1... | collective-permute-start | bytes 3145736 | tf_op jit(solution)/shard_map/ppermute | solution.py:251
  38.3 16.1 %collective-permute-start.5 = (bf16[256,1024]{1,0:T(8,128)(2,1)S(1)}, bf16[256,1024]{1,0:T(8,128)(2,1)S(1)}, u32[]{:S(2)}, u32[]{:S(2)}) collective-permute-start(bf16[256,1024]{1,0:T(8,128)(2,1)S(1)} %pad_maximum_fusion), channel_id=1, source_target_pairs={{4,8},{12,16},{20,24},{5,9},{13,17},{21,25},{6,10},{14,18},{22,26}... | collective-permute-start | bytes 1572872 | tf_op jit(solution)/shard_map/ppermute | solution.py:251
  40.7 23.4 %all-to-all-start.1 = ((bf16[64,4,2048]{2,0,1:T(8,128)(2,1)}), bf16[64,4,2048]{2,0,1:T(8,128)(2,1)S(1)}, u32[]{:S(2)}, u32[]{:S(2)}) async-start(bf16[64,4,2048]{2,0,1:T(8,128)(2,1)} %bitcast.18), calls=%async_computation.1 | async-start | bytes 2097152 | tf_op jit(solution)/shard_map/all_to_all | solution.py:239
  54.4 9.6 %collective-permute-start.7 = (bf16[256,1024]{1,0:T(8,128)(2,1)S(1)}, bf16[256,1024]{1,0:T(8,128)(2,1)S(1)}, u32[]{:S(2)}, u32[]{:S(2)}) collective-permute-start(bf16[256,1024]{1,0:T(8,128)(2,1)S(1)} %collective-permute-done.5.refs_5_.refs_7_.refs_12_.refs_14_), channel_id=1, source_target_pairs={{0,4},{8,12},{16,20},{24,28},{1,5},{9,13},{17,21},{25,29},{2,6},{1... | collective-permute-start | bytes 1572872 | tf_op jit(solution)/shard_map/ppermute | solution.py:251
  55.8 8.3 %collective-permute-start.6 = (bf16[256,512]{1,0:T(8,128)(2,1)S(1)}, bf16[256,512]{1,0:T(8,128)(2,1)S(1)}, u32[]{:S(2)}, u32[]{:S(2)}) collective-permute-start(bf16[256,512]{1,0:T(8,128)(2,1)S(1)} %slice.4), channel_id=1, source_target_pairs={{0,8},{8,16},{16,24},{1,9},{9,17},{17,25},{2,10},{10,18},{18,26},{... | collective-permute-start | bytes 786440 | tf_op jit(solution)/shard_map/ppermute | solution.py:251
  59.3 4.8 %copy-start.1 = (s32[4]{0:T(128)S(1)}, s32[4]{0:T(128)}, u32[]{:S(2)}) copy-start(s32[4]{0:T(128)} %refs_0_.7) | copy-start | bytes 52
